TPU v7x, 128 devices: a whole 4x4x4 slice. The times are simulated.
128 devices in a mesh: dp: 8 (over x_hi, z), tensor: 16 (over y, x_lo, core).
Axes of the slice: x: 4 (x_hi: 2, x_lo: 2; x = x_hi * 2 + x_lo), y: 4, z: 4, core: 2. Of those that a mesh axis runs over, the one named last changes fastest.
Arguments:
- tokens: bfloat16 [16384, 2048], P(('dp', 'tensor')), parts along dimension 0, may hold values from -6 to 6
- segment_ids: int32 [16384], P('dp'), parts along dimension 0, may hold values from 0 to 3, never falling along the last dimension, each value on 1 to 1024 neighbouring positions
- attention_gain: float32 [2048], replicated, may hold values from 0.1 to 1.9
- query_weight: bfloat16 [2048, 2048], P(None, 'tensor'), may hold values from -1 to 1
- key_weight: bfloat16 [2048, 2048], P(None, 'tensor'), may hold values from -1 to 1
- value_weight: bfloat16 [2048, 2048], P(None, 'tensor'), may hold values from -0.125 to 0.125
- output_weight: bfloat16 [2048, 2048], P('tensor'), may hold values from -0.125 to 0.125
- ffn_gain: float32 [2048], replicated, may hold values from 0.1 to 1.9
- shared_gate: bfloat16 [2048, 2816], P(None, 'tensor'), may hold values from -0.125 to 0.125
- shared_up: bfloat16 [2048, 2816], P(None, 'tensor'), may hold values from -0.125 to 0.125
- shared_down: bfloat16 [2816, 2048], P('tensor'), may hold values from -0.109375 to 0.109375
- expert_gate: bfloat16 [16, 2048, 1408], P('tensor'), may hold values from -0.125 to 0.125
- expert_up: bfloat16 [16, 2048, 1408], P('tensor'), may hold values from -0.125 to 0.125
- expert_down: bfloat16 [16, 1408, 2048], P('tensor'), may hold values from -0.15625 to 0.15625
- expert_ids: int32 [16384, 6], P('dp'), parts along dimension 0, may hold values from 0 to 15, all different within a row; in each aligned block of 128 rows (0 to 127, 128 to 255, ...) at most 64 rows name the same one
- gate_weights: float32 [16384, 6], P('dp'), parts along dimension 0, may hold values from 0.05 to 0.35
- page_table: int32 [128], P('dp'), parts along dimension 0, may hold values from 0 to 15, each once
Outputs:
- layer_out: bfloat16 [16384, 2048], P(('dp', 'tensor')), parts along dimension 0
- kv_pages: bfloat16 [2, 128, 128, 2048], P(None, 'dp', None, 'tensor'), parts along dimension 1
There are 8 independent parts, one for each index of `dp`. A program takes and returns all parts, laid end to end along the dimension named above; an argument that names none is the same for every part. Nothing has to cross between parts.
Inputs may be any that keep to these rules, and one draw needn't show every extreme that they name: `segment_ids`: ids never fall along the stream; each of the 4 prompts holds 1 to 1024 tokens and one holds exactly 1024. `expert_ids`: each row names 6 different experts; within each aligned block of 128 rows (the tokens of one index of tensor) no expert is named by more than 64 rows, a bound that some block reaches. `page_table`: each cache page is named once.
All inputs are finite; a program needn't handle non-finite values.
Results may differ from a plain program's by a relative error of at most 0.02.
The roundings to bfloat16 on the way count: a program that leaves them out, or rounds other values in their place, can miss the bound.
Values may be sent and summed in bfloat16 or wider, within the bound.
No kernel may reach another device: no remote copies, remote signals or barrier semaphores. Data moves between devices by JAX's collectives and lax.ppermute only.
A program may use at most 128 MiB of HBM per device.

v0:
```python
import jax
import jax.numpy as jnp
from jax import lax
from jax.sharding import PartitionSpec as P

HD = 128
TOP = 6
PAGE = 128


def rms_scale(hidden, gain):
    widened = hidden.astype(jnp.float32)
    inverse = lax.rsqrt(jnp.mean(widened * widened, axis=-1, keepdims=True) + 1e-06)
    return (widened * inverse * gain).astype(jnp.bfloat16)


def attend(projected, segment_ids, head_count):
    total_tokens = projected.shape[0]
    inner = head_count * HD
    queries = projected[:, :inner].reshape(total_tokens, head_count, HD)
    keys = projected[:, inner : 2 * inner].reshape(total_tokens, head_count, HD)
    values = projected[:, 2 * inner :].reshape(total_tokens, head_count, HD)
    scale = HD ** (-0.5)
    positions = jnp.arange(total_tokens, dtype=jnp.int32)
    span = min(512, total_tokens)

    def one_block(start):
        query_rows = lax.dynamic_slice_in_dim(queries, start, span, 0)
        query_segments = lax.dynamic_slice_in_dim(segment_ids, start, span, 0)
        query_positions = start + jnp.arange(span, dtype=jnp.int32)
        scores = (
            jnp.einsum("qhd,khd->hqk", query_rows, keys, preferred_element_type=jnp.float32) * scale
        )
        allowed = (query_segments[:, None] == segment_ids[None, :]) & (
            positions[None, :] <= query_positions[:, None]
        )
        scores = jnp.where(allowed[None], scores, -jnp.inf)
        highest = jnp.max(scores, axis=-1, keepdims=True)
        weights = jnp.exp(scores - highest)
        probs = (weights / jnp.sum(weights, axis=-1, keepdims=True)).astype(jnp.bfloat16)
        context = jnp.einsum("hqk,khd->qhd", probs, values, preferred_element_type=jnp.float32)
        return context.astype(jnp.bfloat16)

    starts = jnp.arange(total_tokens // span, dtype=jnp.int32) * span
    context = lax.map(one_block, starts).reshape(total_tokens, inner)
    return (context, keys.reshape(total_tokens, inner), values.reshape(total_tokens, inner))


def expert_apply(picked, gate_w, up_w, down_w):
    gate_part = jnp.dot(picked, gate_w, preferred_element_type=jnp.float32)
    upward = jnp.dot(picked, up_w, preferred_element_type=jnp.float32)
    hidden = (jax.nn.silu(gate_part) * upward).astype(jnp.bfloat16)
    return jnp.dot(hidden, down_w, preferred_element_type=jnp.float32).astype(jnp.bfloat16)


def ring_reduce_scatter(partial, groups):
    ring = groups // 4
    rows = partial.shape[0] // groups
    width = partial.shape[1]
    me = lax.axis_index("tensor")
    y = me // 4
    side = (me // 2) % 2
    core = me % 2
    blocks = partial.reshape(ring, 2, 2, rows, width)
    core_pairs = [(t, t ^ 1) for t in range(groups)]
    keep = lax.dynamic_index_in_dim(blocks, core, axis=2, keepdims=False)
    give = lax.dynamic_index_in_dim(blocks, 1 - core, axis=2, keepdims=False)
    got = lax.ppermute(give, "tensor", core_pairs)
    summed = keep.astype(jnp.float32) + got.astype(jnp.float32)
    half = width // 2
    forward_part = summed[..., :half]
    backward_part = summed[..., half:]
    forward_pairs = [(t, ((t // 4 + 1) % ring) * 4 + t % 4) for t in range(groups)]
    backward_pairs = [(t, ((t // 4 + ring - 1) % ring) * 4 + t % 4) for t in range(groups)]
    carry_f = lax.dynamic_index_in_dim(forward_part, (y + ring - 1) % ring, 0, False)
    carry_b = lax.dynamic_index_in_dim(backward_part, (y + 1) % ring, 0, False)
    carry_f = carry_f.astype(jnp.bfloat16)
    carry_b = carry_b.astype(jnp.bfloat16)
    for step in range(ring - 1):
        recv_f = lax.ppermute(carry_f, "tensor", forward_pairs)
        recv_b = lax.ppermute(carry_b, "tensor", backward_pairs)
        index_f = (y + 2 * ring - step - 2) % ring
        index_b = (y + step + 2) % ring
        acc_f = recv_f.astype(jnp.float32) + lax.dynamic_index_in_dim(
            forward_part, index_f, 0, False
        )
        acc_b = recv_b.astype(jnp.float32) + lax.dynamic_index_in_dim(
            backward_part, index_b, 0, False
        )
        carry_f = acc_f.astype(jnp.bfloat16)
        carry_b = acc_b.astype(jnp.bfloat16)
    mine = jnp.concatenate([acc_f, acc_b], axis=-1)
    side_pairs = [(t, t ^ 2) for t in range(groups)]
    keep_side = lax.dynamic_index_in_dim(mine, side, 0, False)
    give_side = lax.dynamic_index_in_dim(mine, 1 - side, 0, False).astype(jnp.bfloat16)
    got_side = lax.ppermute(give_side, "tensor", side_pairs)
    return keep_side + got_side.astype(jnp.float32)


def shards(
    tokens,
    segment_ids,
    attention_gain,
    query_weight,
    key_weight,
    value_weight,
    output_weight,
    ffn_gain,
    shared_gate,
    shared_up,
    shared_down,
    expert_gate,
    expert_up,
    expert_down,
    expert_ids,
    gate_weights,
    page_table,
):
    tok_dev = tokens.shape[0]
    groups = lax.axis_size("tensor")
    position = lax.axis_index("tensor")
    inner = query_weight.shape[1]
    head_count = inner // HD
    model_width = tokens.shape[1]

    projection = jnp.concatenate([query_weight, key_weight, value_weight], axis=1)
    normed_all = lax.all_gather(rms_scale(tokens, attention_gain), "tensor", axis=0, tiled=True)
    out_weight_all = lax.all_gather(output_weight, "tensor", axis=0, tiled=True)
    projected = lax.map(
        lambda rows: jnp.dot(rows, projection, preferred_element_type=jnp.float32).astype(
            jnp.bfloat16
        ),
        normed_all.reshape(4, -1, normed_all.shape[1]),
    ).reshape(normed_all.shape[0], -1)
    context, keys, values = attend(projected, segment_ids, head_count)
    cache = jnp.stack([keys, values]).reshape(2, -1, PAGE, inner)
    kv_pages = jnp.zeros_like(cache).at[:, page_table].set(cache)

    received = lax.all_to_all(
        context.reshape(groups, tok_dev, inner), "tensor", split_axis=0, concat_axis=0, tiled=True
    )
    context_rows = received.transpose(1, 0, 2).reshape(tok_dev, groups * inner)
    attention = jnp.dot(context_rows, out_weight_all, preferred_element_type=jnp.float32)
    residual = (tokens.astype(jnp.float32) + attention).astype(jnp.bfloat16)
    normed_ffn = rms_scale(residual, ffn_gain)
    pieces = 2
    piece_width = model_width // pieces
    normed_stream = lax.all_gather(normed_ffn, "tensor", axis=0, tiled=True)

    local_experts = expert_gate.shape[0]
    expert_count = local_experts * groups
    capacity = tok_dev * TOP // expert_count + tok_dev // 8
    id_blocks = expert_ids.reshape(groups, tok_dev, -1)
    gate_blocks = gate_weights.reshape(groups, tok_dev, -1)
    slots = jnp.arange(capacity, dtype=jnp.int32)
    onehots = []
    weights = []
    for local in range(local_experts):
        expert = position * local_experts + local
        chosen = id_blocks == expert
        hits = jnp.sum(chosen.astype(jnp.int32), axis=2)
        weights.append(jnp.sum(jnp.where(chosen, gate_blocks, 0.0), axis=2))
        rank = jnp.cumsum(hits, axis=1) - hits
        onehots.append(
            ((hits[:, None, :] > 0) & (rank[:, None, :] == slots[None, :, None])).astype(
                jnp.bfloat16
            )
        )

    shared_columns = jnp.concatenate([shared_gate, shared_up], axis=1)
    shared_width = shared_gate.shape[1]
    joined = jnp.dot(normed_stream, shared_columns, preferred_element_type=jnp.float32)
    token_blocks = normed_stream.reshape(groups, tok_dev, model_width)
    expert_gate_parts = []
    expert_up_parts = []
    for local in range(local_experts):
        picked = jnp.einsum(
            "bst,btd->bsd", onehots[local], token_blocks, preferred_element_type=jnp.float32
        ).astype(jnp.bfloat16).reshape(-1, model_width)
        expert_gate_parts.append(
            jnp.dot(picked, expert_gate[local], preferred_element_type=jnp.float32)
        )
        expert_up_parts.append(jnp.dot(picked, expert_up[local], preferred_element_type=jnp.float32))
    hidden_all = (jax.nn.silu(joined[:, :shared_width]) * joined[:, shared_width:]).astype(
        jnp.bfloat16
    )
    expert_hidden = [
        (jax.nn.silu(expert_gate_parts[local]) * expert_up_parts[local]).astype(jnp.bfloat16)
        for local in range(local_experts)
    ]

    outs = []
    for k in range(pieces):
        columns = slice(k * piece_width, (k + 1) * piece_width)
        term = jnp.dot(hidden_all, shared_down[:, columns], preferred_element_type=jnp.float32)
        for local in range(local_experts):
            rows = jnp.dot(
                expert_hidden[local], expert_down[local][:, columns], preferred_element_type=jnp.float32
            ).astype(jnp.bfloat16)
            back = jnp.einsum(
                "bst,bsd->btd",
                onehots[local],
                rows.reshape(groups, capacity, piece_width),
                preferred_element_type=jnp.float32,
            ).astype(jnp.bfloat16)
            term = term + weights[local].reshape(-1, 1) * back.reshape(-1, piece_width).astype(
                jnp.float32
            )
        outs.append(ring_reduce_scatter(term.astype(jnp.bfloat16), groups))
    ffn_out = jnp.concatenate(outs, axis=1)
    layer_out = (residual.astype(jnp.float32) + ffn_out).astype(jnp.bfloat16)
    return (layer_out, kv_pages)


def solution(mesh):
    placed = (
        P(("dp", "tensor"), None),
        P("dp"),
        P(),
        P(None, "tensor"),
        P(None, "tensor"),
        P(None, "tensor"),
        P("tensor", None),
        P(),
        P(None, "tensor"),
        P(None, "tensor"),
        P("tensor", None),
        P("tensor", None, None),
        P("tensor", None, None),
        P("tensor", None, None),
        P("dp", None),
        P("dp", None),
        P("dp"),
    )
    return jax.shard_map(
        shards,
        mesh=mesh,
        in_specs=placed,
        out_specs=(P(("dp", "tensor"), None), P(None, "dp", None, "tensor")),
        check_vma=False,
    )
```

profile of v0, /device:TPU:0, one launch (start us, length us, event | category | flops | bytes accessed | tf_op | source)
XLA Modules:
  0.0 287.7 jit_solution(262670037977427516)
XLA Ops:
  7.2 1.2 fusion.53
  8.4 2.0 fusion.55
  10.6 0.7 all-gather.6.cloned.1.call-update
  11.3 1.6 pad_maximum_fusion
  12.9 52.3 %all-gather.4.cloned.1.call-done = bf16[2048,2048]{1,0:T(8,128)(2,1)} async-done(((bf16[128,2048]{1,0:T(8,128)(2,1)}), bf16[2048,2048]{1,0:T(8,128)(2,1)}) %all-gather.4.cloned.1.call-update) | async-done | bytes 8388624 | tf_op jit(solution)/shard_map/all_gather | solution.py:127
  65.2 14.6 %while.21 = (s32[]{:T(128)}, bf16[4,512,384]{2,1,0:T(8,128)(2,1)}, bf16[4,512,2048]{2,1,0:T(8,128)(2,1)}, bf16[2048,384]{1,0:T(8,128)(2,1)S(1)}, s32[]{:T(128)}) while((s32[]{:T(128)}, bf16[4,512,384]{2,1,0:T(8,128)(2,1)}, bf16[4,512,2048]{2,1,0:T(8,128)(2,1)}, bf16[2048,384]{1,0:T(8,128)(2,1)S(1)}, s32[]{:T(128)}) %tuple.62), condition=%wide.region_2.3_spmd, body=%wide.region_1.2_spmd.sunk | while | flops 805502976 | bytes 4064325 | solution.py:129
  65.2 3.6 %fusion.120 = bf16[4,512,384]{2,1,0:T(8,128)(2,1)} fusion(bf16[4,512,384]{2,1,0:T(8,128)(2,1)} %get-tuple-element.199, s32[]{:T(128)S(6)} %copy.34, bf16[2048,384]{1,0:T(8,128)(2,1)S(1)} %get-tuple-element.206, bf16[4,512,2048]{2,1,0:T(8,128)(2,1)} %get-tuple-element.205), kind=kOutput, calls=%fused_computation.7.clone.1 | convolution fusion | flops 805502976 | bytes 4064256 | tf_op jit(solution)/shard_map/while/body/eval_jaxpr/dot_general | solution.py:130
  68.8 3.6 %fusion.120 = bf16[4,512,384]{2,1,0:T(8,128)(2,1)} fusion(bf16[4,512,384]{2,1,0:T(8,128)(2,1)} %get-tuple-element.199, s32[]{:T(128)S(6)} %copy.34, bf16[2048,384]{1,0:T(8,128)(2,1)S(1)} %get-tuple-element.206, bf16[4,512,2048]{2,1,0:T(8,128)(2,1)} %get-tuple-element.205), kind=kOutput, calls=%fused_computation.7.clone.1 | convolution fusion | flops 805502976 | bytes 4064256 | tf_op jit(solution)/shard_map/while/body/eval_jaxpr/dot_general | solution.py:130
  72.4 3.6 %fusion.120 = bf16[4,512,384]{2,1,0:T(8,128)(2,1)} fusion(bf16[4,512,384]{2,1,0:T(8,128)(2,1)} %get-tuple-element.199, s32[]{:T(128)S(6)} %copy.34, bf16[2048,384]{1,0:T(8,128)(2,1)S(1)} %get-tuple-element.206, bf16[4,512,2048]{2,1,0:T(8,128)(2,1)} %get-tuple-element.205), kind=kOutput, calls=%fused_computation.7.clone.1 | convolution fusion | flops 805502976 | bytes 4064256 | tf_op jit(solution)/shard_map/while/body/eval_jaxpr/dot_general | solution.py:130
  76.0 3.8 %fusion.120 = bf16[4,512,384]{2,1,0:T(8,128)(2,1)} fusion(bf16[4,512,384]{2,1,0:T(8,128)(2,1)} %get-tuple-element.199, s32[]{:T(128)S(6)} %copy.34, bf16[2048,384]{1,0:T(8,128)(2,1)S(1)} %get-tuple-element.206, bf16[4,512,2048]{2,1,0:T(8,128)(2,1)} %get-tuple-element.205), kind=kOutput, calls=%fused_computation.7.clone.1 | convolution fusion | flops 805502976 | bytes 4064256 | tf_op jit(solution)/shard_map/while/body/eval_jaxpr/dot_general | solution.py:130
  79.8 2.6 fusion.97
  82.5 23.1 %while.22 = (s32[]{:T(128)}, bf16[4,512,1,128]{3,1,2,0:T(8,128)(2,1)S(1)}, s32[4]{0:T(128)S(1)}, s32[2048]{0:T(1024)S(1)}, bf16[2048,1,128]{2,0,1:T(8,128)(2,1)S...) while((s32[]{:T(128)}, ...), condition=%wide.region_6.7_spmd.clone, body=%wide.region_3.6_spmd.clone.sunk | while | flops 548470272 | bytes 13922475 | solution.py:45
  85.3 1.3 fusion.122
  86.6 0.7 fusion.123
  87.3 0.9 fusion.124
  91.1 1.3 fusion.122
  92.4 0.7 fusion.123
  93.1 0.9 fusion.124
  96.9 1.3 fusion.122
  98.1 0.7 fusion.123
  98.8 0.9 fusion.124
  102.7 1.3 fusion.122
  103.9 0.7 fusion.123
  104.6 0.9 fusion.124
  105.6 20.5 %all_to_all.5 = bf16[16,128,128]{2,1,0:T(8,128)(2,1)S(1)} all-to-all(bf16[16,128,128]{2,1,0:T(8,128)(2,1)S(1)} %bitcast.200), channel_id=1, replica_groups=mesh['dp'=8,'tensor'=16] {'tensor'}, dimensions={0} | all-to-all | bytes 1048576 | tf_op jit(solution)/shard_map/all_to_all | solution.py:139
  126.4 4.8 %multiply_reduce_fusion = (f32[128]{0:T(128)S(1)}, f32[128,2048]{1,0:T(8,128)S(1)}) fusion(bf16[128,2048]{0,1:T(8,128)(2,1)S(1)} %bitcast.193, bf16[2048,2048]{1,0:T(8,128)(2,1)} %all-gather.6.cloned.1.call-done, bf16[128,2048]{1,0:T(8,128)(2,1)S(1)} %copy-done), kind=kOutput, calls=%fused_computation.76 | convolution fusion | flops 1075314560 | bytes 10486272 | tf_op jit(solution)/shard_map/dot_general | solution.py:143
  131.2 1.0 multiply_convert_fusion.1
  132.7 52.0 %all-gather.8.cloned.1.call-done = bf16[2048,2048]{1,0:T(8,128)(2,1)} async-done(((bf16[128,2048]{1,0:T(8,128)(2,1)}), bf16[2048,2048]{1,0:T(8,128)(2,1)}) %all-gather.8.cloned.1.call-update) | async-done | bytes 8388624 | tf_op jit(solution)/shard_map/all_gather | solution.py:148
  184.7 4.8 %convolution_convert_fusion = bf16[16,64,2048]{2,1,0:T(8,128)(2,1)S(1)} fusion(bf16[16,128,2048]{2,1,0:T(8,128)(2,1)} %bitcast.182, s32[16,128]{1,0:T(8,128)S(1)} %bitcast_subtract_fusion, pred[16,128]{1,0:T(8,128)(4,1)S(1)} %broadcast_compare_fusion.1), kind=kOutput, calls=%fused_computation.38 | convolution fusion | flops 539230208 | bytes 12593152 | tf_op jit(solution)/shard_map/bst,btd->bsd/dot_general | solution.py:177
  189.5 9.4 %fusion.32 = f32[1024,1408]{1,0:T(8,128)S(1)} fusion(bf16[1024,2048]{1,0:T(8,128)(2,1)S(1)} %bitcast.185, bf16[1,2048,1408]{2,1,0:T(8,128)(2,1)} %param.32), kind=kOutput, calls=%fused_computation.33 | convolution fusion | flops 5905580032 | bytes 15728640 | tf_op jit(solution)/shard_map/dot_general | solution.py:181
  198.9 7.0 %multiply_convert_fusion = bf16[1024,1408]{1,0:T(8,128)(2,1)S(1)} fusion(f32[1024,1408]{1,0:T(8,128)S(1)} %fusion.32, bf16[1024,2048]{1,0:T(8,128)(2,1)S(1)} %bitcast.186, bf16[1,2048,1408]{2,1,0:T(8,128)(2,1)S(1)} %bitcast.204), kind=kOutput, calls=%fused_computation.35 | convolution fusion | flops 5914230784 | bytes 18612224 | tf_op jit(solution)/shard_map/dot_general | solution.py:183
  206.0 3.6 %fusion.45 = bf16[1024,1024]{1,0:T(8,128)(2,1)S(1)} fusion(bf16[1024,1408]{1,0:T(8,128)(2,1)S(1)} %multiply_convert_fusion, bf16[1408,2048]{1,0:T(8,128)(2,1)S(1)} %bitcast.207), kind=kOutput, calls=%fused_computation.51 | convolution fusion | flops 2953838592 | bytes 7864320 | tf_op jit(solution)/shard_map/dot_general | solution.py:197
  209.7 3.9 %fusion.42 = bf16[1024,1024]{1,0:T(8,128)(2,1)S(1)} fusion(bf16[1024,1408]{1,0:T(8,128)(2,1)S(1)} %multiply_convert_fusion, bf16[1408,2048]{1,0:T(8,128)(2,1)S(1)} %bitcast.208), kind=kOutput, calls=%fused_computation.50 | convolution fusion | flops 2953838592 | bytes 7864320 | tf_op jit(solution)/shard_map/dot_general | solution.py:197
  213.6 3.2 %fusion.49 = f32[2048,352]{0,1:T(8,128)S(1)} fusion(bf16[2048,2048]{1,0:T(8,128)(2,1)S(1)} %bitcast.184, bf16[2048,176]{0,1:T(8,128)(2,1)S(1)} %copy-done.10, bf16[2048,176]{0,1:T(8,128)(2,1)S(1)} %copy-done.11), kind=kOutput, calls=%fused_computation.57 | convolution fusion | flops 2955673600 | bytes 12713984 | tf_op jit(solution)/shard_map/dot_general | solution.py:172
  217.2 1.3 convolution_convert_fusion.1
  218.5 1.7 fusion.27
  220.2 1.8 dynamic-slice_bitcast_fusion
  222.2 1.3 convolution_convert_fusion.2
  223.5 1.7 fusion.29
  225.3 2.0 copy-done.1
  227.8 3.2 %convert_add_fusion = f32[4,2,128,1024]{3,2,1,0:T(8,128)S(1)} fusion(bf16[4,2,128,1024]{3,2,1,0:T(8,128)(2,1)} %collective-permute-done.8, bf16[4,2,2,128,1024]{4,3,2,1,0:T(8,128)(2,1)} %bitcast.192, s32[]{:T(128)S(6)} %select_n.134), kind=kLoop, calls=%fused_computation.36 | loop fusion | flops 3145728 | bytes 8388612 | tf_op jit(solution)/shard_map/add | solution.py:69
  231.7 1.6 collective-permute-start.9
  233.2 1.8 collective-permute-start.12
  235.1 2.5 convert_add_fusion.1
  237.6 0.6 fusion.95
  238.9 3.0 %collective-permute-start.4 = (bf16[2,128,512]{2,1,0:T(8,128)(2,1)S(1)}, bf16[2,128,512]{2,1,0:T(8,128)(2,1)S(1)}, u32[]{:S(2)}, u32[]{:S(2)}) collective-permute-start(bf16[2,128,512]{2,1,0:T(8,128)(2,1)S(1)} %fusion.82), channel_id=1, source_target_pairs={{0,12},{1,13},{2,14},{3,15},{4,0},{5,1},{6,2},{7,3},{8,4},{9,5},{1... | collective-permute-start | bytes 786440 | tf_op jit(solution)/shard_map/ppermute | solution.py:81
  242.3 3.1 %collective-permute-start.13 = (bf16[2,128,512]{2,1,0:T(8,128)(2,1)S(1)}, bf16[2,128,512]{2,1,0:T(8,128)(2,1)S(1)}, u32[]{:S(2)}, u32[]{:S(2)}) collective-permute-start(bf16[2,128,512]{2,1,0:T(8,128)(2,1)S(1)} %fusion.68), channel_id=1, source_target_pairs={{0,12},{1,13},{2,14},{3,15},{4,0},{5,1},{6,2},{7,3},{8,4},{9,5},{1... | collective-permute-start | bytes 786440 | tf_op jit(solution)/shard_map/ppermute | solution.py:81
  245.4 3.7 %collective-permute-done.1 = bf16[2,128,512]{2,1,0:T(8,128)(2,1)S(1)} collective-permute-done((bf16[2,128,512]{2,1,0:T(8,128)(2,1)S(1)}, bf16[2,128,512]{2,1,0:T(8,128)(2,1)S(1)}, u32[]{:S(2)}, u32[]{:S(2)}) %collective-permute-start.1) | collective-permute-done | bytes 262176 | tf_op jit(solution)/shard_map/ppermute | solution.py:80
  249.3 3.3 %collective-permute-start.5 = (bf16[2,128,512]{2,1,0:T(8,128)(2,1)S(1)}, bf16[2,128,512]{2,1,0:T(8,128)(2,1)S(1)}, u32[]{:S(2)}, u32[]{:S(2)}) collective-permute-start(bf16[2,128,512]{2,1,0:T(8,128)(2,1)S(1)} %fusion.72), channel_id=1, source_target_pairs={{0,12},{1,13},{2,14},{3,15},{4,0},{5,1},{6,2},{7,3},{8,4},{9,5},{1... | collective-permute-start | bytes 786440 | tf_op jit(solution)/shard_map/ppermute | solution.py:81
  252.6 2.1 collective-permute-done.10
  254.9 3.3 %collective-permute-start.14 = (bf16[2,128,512]{2,1,0:T(8,128)(2,1)S(1)}, bf16[2,128,512]{2,1,0:T(8,128)(2,1)S(1)}, u32[]{:S(2)}, u32[]{:S(2)}) collective-permute-start(bf16[2,128,512]{2,1,0:T(8,128)(2,1)S(1)} %fusion.67), channel_id=1, source_target_pairs={{0,12},{1,13},{2,14},{3,15},{4,0},{5,1},{6,2},{7,3},{8,4},{9,5},{1... | collective-permute-start | bytes 786440 | tf_op jit(solution)/shard_map/ppermute | solution.py:81
  258.2 2.1 collective-permute-done.2
  260.6 3.3 %collective-permute-start.6 = (bf16[2,128,512]{2,1,0:T(8,128)(2,1)S(1)}, bf16[2,128,512]{2,1,0:T(8,128)(2,1)S(1)}, u32[]{:S(2)}, u32[]{:S(2)}) collective-permute-start(bf16[2,128,512]{2,1,0:T(8,128)(2,1)S(1)} %fusion.71), channel_id=1, source_target_pairs={{0,12},{1,13},{2,14},{3,15},{4,0},{5,1},{6,2},{7,3},{8,4},{9,5},{1... | collective-permute-start | bytes 786440 | tf_op jit(solution)/shard_map/ppermute | solution.py:81
  263.9 2.1 collective-permute-done.11
  266.1 1.5 collective-permute-start.15
  267.6 2.6 collective-permute-done.3
  270.4 0.7 fusion.85
  271.1 1.4 collective-permute-start.7
  272.5 1.1 maximum_bitcast_fusion
  273.6 1.2 broadcast_in_dim.45
  274.8 3.4 %scatter_fusion = bf16[2,16,128,128]{3,2,1,0:T(8,128)(2,1)} fusion(bf16[2,16,128,128]{3,2,1,0:T(8,128)(2,1)} %broadcast_in_dim.45, s32[16]{0:T(128)S(1)} %compare_select_fusion, bf16[16,2,128,128]{3,2,1,0:T(8,128)(2,1)} %maximum_bitcast_fusion), kind=kCustom, calls=%fused_computation | custom fusion | bytes 3145792 | tf_op jit(solution)/shard_map/scatter | solution.py:137
  278.2 1.0 fusion.61
  279.2 1.0 fusion.66
  280.2 0.9 fusion.56
  (110 shorter events, 9.7 us)
Async XLA Ops:
  7.2 58.1 %all-gather.4.cloned.1.call-start = ((), (), s32[]{:S(2)}) async-start(), calls=%async_computation.1 | async-start | bytes 8912896 | tf_op jit(solution)/shard_map/all_gather | solution.py:127
  10.5 115.9 %all-gather.6.cloned.1.call-start = ((), (), s32[]{:S(2)}) async-start(), calls=%async_computation.2 | async-start | bytes 8912896 | tf_op jit(solution)/shard_map/all_gather | solution.py:128
  11.3 173.4 %all-gather.8.cloned.1.call-start = ((), (), s32[]{:S(2)}) async-start(), calls=%async_computation.3 | async-start | bytes 8912896 | tf_op jit(solution)/shard_map/all_gather | solution.py:148
  79.8 2.6 copy-start.8
  82.5 43.9 %copy-start = (bf16[128,2048]{1,0:T(8,128)(2,1)S(1)}, bf16[128,2048]{1,0:T(8,128)(2,1)}, u32[]{:S(2)}) copy-start(bf16[128,2048]{1,0:T(8,128)(2,1)} %param.21) | copy-start | bytes 1572868
  126.4 4.8 %copy-start.9 = (f32[2048]{0:T(1024)S(1)}, f32[2048]{0:T(1024)}, u32[]{:S(2)}) copy-start(f32[2048]{0:T(1024)} %param.28) | copy-start | bytes 24580
  126.4 5.9 %copy-start.6 = (f32[2048,6]{0,1:T(8,128)S(1)}, f32[2048,6]{0,1:T(8,128)}, u32[]{:S(2)}) copy-start(f32[2048,6]{0,1:T(8,128)} %param.36) | copy-start | bytes 147460
  126.4 5.9 %copy-start.7 = (s32[2048,6]{0,1:T(8,128)S(1)}, s32[2048,6]{0,1:T(8,128)}, u32[]{:S(2)}) copy-start(s32[2048,6]{0,1:T(8,128)} %param.35) | copy-start | bytes 147460
  184.7 14.2 %slice-start.2 = ((s8[5767168]{0:T(1024)(128)(4,1)}), s8[4194304]{0:T(1024)(128)(4,1)S(1)}, s32[]{:S(2)}) async-start(s8[5767168]{0:T(1024)(128)(4,1)} %bitcast.203), calls=%async_computation.6 | async-start | bytes 8388608
  189.5 9.4 %slice-start.3 = ((s8[5767168]{0:T(1024)(128)(4,1)}), s8[1572864]{0:T(1024)(128)(4,1)S(1)}, s32[]{:S(2)}) async-start(s8[5767168]{0:T(1024)(128)(4,1)} %bitcast.203), calls=%async_computation.7 | async-start | bytes 3145728
  189.5 16.5 %slice-start.4 = ((s8[5767168]{0:T(1024)(128)(4,1)}), s8[4194304]{0:T(1024)(128)(4,1)S(1)}, s32[]{:S(2)}) async-start(s8[5767168]{0:T(1024)(128)(4,1)} %bitcast.205), calls=%async_computation.8 | async-start | bytes 8388608
  198.9 7.1 %slice-start.5 = ((s8[5767168]{0:T(1024)(128)(4,1)}), s8[1572864]{0:T(1024)(128)(4,1)S(1)}, s32[]{:S(2)}) async-start(s8[5767168]{0:T(1024)(128)(4,1)} %bitcast.205), calls=%async_computation.9 | async-start | bytes 3145728
  206.0 7.5 %slice-start = ((s8[8388608]{0:T(1024)(128)(4,1)}), s8[4194304]{0:T(1024)(128)(4,1)S(1)}, s32[]{:S(2)}) async-start(s8[8388608]{0:T(1024)(128)(4,1)} %bitcast.183), calls=%async_computation.4 | async-start | bytes 8388608
  209.6 3.9 %slice-start.1 = ((s8[8388608]{0:T(1024)(128)(4,1)}), s8[4194304]{0:T(1024)(128)(4,1)S(1)}, s32[]{:S(2)}) async-start(s8[8388608]{0:T(1024)(128)(4,1)} %bitcast.183), calls=%async_computation.5 | async-start | bytes 8388608
  209.6 3.9 %copy-start.10 = (bf16[2048,176]{0,1:T(8,128)(2,1)S(1)}, bf16[2048,176]{0,1:T(8,128)(2,1)}, u32[]{:S(2)}) copy-start(bf16[2048,176]{0,1:T(8,128)(2,1)} %param.30) | copy-start | bytes 2162692
  209.6 3.9 %copy-start.11 = (bf16[2048,176]{0,1:T(8,128)(2,1)S(1)}, bf16[2048,176]{0,1:T(8,128)(2,1)}, u32[]{:S(2)}) copy-start(bf16[2048,176]{0,1:T(8,128)(2,1)} %param.29) | copy-start | bytes 2162692
  216.7 1.7 copy-start.12
  220.2 3.4 %copy-start.3 = (bf16[2048,1024]{1,0:T(8,128)(2,1)}, bf16[2048,1024]{1,0:T(8,128)(2,1)S(1)}, u32[]{:S(2)}) copy-start(bf16[2048,1024]{1,0:T(8,128)(2,1)S(1)} %fusion.27) | copy-start | bytes 12582916
  222.0 5.8 %collective-permute-start.8 = (bf16[4,2,128,1024]{3,2,1,0:T(8,128)(2,1)}, bf16[4,2,128,1024]{3,2,1,0:T(8,128)(2,1)}, u32[]{:S(2)}, u32[]{:S(2)}) collective-permute-start(bf16[4,2,128,1024]{3,2,1,0:T(8,128)(2,1)} %dynamic-slice_bitcast_fusion), channel_id=1, source_target_pairs={{0,1},{1,0},{2,3},{3,2},{4,5},{5,4},{6,7},{7,6},{8,9},{9,8},{10,11... | collective-permute-start | bytes 6291464 | tf_op jit(solution)/shard_map/ppermute | solution.py:68
  225.2 2.0 copy-start.1
  225.2 2.5 copy-start.13
  227.4 7.6 %collective-permute-start = (bf16[4,2,128,1024]{3,2,1,0:T(8,128)(2,1)S(1)}, bf16[4,2,128,1024]{3,2,1,0:T(8,128)(2,1)}, u32[]{:S(2)}, u32[]{:S(2)}) collective-permute-start(bf16[4,2,128,1024]{3,2,1,0:T(8,128)(2,1)S(1)} %dynamic-slice_bitcast_fusion.1), channel_id=1, source_target_pairs={{0,1},{1,0},{2,3},{3,2},{4,5},{5,4},{6,7},{7,6},{8,9},{9,8},{10,11... | collective-permute-start | bytes 6291464 | tf_op jit(solution)/shard_map/ppermute | solution.py:68
  231.0 4.1 %copy-start.2 = (bf16[2048,1024]{1,0:T(8,128)(2,1)S(1)}, bf16[2048,1024]{1,0:T(8,128)(2,1)}, u32[]{:S(2)}) copy-start(bf16[2048,1024]{1,0:T(8,128)(2,1)} %copy-done.1) | copy-start | bytes 12582916
  231.7 10.2 %collective-permute-start.9 = (bf16[2,128,512]{2,1,0:T(8,128)(2,1)S(1)}, bf16[2,128,512]{2,1,0:T(8,128)(2,1)S(1)}, u32[]{:S(2)}, u32[]{:S(2)}) collective-permute-start(bf16[2,128,512]{2,1,0:T(8,128)(2,1)S(1)} %fusion.83), channel_id=1, source_target_pairs={{0,4},{1,5},{2,6},{3,7},{4,8},{5,9},{6,10},{7,11},{8,12},{9,13},{1... | collective-permute-start | bytes 786440 | tf_op jit(solution)/shard_map/ppermute | solution.py:80
  233.2 9.0 %collective-permute-start.12 = (bf16[2,128,512]{2,1,0:T(8,128)(2,1)S(1)}, bf16[2,128,512]{2,1,0:T(8,128)(2,1)S(1)}, u32[]{:S(2)}, u32[]{:S(2)}) collective-permute-start(bf16[2,128,512]{2,1,0:T(8,128)(2,1)S(1)} %fusion.84), channel_id=1, source_target_pairs={{0,12},{1,13},{2,14},{3,15},{4,0},{5,1},{6,2},{7,3},{8,4},{9,5},{1... | collective-permute-start | bytes 786440 | tf_op jit(solution)/shard_map/ppermute | solution.py:81
  238.3 10.8 %collective-permute-start.1 = (bf16[2,128,512]{2,1,0:T(8,128)(2,1)S(1)}, bf16[2,128,512]{2,1,0:T(8,128)(2,1)S(1)}, u32[]{:S(2)}, u32[]{:S(2)}) collective-permute-start(bf16[2,128,512]{2,1,0:T(8,128)(2,1)S(1)} %fusion.81), channel_id=1, source_target_pairs={{0,4},{1,5},{2,6},{3,7},{4,8},{5,9},{6,10},{7,11},{8,12},{9,13},{1... | collective-permute-start | bytes 786440 | tf_op jit(solution)/shard_map/ppermute | solution.py:80
  238.9 10.3 %collective-permute-start.4 = (bf16[2,128,512]{2,1,0:T(8,128)(2,1)S(1)}, bf16[2,128,512]{2,1,0:T(8,128)(2,1)S(1)}, u32[]{:S(2)}, u32[]{:S(2)}) collective-permute-start(bf16[2,128,512]{2,1,0:T(8,128)(2,1)S(1)} %fusion.82), channel_id=1, source_target_pairs={{0,12},{1,13},{2,14},{3,15},{4,0},{5,1},{6,2},{7,3},{8,4},{9,5},{1... | collective-permute-start | bytes 786440 | tf_op jit(solution)/shard_map/ppermute | solution.py:81
  242.0 12.7 %collective-permute-start.10 = (bf16[2,128,512]{2,1,0:T(8,128)(2,1)S(1)}, bf16[2,128,512]{2,1,0:T(8,128)(2,1)S(1)}, u32[]{:S(2)}, u32[]{:S(2)}) collective-permute-start(bf16[2,128,512]{2,1,0:T(8,128)(2,1)S(1)} %fusion.70), channel_id=1, source_target_pairs={{0,4},{1,5},{2,6},{3,7},{4,8},{5,9},{6,10},{7,11},{8,12},{9,13},{1... | collective-permute-start | bytes 786440 | tf_op jit(solution)/shard_map/ppermute | solution.py:80
  242.3 12.5 %collective-permute-start.13 = (bf16[2,128,512]{2,1,0:T(8,128)(2,1)S(1)}, bf16[2,128,512]{2,1,0:T(8,128)(2,1)S(1)}, u32[]{:S(2)}, u32[]{:S(2)}) collective-permute-start(bf16[2,128,512]{2,1,0:T(8,128)(2,1)S(1)} %fusion.68), channel_id=1, source_target_pairs={{0,12},{1,13},{2,14},{3,15},{4,0},{5,1},{6,2},{7,3},{8,4},{9,5},{1... | collective-permute-start | bytes 786440 | tf_op jit(solution)/shard_map/ppermute | solution.py:81
  249.1 11.2 %collective-permute-start.2 = (bf16[2,128,512]{2,1,0:T(8,128)(2,1)S(1)}, bf16[2,128,512]{2,1,0:T(8,128)(2,1)S(1)}, u32[]{:S(2)}, u32[]{:S(2)}) collective-permute-start(bf16[2,128,512]{2,1,0:T(8,128)(2,1)S(1)} %fusion.74), channel_id=1, source_target_pairs={{0,4},{1,5},{2,6},{3,7},{4,8},{5,9},{6,10},{7,11},{8,12},{9,13},{1... | collective-permute-start | bytes 786440 | tf_op jit(solution)/shard_map/ppermute | solution.py:80
  249.3 11.1 %collective-permute-start.5 = (bf16[2,128,512]{2,1,0:T(8,128)(2,1)S(1)}, bf16[2,128,512]{2,1,0:T(8,128)(2,1)S(1)}, u32[]{:S(2)}, u32[]{:S(2)}) collective-permute-start(bf16[2,128,512]{2,1,0:T(8,128)(2,1)S(1)} %fusion.72), channel_id=1, source_target_pairs={{0,12},{1,13},{2,14},{3,15},{4,0},{5,1},{6,2},{7,3},{8,4},{9,5},{1... | collective-permute-start | bytes 786440 | tf_op jit(solution)/shard_map/ppermute | solution.py:81
  254.8 11.2 %collective-permute-start.11 = (bf16[2,128,512]{2,1,0:T(8,128)(2,1)S(1)}, bf16[2,128,512]{2,1,0:T(8,128)(2,1)S(1)}, u32[]{:S(2)}, u32[]{:S(2)}) collective-permute-start(bf16[2,128,512]{2,1,0:T(8,128)(2,1)S(1)} %fusion.69), channel_id=1, source_target_pairs={{0,4},{1,5},{2,6},{3,7},{4,8},{5,9},{6,10},{7,11},{8,12},{9,13},{1... | collective-permute-start | bytes 786440 | tf_op jit(solution)/shard_map/ppermute | solution.py:80
  254.9 11.1 %collective-permute-start.14 = (bf16[2,128,512]{2,1,0:T(8,128)(2,1)S(1)}, bf16[2,128,512]{2,1,0:T(8,128)(2,1)S(1)}, u32[]{:S(2)}, u32[]{:S(2)}) collective-permute-start(bf16[2,128,512]{2,1,0:T(8,128)(2,1)S(1)} %fusion.67), channel_id=1, source_target_pairs={{0,12},{1,13},{2,14},{3,15},{4,0},{5,1},{6,2},{7,3},{8,4},{9,5},{1... | collective-permute-start | bytes 786440 | tf_op jit(solution)/shard_map/ppermute | solution.py:81
  260.4 9.8 %collective-permute-start.3 = (bf16[2,128,512]{2,1,0:T(8,128)(2,1)S(1)}, bf16[2,128,512]{2,1,0:T(8,128)(2,1)S(1)}, u32[]{:S(2)}, u32[]{:S(2)}) collective-permute-start(bf16[2,128,512]{2,1,0:T(8,128)(2,1)S(1)} %fusion.73), channel_id=1, source_target_pairs={{0,4},{1,5},{2,6},{3,7},{4,8},{5,9},{6,10},{7,11},{8,12},{9,13},{1... | collective-permute-start | bytes 786440 | tf_op jit(solution)/shard_map/ppermute | solution.py:80
  260.5 12.0 %copy-start.4 = (bf16[2048,128]{1,0:T(8,128)(2,1)S(1)}, bf16[2048,128]{1,0:T(8,128)(2,1)}, u32[]{:S(2)}) copy-start(bf16[2048,128]{1,0:T(8,128)(2,1)} %get-tuple-element.114) | copy-start | bytes 1572868
  260.6 12.0 %copy-start.5 = (bf16[2048,128]{1,0:T(8,128)(2,1)S(1)}, bf16[2048,128]{1,0:T(8,128)(2,1)}, u32[]{:S(2)}) copy-start(bf16[2048,128]{1,0:T(8,128)(2,1)} %get-tuple-element.117) | copy-start | bytes 1572868
  260.6 9.7 %collective-permute-start.6 = (bf16[2,128,512]{2,1,0:T(8,128)(2,1)S(1)}, bf16[2,128,512]{2,1,0:T(8,128)(2,1)S(1)}, u32[]{:S(2)}, u32[]{:S(2)}) collective-permute-start(bf16[2,128,512]{2,1,0:T(8,128)(2,1)S(1)} %fusion.71), channel_id=1, source_target_pairs={{0,12},{1,13},{2,14},{3,15},{4,0},{5,1},{6,2},{7,3},{8,4},{9,5},{1... | collective-permute-start | bytes 786440 | tf_op jit(solution)/shard_map/ppermute | solution.py:81
  266.1 12.1 %collective-permute-start.15 = (bf16[128,1024]{1,0:T(8,128)(2,1)S(1)}, bf16[128,1024]{1,0:T(8,128)(2,1)}, u32[]{:S(2)}, u32[]{:S(2)}) collective-permute-start(bf16[128,1024]{1,0:T(8,128)(2,1)S(1)} %fusion.86), channel_id=1, source_target_pairs={{0,2},{1,3},{2,0},{3,1},{4,6},{5,7},{6,4},{7,5},{8,10},{9,11},{10,... | collective-permute-start | bytes 786440 | tf_op jit(solution)/shard_map/ppermute | solution.py:96
  271.1 8.1 %collective-permute-start.7 = (bf16[128,1024]{1,0:T(8,128)(2,1)}, bf16[128,1024]{1,0:T(8,128)(2,1)}, u32[]{:S(2)}, u32[]{:S(2)}) collective-permute-start(bf16[128,1024]{1,0:T(8,128)(2,1)} %fusion.85), channel_id=1, source_target_pairs={{0,2},{1,3},{2,0},{3,1},{4,6},{5,7},{6,4},{7,5},{8,10},{9,11},{10,... | collective-permute-start | bytes 786440 | tf_op jit(solution)/shard_map/ppermute | solution.py:96
Sparse Core Ops, SparseCore 0:
  10.6 54.5 all-gather.3
  66.9 58.6 all-gather.5
  132.4 52.2 all-gather.7
where the time goes:
time: 288 us
  waiting for transfers between devices  118 us (41%)
  matrix products  66 us (23%)
  starting transfers between devices  23.9 us (8%)
  other arithmetic  23 us (8%)
  blocking collectives  20.5 us (7%)
  local copies, waits for them, and re-layouts  15.6 us (5%)
  between operations  14.4 us (5%)
  loops' own time  6.69 us (2%)
    all_gather x1, waiting for transfers between devices, shards(): lax.all_gather(rms_scale(tokens, attention_gain), 'tensor', axis=0, tiled...  52.3 us
    all_gather x1, waiting for transfers between devices, shards(): normed_stream = lax.all_gather(normed_ffn, 'tensor', axis=0, tiled=True)  52 us
    all_to_all x1, blocking collectives, shards(): lax.all_to_all(context.reshape(groups, tok_dev, inner), 'tensor', split_a...  20.5 us
    ppermute x6, starting transfers between devices, ring_reduce_scatter(): recv_b = lax.ppermute(carry_b, 'tensor', backward_pairs)  17.7 us
    dot_general x4, matrix products, shards(): jnp.dot(rows, projection, preferred_element_type=jnp.float32)  14.6 us
    ppermute x6, waiting for transfers between devices, ring_reduce_scatter(): recv_f = lax.ppermute(carry_f, 'tensor', forward_pairs)  12.5 us
    dot_general x1, matrix products, shards(): jnp.dot(picked, expert_gate[local], preferred_element_type=jnp.float32)  9.35 us
    dot_general x2, matrix products, shards(): jnp.dot(expert_hidden[local], expert_down[local][:, columns], preferred_e...  7.49 us
  transfers between devices with their start and end apart: 19, of which 7 were waited for; matrix products, arithmetic and copies ran while one was open for 19% of the time, Pallas kernels for 0%

commit v1 on v0

--- a/solution.py
+++ b/solution.py
@@ -135,6 +135,7 @@
     context, keys, values = attend(projected, segment_ids, head_count)
     cache = jnp.stack([keys, values]).reshape(2, -1, PAGE, inner)
     kv_pages = jnp.zeros_like(cache).at[:, page_table].set(cache)
+    kv_pages, out_weight_all = lax.optimization_barrier((kv_pages, out_weight_all))
 
     received = lax.all_to_all(
         context.reshape(groups, tok_dev, inner), "tensor", split_axis=0, concat_axis=0, tiled=True

time: 288 us -> 289 us (level)
  blocking collectives: 20.5 us -> 0 us
  waiting for transfers between devices: 118 us -> 133 us
  starting transfers between devices: 23.9 us -> 28.7 us
    all_to_all x1 -> x0, blocking collectives: 20.5 us -> none  [shards(): lax.all_to_all(context.reshape(groups, tok_dev, inner), 'tensor', split_a...]
    all_gather x1, waiting for transfers between devices: 0.02 us -> 8.85 us  [shards(): out_weight_all = lax.all_gather(output_weight, 'tensor', axis=0, tiled=True)]
    ppermute x2, waiting for transfers between devices: 0.01 us -> 4.95 us  [ring_reduce_scatter(): got_side = lax.ppermute(give_side, 'tensor', side_pairs)]
    all_to_all x0 -> x1, starting transfers between devices: none -> 4.78 us  [shards(): lax.all_to_all(context.reshape(groups, tok_dev, inner), 'tensor', split_a...]
  transfers between devices with their start and end apart: 19 -> 20, of which waited for: 7 -> 11; matrix products, arithmetic and copies ran while one was open for 19% -> 18% of each run, Pallas kernels for 0% -> 0%
where the time goes in v1:
time: 289 us; the launch traced here: 288 us
  waiting for transfers between devices  133 us (46%)
  matrix products  68.6 us (24%)
  starting transfers between devices  28.7 us (10%)
  other arithmetic  22.4 us (8%)
  between operations  14.4 us (5%)
  local copies, waits for them, and re-layouts  13.9 us (5%)
  loops' own time  7.84 us (3%)
    all_gather x1, waiting for transfers between devices, shards(): lax.all_gather(rms_scale(tokens, attention_gain), 'tensor', axis=0, tiled...  52.4 us
    all_gather x1, waiting for transfers between devices, shards(): normed_stream = lax.all_gather(normed_ffn, 'tensor', axis=0, tiled=True)  51.6 us
    ppermute x6, starting transfers between devices, ring_reduce_scatter(): recv_b = lax.ppermute(carry_b, 'tensor', backward_pairs)  17.7 us
    dot_general x4, matrix products, shards(): jnp.dot(rows, projection, preferred_element_type=jnp.float32)  14.7 us
    ppermute x6, waiting for transfers between devices, ring_reduce_scatter(): recv_f = lax.ppermute(carry_f, 'tensor', forward_pairs)  12.5 us
    dot_general x1, matrix products, shards(): jnp.dot(picked, expert_gate[local], preferred_element_type=jnp.float32)  9.36 us
    all_gather x1, waiting for transfers between devices, shards(): out_weight_all = lax.all_gather(output_weight, 'tensor', axis=0, tiled=True)  8.85 us
    another operation x1, loops' own time, attend(): context = lax.map(one_block, starts).reshape(total_tokens, inner)  7.83 us
  transfers between devices with their start and end apart: 20, of which 11 were waited for; matrix products, arithmetic and copies ran while one was open for 18% of the time, Pallas kernels for 0%

profile of v1, /device:TPU:0, one launch (start us, length us, event | category | flops | bytes accessed | tf_op | source)
XLA Modules:
  0.0 288.5 jit_solution(475896424660539546)
XLA Ops:
  7.2 1.2 fusion.53
  8.4 2.0 fusion.55
  11.3 1.6 pad_maximum_fusion
  12.9 52.4 %all-gather.4.cloned.1.call-done = bf16[2048,2048]{1,0:T(8,128)(2,1)} async-done(((bf16[128,2048]{1,0:T(8,128)(2,1)}), bf16[2048,2048]{1,0:T(8,128)(2,1)}) %all-gather.4.cloned.1.call-update) | async-done | bytes 8388624 | tf_op jit(solution)/shard_map/all_gather | solution.py:127
  65.2 14.7 %while.21 = (s32[]{:T(128)}, bf16[4,512,384]{2,1,0:T(8,128)(2,1)}, bf16[4,512,2048]{2,1,0:T(8,128)(2,1)}, bf16[2048,384]{1,0:T(8,128)(2,1)S(1)}, s32[]{:T(128)}) while((s32[]{:T(128)}, bf16[4,512,384]{2,1,0:T(8,128)(2,1)}, bf16[4,512,2048]{2,1,0:T(8,128)(2,1)}, bf16[2048,384]{1,0:T(8,128)(2,1)S(1)}, s32[]{:T(128)}) %tuple.64), condition=%wide.region_2.3_spmd, body=%wide.region_1.2_spmd.sunk | while | flops 805502976 | bytes 4064325 | solution.py:129
  65.2 3.6 %fusion.120 = bf16[4,512,384]{2,1,0:T(8,128)(2,1)} fusion(bf16[4,512,384]{2,1,0:T(8,128)(2,1)} %get-tuple-element.203, s32[]{:T(128)S(6)} %copy.34, bf16[2048,384]{1,0:T(8,128)(2,1)S(1)} %get-tuple-element.210, bf16[4,512,2048]{2,1,0:T(8,128)(2,1)} %get-tuple-element.209), kind=kOutput, calls=%fused_computation.7.clone.1 | convolution fusion | flops 805502976 | bytes 4064256 | tf_op jit(solution)/shard_map/while/body/eval_jaxpr/dot_general | solution.py:130
  68.8 3.6 %fusion.120 = bf16[4,512,384]{2,1,0:T(8,128)(2,1)} fusion(bf16[4,512,384]{2,1,0:T(8,128)(2,1)} %get-tuple-element.203, s32[]{:T(128)S(6)} %copy.34, bf16[2048,384]{1,0:T(8,128)(2,1)S(1)} %get-tuple-element.210, bf16[4,512,2048]{2,1,0:T(8,128)(2,1)} %get-tuple-element.209), kind=kOutput, calls=%fused_computation.7.clone.1 | convolution fusion | flops 805502976 | bytes 4064256 | tf_op jit(solution)/shard_map/while/body/eval_jaxpr/dot_general | solution.py:130
  72.4 3.6 %fusion.120 = bf16[4,512,384]{2,1,0:T(8,128)(2,1)} fusion(bf16[4,512,384]{2,1,0:T(8,128)(2,1)} %get-tuple-element.203, s32[]{:T(128)S(6)} %copy.34, bf16[2048,384]{1,0:T(8,128)(2,1)S(1)} %get-tuple-element.210, bf16[4,512,2048]{2,1,0:T(8,128)(2,1)} %get-tuple-element.209), kind=kOutput, calls=%fused_computation.7.clone.1 | convolution fusion | flops 805502976 | bytes 4064256 | tf_op jit(solution)/shard_map/while/body/eval_jaxpr/dot_general | solution.py:130
  76.0 3.9 %fusion.120 = bf16[4,512,384]{2,1,0:T(8,128)(2,1)} fusion(bf16[4,512,384]{2,1,0:T(8,128)(2,1)} %get-tuple-element.203, s32[]{:T(128)S(6)} %copy.34, bf16[2048,384]{1,0:T(8,128)(2,1)S(1)} %get-tuple-element.210, bf16[4,512,2048]{2,1,0:T(8,128)(2,1)} %get-tuple-element.209), kind=kOutput, calls=%fused_computation.7.clone.1 | convolution fusion | flops 805502976 | bytes 4064256 | tf_op jit(solution)/shard_map/while/body/eval_jaxpr/dot_general | solution.py:130
  79.9 1.7 fusion.97
  81.6 27.1 %while.22 = (s32[]{:T(128)}, bf16[4,512,1,128]{3,1,2,0:T(8,128)(2,1)}, s32[4]{0:T(128)S(1)}, s32[2048]{0:T(1024)S(1)}, bf16[2048,1,128]{2,0,1:T(8,128)(2,1)S(1)}...) while((s32[]{:T(128)}, ...), condition=%wide.region_6.7_spmd.clone, body=%wide.region_3.6_spmd.clone.sunk | while | flops 548470272 | bytes 13922475 | solution.py:45
  84.9 1.3 fusion.122
  86.1 0.7 fusion.123
  86.8 1.5 fusion.124
  91.7 1.3 fusion.122
  93.6 1.5 fusion.124
  98.4 1.3 fusion.122
  99.7 0.7 fusion.123
  100.4 1.5 fusion.124
  105.2 1.3 fusion.122
  106.5 0.7 fusion.123
  107.2 1.5 fusion.124
  108.7 4.8 %all-to-all-start = ((bf16[16,128,128]{2,1,0:T(8,128)(2,1)}), bf16[16,128,128]{2,1,0:T(8,128)(2,1)S(1)}, u32[]{:S(2)}, u32[]{:S(2)}) async-start(bf16[16,128,128]{2,1,0:T(8,128)(2,1)} %bitcast.7), calls=%async_computation | async-start | bytes 1048576 | tf_op jit(solution)/shard_map/all_to_all | solution.py:140
  113.9 1.8 scatter_fusion
  115.7 8.8 %all-gather.6.cloned.1.call-done = bf16[2048,2048]{1,0:T(8,128)(2,1)} async-done(((bf16[128,2048]{1,0:T(8,128)(2,1)}), bf16[2048,2048]{1,0:T(8,128)(2,1)}) %all-gather.6.cloned.1.call-update) | async-done | bytes 8388624 | tf_op jit(solution)/shard_map/all_gather | solution.py:128
  124.6 1.6 all-to-all-done
  126.2 0.8 copy-done.5
  126.9 1.3 copy.23
  128.3 4.8 %multiply_reduce_fusion = (f32[128]{0:T(128)S(1)}, f32[128,2048]{1,0:T(8,128)S(1)}) fusion(bf16[128,2048]{0,1:T(8,128)(2,1)S(1)} %bitcast.193, bf16[2048,2048]{1,0:T(8,128)(2,1)} %all-gather.6.cloned.1.call-done, bf16[128,2048]{1,0:T(8,128)(2,1)S(1)} %copy-done), kind=kOutput, calls=%fused_computation.76 | convolution fusion | flops 1075314560 | bytes 10486272 | tf_op jit(solution)/shard_map/dot_general | solution.py:144
  133.1 1.0 multiply_convert_fusion.1
  134.5 51.6 %all-gather.8.cloned.1.call-done = bf16[2048,2048]{1,0:T(8,128)(2,1)} async-done(((bf16[128,2048]{1,0:T(8,128)(2,1)}), bf16[2048,2048]{1,0:T(8,128)(2,1)}) %all-gather.8.cloned.1.call-update) | async-done | bytes 8388624 | tf_op jit(solution)/shard_map/all_gather | solution.py:149
  186.1 4.8 %convolution_convert_fusion = bf16[16,64,2048]{2,1,0:T(8,128)(2,1)S(1)} fusion(bf16[16,128,2048]{2,1,0:T(8,128)(2,1)} %bitcast.182, s32[16,128]{1,0:T(8,128)S(1)} %bitcast_subtract_fusion, pred[16,128]{1,0:T(8,128)(4,1)S(1)} %broadcast_compare_fusion.1), kind=kOutput, calls=%fused_computation.38 | convolution fusion | flops 539230208 | bytes 12593152 | tf_op jit(solution)/shard_map/bst,btd->bsd/dot_general | solution.py:178
  190.9 9.4 %fusion.32 = f32[1024,1408]{1,0:T(8,128)S(1)} fusion(bf16[1024,2048]{1,0:T(8,128)(2,1)S(1)} %bitcast.185, bf16[1,2048,1408]{2,1,0:T(8,128)(2,1)} %param.32), kind=kOutput, calls=%fused_computation.33 | convolution fusion | flops 5905580032 | bytes 15728640 | tf_op jit(solution)/shard_map/dot_general | solution.py:182
  200.3 7.1 %multiply_convert_fusion = bf16[1024,1408]{1,0:T(8,128)(2,1)S(1)} fusion(f32[1024,1408]{1,0:T(8,128)S(1)} %fusion.32, bf16[1024,2048]{1,0:T(8,128)(2,1)S(1)} %bitcast.186, bf16[1,2048,1408]{2,1,0:T(8,128)(2,1)S(1)} %bitcast.203), kind=kOutput, calls=%fused_computation.35 | convolution fusion | flops 5914230784 | bytes 18612224 | tf_op jit(solution)/shard_map/dot_general | solution.py:184
  207.4 3.6 %fusion.45 = bf16[1024,1024]{1,0:T(8,128)(2,1)S(1)} fusion(bf16[1024,1408]{1,0:T(8,128)(2,1)S(1)} %multiply_convert_fusion, bf16[1408,2048]{1,0:T(8,128)(2,1)S(1)} %bitcast.206), kind=kOutput, calls=%fused_computation.51 | convolution fusion | flops 2953838592 | bytes 7864320 | tf_op jit(solution)/shard_map/dot_general | solution.py:198
  211.1 3.9 %fusion.42 = bf16[1024,1024]{1,0:T(8,128)(2,1)S(1)} fusion(bf16[1024,1408]{1,0:T(8,128)(2,1)S(1)} %multiply_convert_fusion, bf16[1408,2048]{1,0:T(8,128)(2,1)S(1)} %bitcast.207), kind=kOutput, calls=%fused_computation.50 | convolution fusion | flops 2953838592 | bytes 7864320 | tf_op jit(solution)/shard_map/dot_general | solution.py:198
  215.0 3.2 %fusion.49 = f32[2048,352]{0,1:T(8,128)S(1)} fusion(bf16[2048,2048]{1,0:T(8,128)(2,1)S(1)} %bitcast.184, bf16[2048,176]{0,1:T(8,128)(2,1)S(1)} %copy-done.10, bf16[2048,176]{0,1:T(8,128)(2,1)S(1)} %copy-done.11), kind=kOutput, calls=%fused_computation.57 | convolution fusion | flops 2955673600 | bytes 12713984 | tf_op jit(solution)/shard_map/dot_general | solution.py:173
  218.7 1.3 convolution_convert_fusion.1
  220.0 1.7 fusion.27
  221.7 1.8 dynamic-slice_bitcast_fusion
  223.8 1.3 convolution_convert_fusion.2
  225.1 1.7 fusion.29
  226.8 2.0 copy-done.2
  229.3 3.1 %convert_add_fusion = f32[4,2,128,1024]{3,2,1,0:T(8,128)S(1)} fusion(bf16[4,2,128,1024]{3,2,1,0:T(8,128)(2,1)} %collective-permute-done.8, bf16[4,2,2,128,1024]{4,3,2,1,0:T(8,128)(2,1)} %bitcast.192, s32[]{:T(128)S(6)} %select_n.135), kind=kLoop, calls=%fused_computation.36 | loop fusion | flops 3145728 | bytes 8388612 | tf_op jit(solution)/shard_map/add | solution.py:69
  233.2 1.6 collective-permute-start.9
  234.8 1.8 collective-permute-start.12
  236.6 2.5 convert_add_fusion.1
  240.4 3.0 %collective-permute-start.4 = (bf16[2,128,512]{2,1,0:T(8,128)(2,1)S(1)}, bf16[2,128,512]{2,1,0:T(8,128)(2,1)S(1)}, u32[]{:S(2)}, u32[]{:S(2)}) collective-permute-start(bf16[2,128,512]{2,1,0:T(8,128)(2,1)S(1)} %fusion.82), channel_id=1, source_target_pairs={{0,12},{1,13},{2,14},{3,15},{4,0},{5,1},{6,2},{7,3},{8,4},{9,5},{1... | collective-permute-start | bytes 786440 | tf_op jit(solution)/shard_map/ppermute | solution.py:81
  243.8 3.1 %collective-permute-start.13 = (bf16[2,128,512]{2,1,0:T(8,128)(2,1)S(1)}, bf16[2,128,512]{2,1,0:T(8,128)(2,1)S(1)}, u32[]{:S(2)}, u32[]{:S(2)}) collective-permute-start(bf16[2,128,512]{2,1,0:T(8,128)(2,1)S(1)} %fusion.68), channel_id=1, source_target_pairs={{0,12},{1,13},{2,14},{3,15},{4,0},{5,1},{6,2},{7,3},{8,4},{9,5},{1... | collective-permute-start | bytes 786440 | tf_op jit(solution)/shard_map/ppermute | solution.py:81
  246.9 3.7 %collective-permute-done.1 = bf16[2,128,512]{2,1,0:T(8,128)(2,1)S(1)} collective-permute-done((bf16[2,128,512]{2,1,0:T(8,128)(2,1)S(1)}, bf16[2,128,512]{2,1,0:T(8,128)(2,1)S(1)}, u32[]{:S(2)}, u32[]{:S(2)}) %collective-permute-start.1) | collective-permute-done | bytes 262176 | tf_op jit(solution)/shard_map/ppermute | solution.py:80
  250.8 3.3 %collective-permute-start.5 = (bf16[2,128,512]{2,1,0:T(8,128)(2,1)S(1)}, bf16[2,128,512]{2,1,0:T(8,128)(2,1)S(1)}, u32[]{:S(2)}, u32[]{:S(2)}) collective-permute-start(bf16[2,128,512]{2,1,0:T(8,128)(2,1)S(1)} %fusion.72), channel_id=1, source_target_pairs={{0,12},{1,13},{2,14},{3,15},{4,0},{5,1},{6,2},{7,3},{8,4},{9,5},{1... | collective-permute-start | bytes 786440 | tf_op jit(solution)/shard_map/ppermute | solution.py:81
  254.1 2.1 collective-permute-done.10
  256.4 3.3 %collective-permute-start.14 = (bf16[2,128,512]{2,1,0:T(8,128)(2,1)S(1)}, bf16[2,128,512]{2,1,0:T(8,128)(2,1)S(1)}, u32[]{:S(2)}, u32[]{:S(2)}) collective-permute-start(bf16[2,128,512]{2,1,0:T(8,128)(2,1)S(1)} %fusion.67), channel_id=1, source_target_pairs={{0,12},{1,13},{2,14},{3,15},{4,0},{5,1},{6,2},{7,3},{8,4},{9,5},{1... | collective-permute-start | bytes 786440 | tf_op jit(solution)/shard_map/ppermute | solution.py:81
  259.7 2.1 collective-permute-done.2
  262.1 3.3 %collective-permute-start.6 = (bf16[2,128,512]{2,1,0:T(8,128)(2,1)S(1)}, bf16[2,128,512]{2,1,0:T(8,128)(2,1)S(1)}, u32[]{:S(2)}, u32[]{:S(2)}) collective-permute-start(bf16[2,128,512]{2,1,0:T(8,128)(2,1)S(1)} %fusion.71), channel_id=1, source_target_pairs={{0,12},{1,13},{2,14},{3,15},{4,0},{5,1},{6,2},{7,3},{8,4},{9,5},{1... | collective-permute-start | bytes 786440 | tf_op jit(solution)/shard_map/ppermute | solution.py:81
  265.3 2.1 collective-permute-done.11
  267.6 1.5 collective-permute-start.15
  269.1 2.6 collective-permute-done.3
  271.9 0.7 fusion.85
  272.7 1.4 collective-permute-start.7
  274.2 1.0 fusion.61
  275.2 4.8 %collective-permute-done.7 = bf16[128,1024]{1,0:T(8,128)(2,1)} collective-permute-done((bf16[128,1024]{1,0:T(8,128)(2,1)}, bf16[128,1024]{1,0:T(8,128)(2,1)}, u32[]{:S(2)}, u32[]{:S(2)}) %collective-permute-start.7) | collective-permute-done | bytes 262176 | tf_op jit(solution)/shard_map/ppermute | solution.py:96
  280.0 1.0 fusion.66
  281.0 0.9 fusion.56
  (111 shorter events, 12.4 us)
Async XLA Ops:
  7.2 58.1 %all-gather.4.cloned.1.call-start = ((), (), s32[]{:S(2)}) async-start(), calls=%async_computation.1 | async-start | bytes 8912896 | tf_op jit(solution)/shard_map/all_gather | solution.py:127
  10.5 114.1 %all-gather.6.cloned.1.call-start = ((), (), s32[]{:S(2)}) async-start(), calls=%async_computation.2 | async-start | bytes 8912896 | tf_op jit(solution)/shard_map/all_gather | solution.py:128
  79.9 1.7 copy-start.8
  81.6 32.0 %copy-start.13 = (s32[16]{0:T(128)S(1)}, s32[16]{0:T(128)}, u32[]{:S(2)}) copy-start(s32[16]{0:T(128)} %param.37) | copy-start | bytes 196
  108.7 19.5 %copy-start = (bf16[128,2048]{1,0:T(8,128)(2,1)S(1)}, bf16[128,2048]{1,0:T(8,128)(2,1)}, u32[]{:S(2)}) copy-start(bf16[128,2048]{1,0:T(8,128)(2,1)} %param.21) | copy-start | bytes 1572868
  108.7 17.4 %all-to-all-start = ((bf16[16,128,128]{2,1,0:T(8,128)(2,1)}), bf16[16,128,128]{2,1,0:T(8,128)(2,1)S(1)}, u32[]{:S(2)}, u32[]{:S(2)}) async-start(bf16[16,128,128]{2,1,0:T(8,128)(2,1)} %bitcast.7), calls=%async_computation | async-start | bytes 1048576 | tf_op jit(solution)/shard_map/all_to_all | solution.py:140
  113.5 72.6 %all-gather.8.cloned.1.call-start = ((), (), s32[]{:S(2)}) async-start(), calls=%async_computation.3 | async-start | bytes 8912896 | tf_op jit(solution)/shard_map/all_gather | solution.py:149
  115.7 17.4 %copy-start.1 = (bf16[2,16,128,128]{3,2,1,0:T(8,128)(2,1)}, bf16[2,16,128,128]{3,2,1,0:T(8,128)(2,1)S(1)}, u32[]{:S(2)}) copy-start(bf16[2,16,128,128]{3,2,1,0:T(8,128)(2,1)S(1)} %scatter_fusion) | copy-start | bytes 3145732
  126.2 0.8 copy-start.5
  128.3 4.8 %copy-start.9 = (f32[2048]{0:T(1024)S(1)}, f32[2048]{0:T(1024)}, u32[]{:S(2)}) copy-start(f32[2048]{0:T(1024)} %param.28) | copy-start | bytes 24580
  128.3 5.8 %copy-start.6 = (f32[2048,6]{0,1:T(8,128)S(1)}, f32[2048,6]{0,1:T(8,128)}, u32[]{:S(2)}) copy-start(f32[2048,6]{0,1:T(8,128)} %param.36) | copy-start | bytes 147460
  128.3 5.8 %copy-start.7 = (s32[2048,6]{0,1:T(8,128)S(1)}, s32[2048,6]{0,1:T(8,128)}, u32[]{:S(2)}) copy-start(s32[2048,6]{0,1:T(8,128)} %param.35) | copy-start | bytes 147460
  186.1 14.2 %slice-start.2 = ((s8[5767168]{0:T(1024)(128)(4,1)}), s8[4194304]{0:T(1024)(128)(4,1)S(1)}, s32[]{:S(2)}) async-start(s8[5767168]{0:T(1024)(128)(4,1)} %bitcast.202), calls=%async_computation.6 | async-start | bytes 8388608
  190.9 9.4 %slice-start.3 = ((s8[5767168]{0:T(1024)(128)(4,1)}), s8[1572864]{0:T(1024)(128)(4,1)S(1)}, s32[]{:S(2)}) async-start(s8[5767168]{0:T(1024)(128)(4,1)} %bitcast.202), calls=%async_computation.7 | async-start | bytes 3145728
  190.9 16.5 %slice-start.4 = ((s8[5767168]{0:T(1024)(128)(4,1)}), s8[4194304]{0:T(1024)(128)(4,1)S(1)}, s32[]{:S(2)}) async-start(s8[5767168]{0:T(1024)(128)(4,1)} %bitcast.204), calls=%async_computation.8 | async-start | bytes 8388608
  200.3 7.1 %slice-start.5 = ((s8[5767168]{0:T(1024)(128)(4,1)}), s8[1572864]{0:T(1024)(128)(4,1)S(1)}, s32[]{:S(2)}) async-start(s8[5767168]{0:T(1024)(128)(4,1)} %bitcast.204), calls=%async_computation.9 | async-start | bytes 3145728
  207.4 7.5 %slice-start = ((s8[8388608]{0:T(1024)(128)(4,1)}), s8[4194304]{0:T(1024)(128)(4,1)S(1)}, s32[]{:S(2)}) async-start(s8[8388608]{0:T(1024)(128)(4,1)} %bitcast.183), calls=%async_computation.4 | async-start | bytes 8388608
  211.1 3.9 %slice-start.1 = ((s8[8388608]{0:T(1024)(128)(4,1)}), s8[4194304]{0:T(1024)(128)(4,1)S(1)}, s32[]{:S(2)}) async-start(s8[8388608]{0:T(1024)(128)(4,1)} %bitcast.183), calls=%async_computation.5 | async-start | bytes 8388608
  211.1 3.9 %copy-start.10 = (bf16[2048,176]{0,1:T(8,128)(2,1)S(1)}, bf16[2048,176]{0,1:T(8,128)(2,1)}, u32[]{:S(2)}) copy-start(bf16[2048,176]{0,1:T(8,128)(2,1)} %param.30) | copy-start | bytes 2162692
  211.1 3.9 %copy-start.11 = (bf16[2048,176]{0,1:T(8,128)(2,1)S(1)}, bf16[2048,176]{0,1:T(8,128)(2,1)}, u32[]{:S(2)}) copy-start(bf16[2048,176]{0,1:T(8,128)(2,1)} %param.29) | copy-start | bytes 2162692
  218.3 1.7 copy-start.12
  221.7 3.4 %copy-start.4 = (bf16[2048,1024]{1,0:T(8,128)(2,1)}, bf16[2048,1024]{1,0:T(8,128)(2,1)S(1)}, u32[]{:S(2)}) copy-start(bf16[2048,1024]{1,0:T(8,128)(2,1)S(1)} %fusion.27) | copy-start | bytes 12582916
  223.5 5.8 %collective-permute-start.8 = (bf16[4,2,128,1024]{3,2,1,0:T(8,128)(2,1)}, bf16[4,2,128,1024]{3,2,1,0:T(8,128)(2,1)}, u32[]{:S(2)}, u32[]{:S(2)}) collective-permute-start(bf16[4,2,128,1024]{3,2,1,0:T(8,128)(2,1)} %dynamic-slice_bitcast_fusion), channel_id=1, source_target_pairs={{0,1},{1,0},{2,3},{3,2},{4,5},{5,4},{6,7},{7,6},{8,9},{9,8},{10,11... | collective-permute-start | bytes 6291464 | tf_op jit(solution)/shard_map/ppermute | solution.py:68
  226.8 2.0 copy-start.2
  229.0 7.6 %collective-permute-start = (bf16[4,2,128,1024]{3,2,1,0:T(8,128)(2,1)S(1)}, bf16[4,2,128,1024]{3,2,1,0:T(8,128)(2,1)}, u32[]{:S(2)}, u32[]{:S(2)}) collective-permute-start(bf16[4,2,128,1024]{3,2,1,0:T(8,128)(2,1)S(1)} %dynamic-slice_bitcast_fusion.1), channel_id=1, source_target_pairs={{0,1},{1,0},{2,3},{3,2},{4,5},{5,4},{6,7},{7,6},{8,9},{9,8},{10,11... | collective-permute-start | bytes 6291464 | tf_op jit(solution)/shard_map/ppermute | solution.py:68
  232.5 4.1 %copy-start.3 = (bf16[2048,1024]{1,0:T(8,128)(2,1)S(1)}, bf16[2048,1024]{1,0:T(8,128)(2,1)}, u32[]{:S(2)}) copy-start(bf16[2048,1024]{1,0:T(8,128)(2,1)} %copy-done.2) | copy-start | bytes 12582916
  233.2 10.2 %collective-permute-start.9 = (bf16[2,128,512]{2,1,0:T(8,128)(2,1)S(1)}, bf16[2,128,512]{2,1,0:T(8,128)(2,1)S(1)}, u32[]{:S(2)}, u32[]{:S(2)}) collective-permute-start(bf16[2,128,512]{2,1,0:T(8,128)(2,1)S(1)} %fusion.83), channel_id=1, source_target_pairs={{0,4},{1,5},{2,6},{3,7},{4,8},{5,9},{6,10},{7,11},{8,12},{9,13},{1... | collective-permute-start | bytes 786440 | tf_op jit(solution)/shard_map/ppermute | solution.py:80
  234.8 9.0 %collective-permute-start.12 = (bf16[2,128,512]{2,1,0:T(8,128)(2,1)S(1)}, bf16[2,128,512]{2,1,0:T(8,128)(2,1)S(1)}, u32[]{:S(2)}, u32[]{:S(2)}) collective-permute-start(bf16[2,128,512]{2,1,0:T(8,128)(2,1)S(1)} %fusion.84), channel_id=1, source_target_pairs={{0,12},{1,13},{2,14},{3,15},{4,0},{5,1},{6,2},{7,3},{8,4},{9,5},{1... | collective-permute-start | bytes 786440 | tf_op jit(solution)/shard_map/ppermute | solution.py:81
  239.8 10.8 %collective-permute-start.1 = (bf16[2,128,512]{2,1,0:T(8,128)(2,1)S(1)}, bf16[2,128,512]{2,1,0:T(8,128)(2,1)S(1)}, u32[]{:S(2)}, u32[]{:S(2)}) collective-permute-start(bf16[2,128,512]{2,1,0:T(8,128)(2,1)S(1)} %fusion.81), channel_id=1, source_target_pairs={{0,4},{1,5},{2,6},{3,7},{4,8},{5,9},{6,10},{7,11},{8,12},{9,13},{1... | collective-permute-start | bytes 786440 | tf_op jit(solution)/shard_map/ppermute | solution.py:80
  240.4 10.3 %collective-permute-start.4 = (bf16[2,128,512]{2,1,0:T(8,128)(2,1)S(1)}, bf16[2,128,512]{2,1,0:T(8,128)(2,1)S(1)}, u32[]{:S(2)}, u32[]{:S(2)}) collective-permute-start(bf16[2,128,512]{2,1,0:T(8,128)(2,1)S(1)} %fusion.82), channel_id=1, source_target_pairs={{0,12},{1,13},{2,14},{3,15},{4,0},{5,1},{6,2},{7,3},{8,4},{9,5},{1... | collective-permute-start | bytes 786440 | tf_op jit(solution)/shard_map/ppermute | solution.py:81
  243.5 12.7 %collective-permute-start.10 = (bf16[2,128,512]{2,1,0:T(8,128)(2,1)S(1)}, bf16[2,128,512]{2,1,0:T(8,128)(2,1)S(1)}, u32[]{:S(2)}, u32[]{:S(2)}) collective-permute-start(bf16[2,128,512]{2,1,0:T(8,128)(2,1)S(1)} %fusion.70), channel_id=1, source_target_pairs={{0,4},{1,5},{2,6},{3,7},{4,8},{5,9},{6,10},{7,11},{8,12},{9,13},{1... | collective-permute-start | bytes 786440 | tf_op jit(solution)/shard_map/ppermute | solution.py:80
  243.8 12.5 %collective-permute-start.13 = (bf16[2,128,512]{2,1,0:T(8,128)(2,1)S(1)}, bf16[2,128,512]{2,1,0:T(8,128)(2,1)S(1)}, u32[]{:S(2)}, u32[]{:S(2)}) collective-permute-start(bf16[2,128,512]{2,1,0:T(8,128)(2,1)S(1)} %fusion.68), channel_id=1, source_target_pairs={{0,12},{1,13},{2,14},{3,15},{4,0},{5,1},{6,2},{7,3},{8,4},{9,5},{1... | collective-permute-start | bytes 786440 | tf_op jit(solution)/shard_map/ppermute | solution.py:81
  250.6 11.2 %collective-permute-start.2 = (bf16[2,128,512]{2,1,0:T(8,128)(2,1)S(1)}, bf16[2,128,512]{2,1,0:T(8,128)(2,1)S(1)}, u32[]{:S(2)}, u32[]{:S(2)}) collective-permute-start(bf16[2,128,512]{2,1,0:T(8,128)(2,1)S(1)} %fusion.74), channel_id=1, source_target_pairs={{0,4},{1,5},{2,6},{3,7},{4,8},{5,9},{6,10},{7,11},{8,12},{9,13},{1... | collective-permute-start | bytes 786440 | tf_op jit(solution)/shard_map/ppermute | solution.py:80
  250.8 11.1 %collective-permute-start.5 = (bf16[2,128,512]{2,1,0:T(8,128)(2,1)S(1)}, bf16[2,128,512]{2,1,0:T(8,128)(2,1)S(1)}, u32[]{:S(2)}, u32[]{:S(2)}) collective-permute-start(bf16[2,128,512]{2,1,0:T(8,128)(2,1)S(1)} %fusion.72), channel_id=1, source_target_pairs={{0,12},{1,13},{2,14},{3,15},{4,0},{5,1},{6,2},{7,3},{8,4},{9,5},{1... | collective-permute-start | bytes 786440 | tf_op jit(solution)/shard_map/ppermute | solution.py:81
  256.3 11.2 %collective-permute-start.11 = (bf16[2,128,512]{2,1,0:T(8,128)(2,1)S(1)}, bf16[2,128,512]{2,1,0:T(8,128)(2,1)S(1)}, u32[]{:S(2)}, u32[]{:S(2)}) collective-permute-start(bf16[2,128,512]{2,1,0:T(8,128)(2,1)S(1)} %fusion.69), channel_id=1, source_target_pairs={{0,4},{1,5},{2,6},{3,7},{4,8},{5,9},{6,10},{7,11},{8,12},{9,13},{1... | collective-permute-start | bytes 786440 | tf_op jit(solution)/shard_map/ppermute | solution.py:80
  256.4 11.1 %collective-permute-start.14 = (bf16[2,128,512]{2,1,0:T(8,128)(2,1)S(1)}, bf16[2,128,512]{2,1,0:T(8,128)(2,1)S(1)}, u32[]{:S(2)}, u32[]{:S(2)}) collective-permute-start(bf16[2,128,512]{2,1,0:T(8,128)(2,1)S(1)} %fusion.67), channel_id=1, source_target_pairs={{0,12},{1,13},{2,14},{3,15},{4,0},{5,1},{6,2},{7,3},{8,4},{9,5},{1... | collective-permute-start | bytes 786440 | tf_op jit(solution)/shard_map/ppermute | solution.py:81
  261.9 9.9 %collective-permute-start.3 = (bf16[2,128,512]{2,1,0:T(8,128)(2,1)S(1)}, bf16[2,128,512]{2,1,0:T(8,128)(2,1)S(1)}, u32[]{:S(2)}, u32[]{:S(2)}) collective-permute-start(bf16[2,128,512]{2,1,0:T(8,128)(2,1)S(1)} %fusion.73), channel_id=1, source_target_pairs={{0,4},{1,5},{2,6},{3,7},{4,8},{5,9},{6,10},{7,11},{8,12},{9,13},{1... | collective-permute-start | bytes 786440 | tf_op jit(solution)/shard_map/ppermute | solution.py:80
  262.1 9.8 %collective-permute-start.6 = (bf16[2,128,512]{2,1,0:T(8,128)(2,1)S(1)}, bf16[2,128,512]{2,1,0:T(8,128)(2,1)S(1)}, u32[]{:S(2)}, u32[]{:S(2)}) collective-permute-start(bf16[2,128,512]{2,1,0:T(8,128)(2,1)S(1)} %fusion.71), channel_id=1, source_target_pairs={{0,12},{1,13},{2,14},{3,15},{4,0},{5,1},{6,2},{7,3},{8,4},{9,5},{1... | collective-permute-start | bytes 786440 | tf_op jit(solution)/shard_map/ppermute | solution.py:81
  267.6 6.6 %collective-permute-start.15 = (bf16[128,1024]{1,0:T(8,128)(2,1)S(1)}, bf16[128,1024]{1,0:T(8,128)(2,1)}, u32[]{:S(2)}, u32[]{:S(2)}) collective-permute-start(bf16[128,1024]{1,0:T(8,128)(2,1)S(1)} %fusion.86), channel_id=1, source_target_pairs={{0,2},{1,3},{2,0},{3,1},{4,6},{5,7},{6,4},{7,5},{8,10},{9,11},{10,... | collective-permute-start | bytes 786440 | tf_op jit(solution)/shard_map/ppermute | solution.py:96
  272.7 7.3 %collective-permute-start.7 = (bf16[128,1024]{1,0:T(8,128)(2,1)}, bf16[128,1024]{1,0:T(8,128)(2,1)}, u32[]{:S(2)}, u32[]{:S(2)}) collective-permute-start(bf16[128,1024]{1,0:T(8,128)(2,1)} %fusion.85), channel_id=1, source_target_pairs={{0,2},{1,3},{2,0},{3,1},{4,6},{5,7},{6,4},{7,5},{8,10},{9,11},{10,... | collective-permute-start | bytes 786440 | tf_op jit(solution)/shard_map/ppermute | solution.py:96
Sparse Core Ops, SparseCore 0:
  10.6 54.5 all-gather.3
  66.9 57.5 all-gather.5
  134.2 51.8 all-gather.7

commit v2 on v0

--- a/solution.py
+++ b/solution.py
@@ -53,7 +53,7 @@
     return jnp.dot(hidden, down_w, preferred_element_type=jnp.float32).astype(jnp.bfloat16)
 
 
-def ring_reduce_scatter(partial, groups):
+def ring_reduce_scatter(partial, groups, direction):
     ring = groups // 4
     rows = partial.shape[0] // groups
     width = partial.shape[1]
@@ -67,32 +67,17 @@
     give = lax.dynamic_index_in_dim(blocks, 1 - core, axis=2, keepdims=False)
     got = lax.ppermute(give, "tensor", core_pairs)
     summed = keep.astype(jnp.float32) + got.astype(jnp.float32)
-    half = width // 2
-    forward_part = summed[..., :half]
-    backward_part = summed[..., half:]
-    forward_pairs = [(t, ((t // 4 + 1) % ring) * 4 + t % 4) for t in range(groups)]
-    backward_pairs = [(t, ((t // 4 + ring - 1) % ring) * 4 + t % 4) for t in range(groups)]
-    carry_f = lax.dynamic_index_in_dim(forward_part, (y + ring - 1) % ring, 0, False)
-    carry_b = lax.dynamic_index_in_dim(backward_part, (y + 1) % ring, 0, False)
-    carry_f = carry_f.astype(jnp.bfloat16)
-    carry_b = carry_b.astype(jnp.bfloat16)
+    ring_pairs = [(t, ((t // 4 + direction) % ring) * 4 + t % 4) for t in range(groups)]
+    carry = lax.dynamic_index_in_dim(summed, (y + ring - direction) % ring, 0, False)
+    carry = carry.astype(jnp.bfloat16)
     for step in range(ring - 1):
-        recv_f = lax.ppermute(carry_f, "tensor", forward_pairs)
-        recv_b = lax.ppermute(carry_b, "tensor", backward_pairs)
-        index_f = (y + 2 * ring - step - 2) % ring
-        index_b = (y + step + 2) % ring
-        acc_f = recv_f.astype(jnp.float32) + lax.dynamic_index_in_dim(
-            forward_part, index_f, 0, False
-        )
-        acc_b = recv_b.astype(jnp.float32) + lax.dynamic_index_in_dim(
-            backward_part, index_b, 0, False
-        )
-        carry_f = acc_f.astype(jnp.bfloat16)
-        carry_b = acc_b.astype(jnp.bfloat16)
-    mine = jnp.concatenate([acc_f, acc_b], axis=-1)
+        received = lax.ppermute(carry, "tensor", ring_pairs)
+        index = (y + 2 * ring - direction * (step + 2)) % ring
+        acc = received.astype(jnp.float32) + lax.dynamic_index_in_dim(summed, index, 0, False)
+        carry = acc.astype(jnp.bfloat16)
     side_pairs = [(t, t ^ 2) for t in range(groups)]
-    keep_side = lax.dynamic_index_in_dim(mine, side, 0, False)
-    give_side = lax.dynamic_index_in_dim(mine, 1 - side, 0, False).astype(jnp.bfloat16)
+    keep_side = lax.dynamic_index_in_dim(acc, side, 0, False)
+    give_side = lax.dynamic_index_in_dim(acc, 1 - side, 0, False).astype(jnp.bfloat16)
     got_side = lax.ppermute(give_side, "tensor", side_pairs)
     return keep_side + got_side.astype(jnp.float32)
 
@@ -206,7 +191,7 @@
             term = term + weights[local].reshape(-1, 1) * back.reshape(-1, piece_width).astype(
                 jnp.float32
             )
-        outs.append(ring_reduce_scatter(term.astype(jnp.bfloat16), groups))
+        outs.append(ring_reduce_scatter(term.astype(jnp.bfloat16), groups, 1 - 2 * (k % 2)))
     ffn_out = jnp.concatenate(outs, axis=1)
     layer_out = (residual.astype(jnp.float32) + ffn_out).astype(jnp.bfloat16)
     return (layer_out, kv_pages)

time: 288 us -> 303 us (1.052)
  waiting for transfers between devices: 118 us -> 136 us
  starting transfers between devices: 23.9 us -> 13.2 us
  other arithmetic: 23 us -> 29.5 us
    ppermute x12 -> x6, waiting for transfers between devices: 12.5 us -> 28.5 us  [ring_reduce_scatter(): received = lax.ppermute(carry, 'tensor', ring_pairs)]
    ppermute x12 -> x6, starting transfers between devices: 20.4 us -> 10.7 us  [ring_reduce_scatter(): received = lax.ppermute(carry, 'tensor', ring_pairs)]
    convert_element_type x10 -> x4, other arithmetic: 1.36 us -> 5.59 us  [ring_reduce_scatter(): carry = acc.astype(jnp.bfloat16)]
  transfers between devices with their start and end apart: 19 -> 13, of which waited for: 7 -> 9; matrix products, arithmetic and copies ran while one was open for 19% -> 19% of each run, Pallas kernels for 0% -> 0%
where the time goes in v2:
time: 303 us; the launch traced here: 302 us
  waiting for transfers between devices  136 us (45%)
  matrix products  66 us (22%)
  other arithmetic  29.5 us (10%)
  blocking collectives  20 us (7%)
  local copies, waits for them, and re-layouts  16.2 us (5%)
  between operations  14.4 us (5%)
  starting transfers between devices  13.2 us (4%)
  loops' own time  6.95 us (2%)
    all_gather x1, waiting for transfers between devices, shards(): lax.all_gather(rms_scale(tokens, attention_gain), 'tensor', axis=0, tiled...  52.3 us
    all_gather x1, waiting for transfers between devices, shards(): normed_stream = lax.all_gather(normed_ffn, 'tensor', axis=0, tiled=True)  52 us
    ppermute x6, waiting for transfers between devices, ring_reduce_scatter(): received = lax.ppermute(carry, 'tensor', ring_pairs)  28.5 us
    all_to_all x1, blocking collectives, shards(): lax.all_to_all(context.reshape(groups, tok_dev, inner), 'tensor', split_a...  20 us
    dot_general x4, matrix products, shards(): jnp.dot(rows, projection, preferred_element_type=jnp.float32)  14.7 us
    ppermute x6, starting transfers between devices, ring_reduce_scatter(): received = lax.ppermute(carry, 'tensor', ring_pairs)  10.7 us
    dot_general x1, matrix products, shards(): jnp.dot(picked, expert_gate[local], preferred_element_type=jnp.float32)  9.36 us
    dot_general x2, matrix products, shards(): jnp.dot(expert_hidden[local], expert_down[local][:, columns], preferred_e...  7.49 us
  transfers between devices with their start and end apart: 13, of which 9 were waited for; matrix products, arithmetic and copies ran while one was open for 19% of the time, Pallas kernels for 0%

profile of v2, /device:TPU:0, one launch (start us, length us, event | category | flops | bytes accessed | tf_op | source)
XLA Modules:
  0.0 302.3 jit_solution(14235379711390223367)
XLA Ops:
  7.2 1.2 fusion.53
  8.4 2.0 fusion.55
  11.3 1.6 pad_maximum_fusion
  12.9 52.3 %all-gather.4.cloned.1.call-done = bf16[2048,2048]{1,0:T(8,128)(2,1)} async-done(((bf16[128,2048]{1,0:T(8,128)(2,1)}), bf16[2048,2048]{1,0:T(8,128)(2,1)}) %all-gather.4.cloned.1.call-update) | async-done | bytes 8388624 | tf_op jit(solution)/shard_map/all_gather | solution.py:112
  65.2 14.7 %while.21 = (s32[]{:T(128)}, bf16[4,512,384]{2,1,0:T(8,128)(2,1)}, bf16[4,512,2048]{2,1,0:T(8,128)(2,1)}, bf16[2048,384]{1,0:T(8,128)(2,1)S(1)}, s32[]{:T(128)}) while((s32[]{:T(128)}, bf16[4,512,384]{2,1,0:T(8,128)(2,1)}, bf16[4,512,2048]{2,1,0:T(8,128)(2,1)}, bf16[2048,384]{1,0:T(8,128)(2,1)S(1)}, s32[]{:T(128)}) %tuple.60), condition=%wide.region_2.3_spmd, body=%wide.region_1.2_spmd.sunk | while | flops 805502976 | bytes 4064325 | solution.py:114
  65.2 3.6 %fusion.102 = bf16[4,512,384]{2,1,0:T(8,128)(2,1)} fusion(bf16[4,512,384]{2,1,0:T(8,128)(2,1)} %get-tuple-element.195, s32[]{:T(128)S(6)} %copy.34, bf16[2048,384]{1,0:T(8,128)(2,1)S(1)} %get-tuple-element.202, bf16[4,512,2048]{2,1,0:T(8,128)(2,1)} %get-tuple-element.201), kind=kOutput, calls=%fused_computation.7.clone.1 | convolution fusion | flops 805502976 | bytes 4064256 | tf_op jit(solution)/shard_map/while/body/eval_jaxpr/dot_general | solution.py:115
  68.8 3.6 %fusion.102 = bf16[4,512,384]{2,1,0:T(8,128)(2,1)} fusion(bf16[4,512,384]{2,1,0:T(8,128)(2,1)} %get-tuple-element.195, s32[]{:T(128)S(6)} %copy.34, bf16[2048,384]{1,0:T(8,128)(2,1)S(1)} %get-tuple-element.202, bf16[4,512,2048]{2,1,0:T(8,128)(2,1)} %get-tuple-element.201), kind=kOutput, calls=%fused_computation.7.clone.1 | convolution fusion | flops 805502976 | bytes 4064256 | tf_op jit(solution)/shard_map/while/body/eval_jaxpr/dot_general | solution.py:115
  72.4 3.6 %fusion.102 = bf16[4,512,384]{2,1,0:T(8,128)(2,1)} fusion(bf16[4,512,384]{2,1,0:T(8,128)(2,1)} %get-tuple-element.195, s32[]{:T(128)S(6)} %copy.34, bf16[2048,384]{1,0:T(8,128)(2,1)S(1)} %get-tuple-element.202, bf16[4,512,2048]{2,1,0:T(8,128)(2,1)} %get-tuple-element.201), kind=kOutput, calls=%fused_computation.7.clone.1 | convolution fusion | flops 805502976 | bytes 4064256 | tf_op jit(solution)/shard_map/while/body/eval_jaxpr/dot_general | solution.py:115
  76.0 3.9 %fusion.102 = bf16[4,512,384]{2,1,0:T(8,128)(2,1)} fusion(bf16[4,512,384]{2,1,0:T(8,128)(2,1)} %get-tuple-element.195, s32[]{:T(128)S(6)} %copy.34, bf16[2048,384]{1,0:T(8,128)(2,1)S(1)} %get-tuple-element.202, bf16[4,512,2048]{2,1,0:T(8,128)(2,1)} %get-tuple-element.201), kind=kOutput, calls=%fused_computation.7.clone.1 | convolution fusion | flops 805502976 | bytes 4064256 | tf_op jit(solution)/shard_map/while/body/eval_jaxpr/dot_general | solution.py:115
  79.9 2.6 fusion.79
  82.5 23.5 %while.22 = (s32[]{:T(128)}, bf16[4,512,1,128]{3,1,2,0:T(8,128)(2,1)S(1)}, s32[4]{0:T(128)S(1)}, s32[2048]{0:T(1024)S(1)}, bf16[2048,1,128]{2,0,1:T(8,128)(2,1)S...) while((s32[]{:T(128)}, ...), condition=%wide.region_6.7_spmd.clone, body=%wide.region_3.6_spmd.clone.sunk | while | flops 548470272 | bytes 13922475 | solution.py:45
  85.5 1.3 fusion.104
  86.8 0.7 fusion.105
  87.5 0.9 fusion.106
  91.4 1.3 fusion.104
  93.4 0.9 fusion.106
  97.3 1.3 fusion.104
  99.2 0.9 fusion.106
  103.2 1.3 fusion.104
  105.1 0.9 fusion.106
  106.1 20.0 %all_to_all.5 = bf16[16,128,128]{2,1,0:T(8,128)(2,1)S(1)} all-to-all(bf16[16,128,128]{2,1,0:T(8,128)(2,1)S(1)} %bitcast.172), channel_id=1, replica_groups=mesh['dp'=8,'tensor'=16] {'tensor'}, dimensions={0} | all-to-all | bytes 1048576 | tf_op jit(solution)/shard_map/all_to_all | solution.py:124
  126.4 4.8 %multiply_reduce_fusion = (f32[128]{0:T(128)S(1)}, f32[128,2048]{1,0:T(8,128)S(1)}) fusion(bf16[128,2048]{0,1:T(8,128)(2,1)S(1)} %bitcast.165, bf16[2048,2048]{1,0:T(8,128)(2,1)} %all-gather.6.cloned.1.call-done, bf16[128,2048]{1,0:T(8,128)(2,1)S(1)} %copy-done.2), kind=kOutput, calls=%fused_computation.80 | convolution fusion | flops 1075314560 | bytes 10486272 | tf_op jit(solution)/shard_map/dot_general | solution.py:128
  131.2 1.0 multiply_convert_fusion.1
  132.7 52.0 %all-gather.8.cloned.1.call-done = bf16[2048,2048]{1,0:T(8,128)(2,1)} async-done(((bf16[128,2048]{1,0:T(8,128)(2,1)}), bf16[2048,2048]{1,0:T(8,128)(2,1)}) %all-gather.8.cloned.1.call-update) | async-done | bytes 8388624 | tf_op jit(solution)/shard_map/all_gather | solution.py:133
  184.7 4.8 %convolution_convert_fusion = bf16[16,64,2048]{2,1,0:T(8,128)(2,1)S(1)} fusion(bf16[16,128,2048]{2,1,0:T(8,128)(2,1)} %bitcast.154, s32[16,128]{1,0:T(8,128)S(1)} %bitcast_subtract_fusion, pred[16,128]{1,0:T(8,128)(4,1)S(1)} %broadcast_compare_fusion.1), kind=kOutput, calls=%fused_computation.38 | convolution fusion | flops 539230208 | bytes 12593152 | tf_op jit(solution)/shard_map/bst,btd->bsd/dot_general | solution.py:162
  189.5 9.4 %fusion.32 = f32[1024,1408]{1,0:T(8,128)S(1)} fusion(bf16[1024,2048]{1,0:T(8,128)(2,1)S(1)} %bitcast.157, bf16[1,2048,1408]{2,1,0:T(8,128)(2,1)} %param.32), kind=kOutput, calls=%fused_computation.33 | convolution fusion | flops 5905580032 | bytes 15728640 | tf_op jit(solution)/shard_map/dot_general | solution.py:166
  198.9 7.0 %multiply_convert_fusion = bf16[1024,1408]{1,0:T(8,128)(2,1)S(1)} fusion(f32[1024,1408]{1,0:T(8,128)S(1)} %fusion.32, bf16[1024,2048]{1,0:T(8,128)(2,1)S(1)} %bitcast.158, bf16[1,2048,1408]{2,1,0:T(8,128)(2,1)S(1)} %bitcast.176), kind=kOutput, calls=%fused_computation.35 | convolution fusion | flops 5914230784 | bytes 18612224 | tf_op jit(solution)/shard_map/dot_general | solution.py:168
  206.0 3.6 %fusion.45 = bf16[1024,1024]{1,0:T(8,128)(2,1)S(1)} fusion(bf16[1024,1408]{1,0:T(8,128)(2,1)S(1)} %multiply_convert_fusion, bf16[1408,2048]{1,0:T(8,128)(2,1)S(1)} %bitcast.179), kind=kOutput, calls=%fused_computation.51 | convolution fusion | flops 2953838592 | bytes 7864320 | tf_op jit(solution)/shard_map/dot_general | solution.py:182
  209.7 3.9 %fusion.42 = bf16[1024,1024]{1,0:T(8,128)(2,1)S(1)} fusion(bf16[1024,1408]{1,0:T(8,128)(2,1)S(1)} %multiply_convert_fusion, bf16[1408,2048]{1,0:T(8,128)(2,1)S(1)} %bitcast.180), kind=kOutput, calls=%fused_computation.50 | convolution fusion | flops 2953838592 | bytes 7864320 | tf_op jit(solution)/shard_map/dot_general | solution.py:182
  213.6 3.2 %fusion.49 = f32[2048,352]{0,1:T(8,128)S(1)} fusion(bf16[2048,2048]{1,0:T(8,128)(2,1)S(1)} %bitcast.156, bf16[2048,176]{0,1:T(8,128)(2,1)S(1)} %copy-done.15, bf16[2048,176]{0,1:T(8,128)(2,1)S(1)} %copy-done.16), kind=kOutput, calls=%fused_computation.57 | convolution fusion | flops 2955673600 | bytes 12713984 | tf_op jit(solution)/shard_map/dot_general | solution.py:157
  217.2 1.3 convolution_convert_fusion.1
  218.5 1.3 convolution_convert_fusion.2
  219.8 1.7 fusion.27
  221.5 1.8 dynamic-slice_bitcast_fusion
  223.6 1.7 fusion.29
  225.3 2.0 copy-done.4
  227.8 3.3 %convert_add_fusion = f32[4,2,128,1024]{3,2,1,0:T(8,128)S(1)} fusion(bf16[4,2,128,1024]{3,2,1,0:T(8,128)(2,1)} %collective-permute-done.5, bf16[4,2,2,128,1024]{4,3,2,1,0:T(8,128)(2,1)} %bitcast.164, s32[]{:T(128)S(6)} %select_n.114), kind=kLoop, calls=%fused_computation.36 | loop fusion | flops 3145728 | bytes 8388612 | tf_op jit(solution)/shard_map/add | solution.py:69
  231.1 1.0 fusion.62
  232.1 2.7 collective-permute-start.6
  234.9 2.5 convert_add_fusion.1
  237.4 2.0 copy-done
  239.6 7.2 %collective-permute-done.6 = bf16[2,128,1024]{2,1,0:T(8,128)(2,1)} collective-permute-done((bf16[2,128,1024]{2,1,0:T(8,128)(2,1)}, bf16[2,128,1024]{2,1,0:T(8,128)(2,1)}, u32[]{:S(2)}, u32[]{:S(2)}) %collective-permute-start.6) | collective-permute-done | bytes 524320 | tf_op jit(solution)/shard_map/ppermute | solution.py:74
  246.8 1.5 fusion.58
  248.3 3.8 %collective-permute-start.7 = (bf16[2,128,1024]{2,1,0:T(8,128)(2,1)S(1)}, bf16[2,128,1024]{2,1,0:T(8,128)(2,1)S(1)}, u32[]{:S(2)}, u32[]{:S(2)}) collective-permute-start(bf16[2,128,1024]{2,1,0:T(8,128)(2,1)S(1)} %fusion.58), channel_id=1, source_target_pairs={{0,12},{1,13},{2,14},{3,15},{4,0},{5,1},{6,2},{7,3},{8,4},{9,5},{1... | collective-permute-start | bytes 1572872 | tf_op jit(solution)/shard_map/ppermute | solution.py:74
  252.0 2.5 collective-permute-done.1
  254.5 1.4 fusion.60
  256.0 6.8 %collective-permute-done.7 = bf16[2,128,1024]{2,1,0:T(8,128)(2,1)S(1)} collective-permute-done((bf16[2,128,1024]{2,1,0:T(8,128)(2,1)S(1)}, bf16[2,128,1024]{2,1,0:T(8,128)(2,1)S(1)}, u32[]{:S(2)}, u32[]{:S(2)}) %collective-permute-start.7) | collective-permute-done | bytes 524320 | tf_op jit(solution)/shard_map/ppermute | solution.py:74
  262.8 1.4 fusion.57
  264.2 4.0 %collective-permute-start.8 = (bf16[2,128,1024]{2,1,0:T(8,128)(2,1)S(1)}, bf16[2,128,1024]{2,1,0:T(8,128)(2,1)S(1)}, u32[]{:S(2)}, u32[]{:S(2)}) collective-permute-start(bf16[2,128,1024]{2,1,0:T(8,128)(2,1)S(1)} %fusion.57), channel_id=1, source_target_pairs={{0,12},{1,13},{2,14},{3,15},{4,0},{5,1},{6,2},{7,3},{8,4},{9,5},{1... | collective-permute-start | bytes 1572872 | tf_op jit(solution)/shard_map/ppermute | solution.py:74
  268.2 1.9 collective-permute-done.2
  270.1 1.4 fusion.59
  271.6 6.4 %collective-permute-done.8 = bf16[2,128,1024]{2,1,0:T(8,128)(2,1)S(1)} collective-permute-done((bf16[2,128,1024]{2,1,0:T(8,128)(2,1)S(1)}, bf16[2,128,1024]{2,1,0:T(8,128)(2,1)S(1)}, u32[]{:S(2)}, u32[]{:S(2)}) %collective-permute-start.8) | collective-permute-done | bytes 524320 | tf_op jit(solution)/shard_map/ppermute | solution.py:74
  278.0 1.4 bitcast_add_fusion
  279.4 0.8 fusion.70
  280.2 0.9 collective-permute-start.9
  281.1 3.7 %collective-permute-done.3 = bf16[2,128,1024]{2,1,0:T(8,128)(2,1)S(1)} collective-permute-done((bf16[2,128,1024]{2,1,0:T(8,128)(2,1)S(1)}, bf16[2,128,1024]{2,1,0:T(8,128)(2,1)S(1)}, u32[]{:S(2)}, u32[]{:S(2)}) %collective-permute-start.3) | collective-permute-done | bytes 524320 | tf_op jit(solution)/shard_map/ppermute | solution.py:74
  284.8 1.4 bitcast_add_fusion.3
  286.2 0.8 fusion.69
  287.0 0.9 collective-permute-start.4
  288.2 1.6 scatter_fusion
  289.9 1.5 bitcast_add_fusion.6
  291.3 2.3 collective-permute-done.4
  293.7 1.2 bitcast_add_fusion.7
  294.9 0.9 fusion.56
  (98 shorter events, 10.5 us)
Async XLA Ops:
  7.2 58.1 %all-gather.4.cloned.1.call-start = ((), (), s32[]{:S(2)}) async-start(), calls=%async_computation.1 | async-start | bytes 8912896 | tf_op jit(solution)/shard_map/all_gather | solution.py:112
  10.5 115.9 %all-gather.6.cloned.1.call-start = ((), (), s32[]{:S(2)}) async-start(), calls=%async_computation.2 | async-start | bytes 8912896 | tf_op jit(solution)/shard_map/all_gather | solution.py:113
  11.3 173.4 %all-gather.8.cloned.1.call-start = ((), (), s32[]{:S(2)}) async-start(), calls=%async_computation.3 | async-start | bytes 8912896 | tf_op jit(solution)/shard_map/all_gather | solution.py:133
  79.9 2.6 copy-start.13
  82.5 43.9 %copy-start.2 = (bf16[128,2048]{1,0:T(8,128)(2,1)S(1)}, bf16[128,2048]{1,0:T(8,128)(2,1)}, u32[]{:S(2)}) copy-start(bf16[128,2048]{1,0:T(8,128)(2,1)} %param.21) | copy-start | bytes 1572868
  126.4 4.8 %copy-start.14 = (f32[2048]{0:T(1024)S(1)}, f32[2048]{0:T(1024)}, u32[]{:S(2)}) copy-start(f32[2048]{0:T(1024)} %param.28) | copy-start | bytes 24580
  126.4 5.9 %copy-start.11 = (f32[2048,6]{0,1:T(8,128)S(1)}, f32[2048,6]{0,1:T(8,128)}, u32[]{:S(2)}) copy-start(f32[2048,6]{0,1:T(8,128)} %param.36) | copy-start | bytes 147460
  126.4 5.9 %copy-start.12 = (s32[2048,6]{0,1:T(8,128)S(1)}, s32[2048,6]{0,1:T(8,128)}, u32[]{:S(2)}) copy-start(s32[2048,6]{0,1:T(8,128)} %param.35) | copy-start | bytes 147460
  184.7 14.2 %slice-start.2 = ((s8[5767168]{0:T(1024)(128)(4,1)}), s8[4194304]{0:T(1024)(128)(4,1)S(1)}, s32[]{:S(2)}) async-start(s8[5767168]{0:T(1024)(128)(4,1)} %bitcast.175), calls=%async_computation.6 | async-start | bytes 8388608
  189.5 9.4 %slice-start.3 = ((s8[5767168]{0:T(1024)(128)(4,1)}), s8[1572864]{0:T(1024)(128)(4,1)S(1)}, s32[]{:S(2)}) async-start(s8[5767168]{0:T(1024)(128)(4,1)} %bitcast.175), calls=%async_computation.7 | async-start | bytes 3145728
  189.5 16.5 %slice-start.4 = ((s8[5767168]{0:T(1024)(128)(4,1)}), s8[4194304]{0:T(1024)(128)(4,1)S(1)}, s32[]{:S(2)}) async-start(s8[5767168]{0:T(1024)(128)(4,1)} %bitcast.177), calls=%async_computation.8 | async-start | bytes 8388608
  198.9 7.1 %slice-start.5 = ((s8[5767168]{0:T(1024)(128)(4,1)}), s8[1572864]{0:T(1024)(128)(4,1)S(1)}, s32[]{:S(2)}) async-start(s8[5767168]{0:T(1024)(128)(4,1)} %bitcast.177), calls=%async_computation.9 | async-start | bytes 3145728
  206.0 7.5 %slice-start = ((s8[8388608]{0:T(1024)(128)(4,1)}), s8[4194304]{0:T(1024)(128)(4,1)S(1)}, s32[]{:S(2)}) async-start(s8[8388608]{0:T(1024)(128)(4,1)} %bitcast.155), calls=%async_computation.4 | async-start | bytes 8388608
  209.7 3.9 %slice-start.1 = ((s8[8388608]{0:T(1024)(128)(4,1)}), s8[4194304]{0:T(1024)(128)(4,1)S(1)}, s32[]{:S(2)}) async-start(s8[8388608]{0:T(1024)(128)(4,1)} %bitcast.155), calls=%async_computation.5 | async-start | bytes 8388608
  209.7 3.9 %copy-start.15 = (bf16[2048,176]{0,1:T(8,128)(2,1)S(1)}, bf16[2048,176]{0,1:T(8,128)(2,1)}, u32[]{:S(2)}) copy-start(bf16[2048,176]{0,1:T(8,128)(2,1)} %param.30) | copy-start | bytes 2162692
  209.7 3.9 %copy-start.16 = (bf16[2048,176]{0,1:T(8,128)(2,1)S(1)}, bf16[2048,176]{0,1:T(8,128)(2,1)}, u32[]{:S(2)}) copy-start(bf16[2048,176]{0,1:T(8,128)(2,1)} %param.29) | copy-start | bytes 2162692
  218.5 1.3 copy-start.17
  221.5 3.7 %copy-start.6 = (bf16[2048,1024]{1,0:T(8,128)(2,1)}, bf16[2048,1024]{1,0:T(8,128)(2,1)S(1)}, u32[]{:S(2)}) copy-start(bf16[2048,1024]{1,0:T(8,128)(2,1)S(1)} %fusion.27) | copy-start | bytes 12582916
  223.3 4.5 %collective-permute-start.5 = (bf16[4,2,128,1024]{3,2,1,0:T(8,128)(2,1)}, bf16[4,2,128,1024]{3,2,1,0:T(8,128)(2,1)}, u32[]{:S(2)}, u32[]{:S(2)}) collective-permute-start(bf16[4,2,128,1024]{3,2,1,0:T(8,128)(2,1)} %dynamic-slice_bitcast_fusion), channel_id=1, source_target_pairs={{0,1},{1,0},{2,3},{3,2},{4,5},{5,4},{6,7},{7,6},{8,9},{9,8},{10,11... | collective-permute-start | bytes 6291464 | tf_op jit(solution)/shard_map/ppermute | solution.py:68
  225.3 2.0 copy-start.4
  227.5 7.4 %collective-permute-start = (bf16[4,2,128,1024]{3,2,1,0:T(8,128)(2,1)S(1)}, bf16[4,2,128,1024]{3,2,1,0:T(8,128)(2,1)}, u32[]{:S(2)}, u32[]{:S(2)}) collective-permute-start(bf16[4,2,128,1024]{3,2,1,0:T(8,128)(2,1)S(1)} %dynamic-slice_bitcast_fusion.1), channel_id=1, source_target_pairs={{0,1},{1,0},{2,3},{3,2},{4,5},{5,4},{6,7},{7,6},{8,9},{9,8},{10,11... | collective-permute-start | bytes 6291464 | tf_op jit(solution)/shard_map/ppermute | solution.py:68
  227.8 7.0 %copy-start.5 = (bf16[2048,1024]{1,0:T(8,128)(2,1)S(1)}, bf16[2048,1024]{1,0:T(8,128)(2,1)}, u32[]{:S(2)}) copy-start(bf16[2048,1024]{1,0:T(8,128)(2,1)} %copy-done.4) | copy-start | bytes 12582916
  231.1 3.7 %copy-start.1 = (f32[4,2,128,1024]{3,2,1,0:T(8,128)}, f32[4,2,128,1024]{3,2,1,0:T(8,128)S(1)}, u32[]{:S(2)}) copy-start(f32[4,2,128,1024]{3,2,1,0:T(8,128)S(1)} %convert_add_fusion) | copy-start | bytes 12582916
  232.1 14.6 %collective-permute-start.6 = (bf16[2,128,1024]{2,1,0:T(8,128)(2,1)}, bf16[2,128,1024]{2,1,0:T(8,128)(2,1)}, u32[]{:S(2)}, u32[]{:S(2)}) collective-permute-start(bf16[2,128,1024]{2,1,0:T(8,128)(2,1)} %fusion.62), channel_id=1, source_target_pairs={{0,12},{1,13},{2,14},{3,15},{4,0},{5,1},{6,2},{7,3},{8,4},{9,5},{1... | collective-permute-start | bytes 1572872 | tf_op jit(solution)/shard_map/ppermute | solution.py:74
  237.4 2.0 copy-start
  239.5 15.1 %collective-permute-start.1 = (bf16[2,128,1024]{2,1,0:T(8,128)(2,1)S(1)}, bf16[2,128,1024]{2,1,0:T(8,128)(2,1)S(1)}, u32[]{:S(2)}, u32[]{:S(2)}) collective-permute-start(bf16[2,128,1024]{2,1,0:T(8,128)(2,1)S(1)} %fusion.61), channel_id=1, source_target_pairs={{0,4},{1,5},{2,6},{3,7},{4,8},{5,9},{6,10},{7,11},{8,12},{9,13},{1... | collective-permute-start | bytes 1572872 | tf_op jit(solution)/shard_map/ppermute | solution.py:74
  239.6 32.0 %copy-start.18 = (s32[16]{0:T(128)S(1)}, s32[16]{0:T(128)}, u32[]{:S(2)}) copy-start(s32[16]{0:T(128)} %param.37) | copy-start | bytes 196
  248.3 14.5 %collective-permute-start.7 = (bf16[2,128,1024]{2,1,0:T(8,128)(2,1)S(1)}, bf16[2,128,1024]{2,1,0:T(8,128)(2,1)S(1)}, u32[]{:S(2)}, u32[]{:S(2)}) collective-permute-start(bf16[2,128,1024]{2,1,0:T(8,128)(2,1)S(1)} %fusion.58), channel_id=1, source_target_pairs={{0,12},{1,13},{2,14},{3,15},{4,0},{5,1},{6,2},{7,3},{8,4},{9,5},{1... | collective-permute-start | bytes 1572872 | tf_op jit(solution)/shard_map/ppermute | solution.py:74
  255.9 14.2 %collective-permute-start.2 = (bf16[2,128,1024]{2,1,0:T(8,128)(2,1)S(1)}, bf16[2,128,1024]{2,1,0:T(8,128)(2,1)S(1)}, u32[]{:S(2)}, u32[]{:S(2)}) collective-permute-start(bf16[2,128,1024]{2,1,0:T(8,128)(2,1)S(1)} %fusion.60), channel_id=1, source_target_pairs={{0,4},{1,5},{2,6},{3,7},{4,8},{5,9},{6,10},{7,11},{8,12},{9,13},{1... | collective-permute-start | bytes 1572872 | tf_op jit(solution)/shard_map/ppermute | solution.py:74
  264.2 13.9 %collective-permute-start.8 = (bf16[2,128,1024]{2,1,0:T(8,128)(2,1)S(1)}, bf16[2,128,1024]{2,1,0:T(8,128)(2,1)S(1)}, u32[]{:S(2)}, u32[]{:S(2)}) collective-permute-start(bf16[2,128,1024]{2,1,0:T(8,128)(2,1)S(1)} %fusion.57), channel_id=1, source_target_pairs={{0,12},{1,13},{2,14},{3,15},{4,0},{5,1},{6,2},{7,3},{8,4},{9,5},{1... | collective-permute-start | bytes 1572872 | tf_op jit(solution)/shard_map/ppermute | solution.py:74
  268.2 19.7 %copy-start.9 = (bf16[2048,128]{1,0:T(8,128)(2,1)S(1)}, bf16[2048,128]{1,0:T(8,128)(2,1)}, u32[]{:S(2)}) copy-start(bf16[2048,128]{1,0:T(8,128)(2,1)} %get-tuple-element.110) | copy-start | bytes 1572868
  268.2 19.7 %copy-start.10 = (bf16[2048,128]{1,0:T(8,128)(2,1)S(1)}, bf16[2048,128]{1,0:T(8,128)(2,1)}, u32[]{:S(2)}) copy-start(bf16[2048,128]{1,0:T(8,128)(2,1)} %get-tuple-element.113) | copy-start | bytes 1572868
  271.5 13.3 %collective-permute-start.3 = (bf16[2,128,1024]{2,1,0:T(8,128)(2,1)S(1)}, bf16[2,128,1024]{2,1,0:T(8,128)(2,1)S(1)}, u32[]{:S(2)}, u32[]{:S(2)}) collective-permute-start(bf16[2,128,1024]{2,1,0:T(8,128)(2,1)S(1)} %fusion.59), channel_id=1, source_target_pairs={{0,4},{1,5},{2,6},{3,7},{4,8},{5,9},{6,10},{7,11},{8,12},{9,13},{1... | collective-permute-start | bytes 1572872 | tf_op jit(solution)/shard_map/ppermute | solution.py:74
  279.4 8.6 %copy-start.7 = (f32[2,128,1024]{2,1,0:T(8,128)}, f32[2,128,1024]{2,1,0:T(8,128)S(1)}, u32[]{:S(2)}) copy-start(f32[2,128,1024]{2,1,0:T(8,128)S(1)} %bitcast_add_fusion) | copy-start | bytes 3145732
  280.2 9.6 %collective-permute-start.9 = (bf16[128,1024]{1,0:T(8,128)(2,1)}, bf16[128,1024]{1,0:T(8,128)(2,1)S(1)}, u32[]{:S(2)}, u32[]{:S(2)}) collective-permute-start(bf16[128,1024]{1,0:T(8,128)(2,1)} %fusion.70), channel_id=1, source_target_pairs={{0,2},{1,3},{2,0},{3,1},{4,6},{5,7},{6,4},{7,5},{8,10},{9,11},{10,... | collective-permute-start | bytes 786440 | tf_op jit(solution)/shard_map/ppermute | solution.py:81
  286.1 1.9 copy-start.8
  287.0 6.7 %collective-permute-start.4 = (bf16[128,1024]{1,0:T(8,128)(2,1)}, bf16[128,1024]{1,0:T(8,128)(2,1)}, u32[]{:S(2)}, u32[]{:S(2)}) collective-permute-start(bf16[128,1024]{1,0:T(8,128)(2,1)} %fusion.69), channel_id=1, source_target_pairs={{0,2},{1,3},{2,0},{3,1},{4,6},{5,7},{6,4},{7,5},{8,10},{9,11},{10,... | collective-permute-start | bytes 786440 | tf_op jit(solution)/shard_map/ppermute | solution.py:81
  289.8 6.0 %copy-start.3 = (bf16[2,16,128,128]{3,2,1,0:T(8,128)(2,1)}, bf16[2,16,128,128]{3,2,1,0:T(8,128)(2,1)S(1)}, u32[]{:S(2)}) copy-start(bf16[2,16,128,128]{3,2,1,0:T(8,128)(2,1)S(1)} %scatter_fusion) | copy-start | bytes 3145732
Sparse Core Ops, SparseCore 0:
  10.6 54.5 all-gather.3
  66.9 58.6 all-gather.5
  132.4 52.2 all-gather.7

commit v3 on v0

--- a/solution.py
+++ b/solution.py
@@ -206,7 +206,14 @@
             term = term + weights[local].reshape(-1, 1) * back.reshape(-1, piece_width).astype(
                 jnp.float32
             )
-        outs.append(ring_reduce_scatter(term.astype(jnp.bfloat16), groups))
+        if k == 0:
+            outs.append(
+                lax.psum_scatter(
+                    term.astype(jnp.bfloat16), "tensor", scatter_dimension=0, tiled=True
+                ).astype(jnp.float32)
+            )
+        else:
+            outs.append(ring_reduce_scatter(term.astype(jnp.bfloat16), groups))
     ffn_out = jnp.concatenate(outs, axis=1)
     layer_out = (residual.astype(jnp.float32) + ffn_out).astype(jnp.bfloat16)
     return (layer_out, kv_pages)

time: 288 us -> 299 us (1.038)
  waiting for transfers between devices: 118 us -> 135 us
  starting transfers between devices: 23.9 us -> 10.5 us
  other arithmetic: 23 us -> 27.9 us
    ppermute x6 -> x3, waiting for transfers between devices: 12.5 us -> 23.9 us  [ring_reduce_scatter(): recv_f = lax.ppermute(carry_f, 'tensor', forward_pairs)]
    ppermute x6 -> x3, starting transfers between devices: 17.7 us -> 7.31 us  [ring_reduce_scatter(): recv_b = lax.ppermute(carry_b, 'tensor', backward_pairs)]
    ppermute x2 -> x1, waiting for transfers between devices: 0.01 us -> 4.04 us  [ring_reduce_scatter(): got = lax.ppermute(give, 'tensor', core_pairs)]
    dot_general x1, matrix products: 4.77 us -> 1.24 us  [shards(): jnp.einsum('bst,btd->bsd', onehots[local], token_blocks, preferred_elemen...]
    convert_element_type x4 -> x2, other arithmetic: 0.28 us -> 3.8 us  [ring_reduce_scatter(): carry_f = acc_f.astype(jnp.bfloat16)]
    dot_general x1, matrix products: 3.17 us -> 6.5 us  [shards(): jnp.dot(normed_stream, shared_columns, preferred_element_type=jnp.float32)]
    unnamed x40 -> x48, local copies, waits for them, and re-layouts: 2.12 us -> 5.31 us
    convert_element_type x4 -> x2, other arithmetic: 0.3 us -> 3.44 us  [ring_reduce_scatter(): carry_b = acc_b.astype(jnp.bfloat16)]
  transfers between devices with their start and end apart: 19 -> 12, of which waited for: 7 -> 7; matrix products, arithmetic and copies ran while one was open for 19% -> 22% of each run, Pallas kernels for 0% -> 0%
where the time goes in v3:
time: 299 us; the launch traced here: 298 us
  waiting for transfers between devices  135 us (45%)
  matrix products  67 us (22%)
  other arithmetic  27.9 us (9%)
  blocking collectives  18.8 us (6%)
  local copies, waits for them, and re-layouts  16.8 us (6%)
  between operations  14.3 us (5%)
  starting transfers between devices  10.5 us (4%)
  loops' own time  7.77 us (3%)
    all_gather x1, waiting for transfers between devices, shards(): lax.all_gather(rms_scale(tokens, attention_gain), 'tensor', axis=0, tiled...  52.3 us
    all_gather x1, waiting for transfers between devices, shards(): normed_stream = lax.all_gather(normed_ffn, 'tensor', axis=0, tiled=True)  51.8 us
    ppermute x3, waiting for transfers between devices, ring_reduce_scatter(): recv_f = lax.ppermute(carry_f, 'tensor', forward_pairs)  23.9 us
    all_to_all x1, blocking collectives, shards(): lax.all_to_all(context.reshape(groups, tok_dev, inner), 'tensor', split_a...  18.8 us
    dot_general x4, matrix products, shards(): jnp.dot(rows, projection, preferred_element_type=jnp.float32)  14.7 us
    dot_general x2, matrix products, shards(): jnp.dot(expert_hidden[local], expert_down[local][:, columns], preferred_e...  9.73 us
    another operation x1, loops' own time, attend(): context = lax.map(one_block, starts).reshape(total_tokens, inner)  7.76 us
    ppermute x3, starting transfers between devices, ring_reduce_scatter(): recv_b = lax.ppermute(carry_b, 'tensor', backward_pairs)  7.31 us
  transfers between devices with their start and end apart: 12, of which 7 were waited for; matrix products, arithmetic and copies ran while one was open for 22% of the time, Pallas kernels for 0%

profile of v3, /device:TPU:0, one launch (start us, length us, event | category | flops | bytes accessed | tf_op | source)
XLA Modules:
  0.0 297.9 jit_solution(10547612465156042564)
XLA Ops:
  7.2 1.2 fusion.53
  8.4 2.0 fusion.55
  10.6 0.7 all-gather.6.cloned.1.call-update
  11.3 1.6 pad_maximum_fusion
  12.9 52.3 %all-gather.4.cloned.1.call-done = bf16[2048,2048]{1,0:T(8,128)(2,1)} async-done(((bf16[128,2048]{1,0:T(8,128)(2,1)}), bf16[2048,2048]{1,0:T(8,128)(2,1)}) %all-gather.4.cloned.1.call-update) | async-done | bytes 8388624 | tf_op jit(solution)/shard_map/all_gather | solution.py:127
  65.2 14.7 %while.21 = (s32[]{:T(128)}, bf16[4,512,384]{2,1,0:T(8,128)(2,1)}, bf16[4,512,2048]{2,1,0:T(8,128)(2,1)}, bf16[2048,384]{1,0:T(8,128)(2,1)S(1)}, s32[]{:T(128)}) while((s32[]{:T(128)}, bf16[4,512,384]{2,1,0:T(8,128)(2,1)}, bf16[4,512,2048]{2,1,0:T(8,128)(2,1)}, bf16[2048,384]{1,0:T(8,128)(2,1)S(1)}, s32[]{:T(128)}) %tuple.63), condition=%wide.region_2.3_spmd, body=%wide.region_1.2_spmd.sunk | while | flops 805502976 | bytes 4064325 | solution.py:129
  65.2 3.6 %fusion.107 = bf16[4,512,384]{2,1,0:T(8,128)(2,1)} fusion(bf16[4,512,384]{2,1,0:T(8,128)(2,1)} %get-tuple-element.197, s32[]{:T(128)S(6)} %copy.31, bf16[2048,384]{1,0:T(8,128)(2,1)S(1)} %get-tuple-element.204, bf16[4,512,2048]{2,1,0:T(8,128)(2,1)} %get-tuple-element.203), kind=kOutput, calls=%fused_computation.7.clone.1 | convolution fusion | flops 805502976 | bytes 4064256 | tf_op jit(solution)/shard_map/while/body/eval_jaxpr/dot_general | solution.py:130
  68.8 3.6 %fusion.107 = bf16[4,512,384]{2,1,0:T(8,128)(2,1)} fusion(bf16[4,512,384]{2,1,0:T(8,128)(2,1)} %get-tuple-element.197, s32[]{:T(128)S(6)} %copy.31, bf16[2048,384]{1,0:T(8,128)(2,1)S(1)} %get-tuple-element.204, bf16[4,512,2048]{2,1,0:T(8,128)(2,1)} %get-tuple-element.203), kind=kOutput, calls=%fused_computation.7.clone.1 | convolution fusion | flops 805502976 | bytes 4064256 | tf_op jit(solution)/shard_map/while/body/eval_jaxpr/dot_general | solution.py:130
  72.4 3.6 %fusion.107 = bf16[4,512,384]{2,1,0:T(8,128)(2,1)} fusion(bf16[4,512,384]{2,1,0:T(8,128)(2,1)} %get-tuple-element.197, s32[]{:T(128)S(6)} %copy.31, bf16[2048,384]{1,0:T(8,128)(2,1)S(1)} %get-tuple-element.204, bf16[4,512,2048]{2,1,0:T(8,128)(2,1)} %get-tuple-element.203), kind=kOutput, calls=%fused_computation.7.clone.1 | convolution fusion | flops 805502976 | bytes 4064256 | tf_op jit(solution)/shard_map/while/body/eval_jaxpr/dot_general | solution.py:130
  76.0 3.9 %fusion.107 = bf16[4,512,384]{2,1,0:T(8,128)(2,1)} fusion(bf16[4,512,384]{2,1,0:T(8,128)(2,1)} %get-tuple-element.197, s32[]{:T(128)S(6)} %copy.31, bf16[2048,384]{1,0:T(8,128)(2,1)S(1)} %get-tuple-element.204, bf16[4,512,2048]{2,1,0:T(8,128)(2,1)} %get-tuple-element.203), kind=kOutput, calls=%fused_computation.7.clone.1 | convolution fusion | flops 805502976 | bytes 4064256 | tf_op jit(solution)/shard_map/while/body/eval_jaxpr/dot_general | solution.py:130
  79.9 2.6 fusion.84
  82.5 24.7 %while.22 = (s32[]{:T(128)}, bf16[4,512,1,128]{3,1,2,0:T(8,128)(2,1)S(1)}, s32[4]{0:T(128)S(1)}, s32[2048]{0:T(1024)S(1)}, bf16[2048,1,128]{2,0,1:T(8,128)(2,1)S...) while((s32[]{:T(128)}, ...), condition=%wide.region_6.7_spmd.clone, body=%wide.region_3.6_spmd.clone.sunk | while | flops 548470272 | bytes 13922475 | solution.py:45
  85.8 1.3 fusion.109
  87.1 0.7 fusion.110
  87.8 0.9 fusion.111
  92.0 1.3 fusion.109
  93.2 0.7 fusion.110
  94.0 0.9 fusion.111
  98.2 1.3 fusion.109
  99.4 0.7 fusion.110
  100.1 0.9 fusion.111
  104.4 1.3 fusion.109
  105.6 0.7 fusion.110
  106.3 0.9 fusion.111
  107.3 18.8 %all_to_all.5 = bf16[16,128,128]{2,1,0:T(8,128)(2,1)S(1)} all-to-all(bf16[16,128,128]{2,1,0:T(8,128)(2,1)S(1)} %bitcast.158), channel_id=1, replica_groups=mesh['dp'=8,'tensor'=16] {'tensor'}, dimensions={0} | all-to-all | bytes 1048576 | tf_op jit(solution)/shard_map/all_to_all | solution.py:139
  126.4 4.8 %multiply_reduce_fusion = (f32[128]{0:T(128)S(1)}, f32[128,2048]{1,0:T(8,128)S(1)}) fusion(bf16[128,2048]{0,1:T(8,128)(2,1)S(1)} %bitcast.151, bf16[2048,2048]{1,0:T(8,128)(2,1)} %all-gather.6.cloned.1.call-done, bf16[128,2048]{1,0:T(8,128)(2,1)S(1)} %copy-done.2), kind=kOutput, calls=%fused_computation.70 | convolution fusion | flops 1075314560 | bytes 10486272 | tf_op jit(solution)/shard_map/dot_general | solution.py:143
  131.3 1.0 multiply_convert_fusion.1
  133.0 51.8 %all-gather.8.cloned.1.call-done = bf16[2048,2048]{1,0:T(8,128)(2,1)} async-done(((bf16[128,2048]{1,0:T(8,128)(2,1)}), bf16[2048,2048]{1,0:T(8,128)(2,1)}) %all-gather.8.cloned.1.call-update) | async-done | bytes 8388624 | tf_op jit(solution)/shard_map/all_gather | solution.py:148
  184.8 6.5 %fusion.49 = f32[2048,352]{0,1:T(8,128)S(1)} fusion(bf16[2048,2048]{1,0:T(8,128)(2,1)} %all-gather.8.cloned.1.call-done, bf16[2048,176]{0,1:T(8,128)(2,1)S(1)} %copy-done.14, bf16[2048,176]{0,1:T(8,128)(2,1)} %param.29), kind=kOutput, calls=%fused_computation.55 | convolution fusion | flops 2955673600 | bytes 12713984 | tf_op jit(solution)/shard_map/dot_general | solution.py:172
  191.7 1.2 convolution_convert_fusion
  194.1 6.6 %fusion.32 = f32[1024,1408]{1,0:T(8,128)S(1)} fusion(bf16[1024,2048]{1,0:T(8,128)(2,1)S(1)} %bitcast.145, bf16[1,2048,1408]{2,1,0:T(8,128)(2,1)S(1)} %bitcast.162), kind=kOutput, calls=%fused_computation.33 | convolution fusion | flops 5905580032 | bytes 15728640 | tf_op jit(solution)/shard_map/dot_general | solution.py:181
  200.8 7.1 %multiply_convert_fusion = bf16[1024,1408]{1,0:T(8,128)(2,1)S(1)} fusion(f32[1024,1408]{1,0:T(8,128)S(1)} %fusion.32, bf16[1024,2048]{1,0:T(8,128)(2,1)S(1)} %bitcast.146, bf16[1,2048,1408]{2,1,0:T(8,128)(2,1)S(1)} %bitcast.164), kind=kOutput, calls=%fused_computation.35 | convolution fusion | flops 5914230784 | bytes 18612224 | tf_op jit(solution)/shard_map/dot_general | solution.py:183
  207.9 3.6 %fusion.42 = bf16[1024,1024]{1,0:T(8,128)(2,1)S(1)} fusion(bf16[1024,1408]{1,0:T(8,128)(2,1)S(1)} %multiply_convert_fusion, bf16[1408,2048]{1,0:T(8,128)(2,1)S(1)} %bitcast.168), kind=kOutput, calls=%fused_computation.48 | convolution fusion | flops 2953838592 | bytes 7864320 | tf_op jit(solution)/shard_map/dot_general | solution.py:197
  211.6 1.3 convolution_convert_fusion.2
  212.9 3.2 %fusion.29 = bf16[2048,1024]{1,0:T(8,128)(2,1)} fusion(bf16[2048,1024]{1,0:T(8,128)(2,1)S(1)} %bitcast.148, bf16[2048,176]{0,1:T(8,128)(2,1)S(1)} %fusion.48, f32[2048]{0:T(1024)S(1)} %get-tuple-element.106, bf16[176,2048]{1,0:T(8,128)(2,1)S(1)} %copy-done.15), kind=kOutput, calls=%fused_computation.30 | convolution fusion | flops 746586112 | bytes 9478144 | tf_op jit(solution)/shard_map/dot_general | solution.py:195
  216.1 6.1 %fusion.45 = bf16[1024,1024]{1,0:T(8,128)(2,1)S(1)} fusion(bf16[1024,1408]{1,0:T(8,128)(2,1)} %copy-done.17, bf16[1408,2048]{1,0:T(8,128)(2,1)} %bitcast.165), kind=kOutput, calls=%fused_computation.49 | convolution fusion | flops 2953838592 | bytes 7864320 | tf_op jit(solution)/shard_map/dot_general | solution.py:197
  222.2 1.3 convolution_convert_fusion.1
  223.5 1.7 fusion.27
  225.2 2.0 copy-done.7
  227.7 4.0 %collective-permute-done = bf16[4,2,128,1024]{3,2,1,0:T(8,128)(2,1)} collective-permute-done((bf16[4,2,128,1024]{3,2,1,0:T(8,128)(2,1)S(1)}, bf16[4,2,128,1024]{3,2,1,0:T(8,128)(2,1)}, u32[]{:S(2)}, u32[]{:S(2)}) %collective-permute-start) | collective-permute-done | bytes 2097184 | tf_op jit(solution)/shard_map/ppermute | solution.py:68
  231.8 3.2 %convert_add_fusion = f32[4,2,128,1024]{3,2,1,0:T(8,128)S(1)} fusion(bf16[4,2,128,1024]{3,2,1,0:T(8,128)(2,1)} %collective-permute-done, bf16[4,2,2,128,1024]{4,3,2,1,0:T(8,128)(2,1)} %bitcast.150, s32[]{:T(128)S(6)} %select_n.100), kind=kLoop, calls=%fused_computation.36 | loop fusion | flops 3145728 | bytes 8388612 | tf_op jit(solution)/shard_map/add | solution.py:69
  235.6 1.4 copy-done.1
  237.0 0.7 fusion.72
  237.8 1.5 collective-permute-start.1
  239.3 1.8 collective-permute-start.4
  241.1 9.8 %collective-permute-done.1 = bf16[2,128,512]{2,1,0:T(8,128)(2,1)} collective-permute-done((bf16[2,128,512]{2,1,0:T(8,128)(2,1)}, bf16[2,128,512]{2,1,0:T(8,128)(2,1)}, u32[]{:S(2)}, u32[]{:S(2)}) %collective-permute-start.1) | collective-permute-done | bytes 262176 | tf_op jit(solution)/shard_map/ppermute | solution.py:80
  250.9 1.9 fusion.65
  252.9 1.0 collective-permute-start.2
  253.8 1.7 fusion.63
  255.5 2.3 collective-permute-start.5
  257.8 7.7 %collective-permute-done.2 = bf16[2,128,512]{2,1,0:T(8,128)(2,1)} collective-permute-done((bf16[2,128,512]{2,1,0:T(8,128)(2,1)}, bf16[2,128,512]{2,1,0:T(8,128)(2,1)}, u32[]{:S(2)}, u32[]{:S(2)}) %collective-permute-start.2) | collective-permute-done | bytes 262176 | tf_op jit(solution)/shard_map/ppermute | solution.py:80
  265.5 1.9 fusion.64
  267.4 1.7 fusion.62
  269.2 3.2 %collective-permute-start.6 = (bf16[2,128,512]{2,1,0:T(8,128)(2,1)}, bf16[2,128,512]{2,1,0:T(8,128)(2,1)}, u32[]{:S(2)}, u32[]{:S(2)}) collective-permute-start(bf16[2,128,512]{2,1,0:T(8,128)(2,1)} %fusion.62), channel_id=1, source_target_pairs={{0,12},{1,13},{2,14},{3,15},{4,0},{5,1},{6,2},{7,3},{8,4},{9,5},{1... | collective-permute-start | bytes 786440 | tf_op jit(solution)/shard_map/ppermute | solution.py:81
  272.4 6.3 %collective-permute-done.3 = bf16[2,128,512]{2,1,0:T(8,128)(2,1)S(1)} collective-permute-done((bf16[2,128,512]{2,1,0:T(8,128)(2,1)}, bf16[2,128,512]{2,1,0:T(8,128)(2,1)S(1)}, u32[]{:S(2)}, u32[]{:S(2)}) %collective-permute-start.3) | collective-permute-done | bytes 262176 | tf_op jit(solution)/shard_map/ppermute | solution.py:80
  278.7 1.1 bitcast_add_fusion.3
  279.9 1.2 bitcast_add_fusion
  281.2 0.8 copy-done.5
  282.1 1.2 broadcast_in_dim.45
  283.3 3.0 scatter_fusion
  286.2 2.1 collective-permute-done.7
  288.4 1.0 fusion.61
  289.4 1.0 convert_element_type.160
  290.4 0.9 fusion.56
  (93 shorter events, 9.3 us)
Async XLA Ops:
  7.2 58.1 %all-gather.4.cloned.1.call-start = ((), (), s32[]{:S(2)}) async-start(), calls=%async_computation.2 | async-start | bytes 8912896 | tf_op jit(solution)/shard_map/all_gather | solution.py:127
  10.5 115.9 %all-gather.6.cloned.1.call-start = ((), (), s32[]{:S(2)}) async-start(), calls=%async_computation.3 | async-start | bytes 8912896 | tf_op jit(solution)/shard_map/all_gather | solution.py:128
  11.3 173.5 %all-gather.8.cloned.1.call-start = ((), (), s32[]{:S(2)}) async-start(), calls=%async_computation.4 | async-start | bytes 8912896 | tf_op jit(solution)/shard_map/all_gather | solution.py:148
  79.9 2.6 copy-start.12
  82.5 43.9 %copy-start.2 = (bf16[128,2048]{1,0:T(8,128)(2,1)S(1)}, bf16[128,2048]{1,0:T(8,128)(2,1)}, u32[]{:S(2)}) copy-start(bf16[128,2048]{1,0:T(8,128)(2,1)} %param.21) | copy-start | bytes 1572868
  126.4 4.9 %copy-start.13 = (f32[2048]{0:T(1024)S(1)}, f32[2048]{0:T(1024)}, u32[]{:S(2)}) copy-start(f32[2048]{0:T(1024)} %param.28) | copy-start | bytes 24580
  126.4 6.2 %copy-start.10 = (f32[2048,6]{0,1:T(8,128)S(1)}, f32[2048,6]{0,1:T(8,128)}, u32[]{:S(2)}) copy-start(f32[2048,6]{0,1:T(8,128)} %param.36) | copy-start | bytes 147460
  126.4 6.2 %copy-start.11 = (s32[2048,6]{0,1:T(8,128)S(1)}, s32[2048,6]{0,1:T(8,128)}, u32[]{:S(2)}) copy-start(s32[2048,6]{0,1:T(8,128)} %param.35) | copy-start | bytes 147460
  126.4 58.3 %copy-start.14 = (bf16[2048,176]{0,1:T(8,128)(2,1)S(1)}, bf16[2048,176]{0,1:T(8,128)(2,1)}, u32[]{:S(2)}) copy-start(bf16[2048,176]{0,1:T(8,128)(2,1)} %param.30) | copy-start | bytes 2162692
  132.3 157.1 %reduce-scatter.2.cloned.1.call-start = ((), (), s32[]{:S(2)}) async-start(), calls=%async_computation.5 | async-start | bytes 4456448 | tf_op jit(solution)/shard_map/reduce_scatter | solution.py:211
  184.8 6.9 %copy-start = (bf16[2048,2048]{1,0:T(8,128)(2,1)S(1)}, bf16[2048,2048]{1,0:T(8,128)(2,1)}, u32[]{:S(2)}) copy-start(bf16[2048,2048]{1,0:T(8,128)(2,1)} %all-gather.8.cloned.1.call-done) | copy-start | bytes 25165828
  191.3 2.2 slice-start
  191.7 2.4 slice-start.1
  191.7 9.0 %slice-start.2 = ((s8[5767168]{0:T(1024)(128)(4,1)}), s8[4194304]{0:T(1024)(128)(4,1)S(1)}, s32[]{:S(2)}) async-start(s8[5767168]{0:T(1024)(128)(4,1)} %bitcast.163), calls=%async_computation.8 | async-start | bytes 8388608
  194.1 6.7 %slice-start.3 = ((s8[5767168]{0:T(1024)(128)(4,1)}), s8[1572864]{0:T(1024)(128)(4,1)S(1)}, s32[]{:S(2)}) async-start(s8[5767168]{0:T(1024)(128)(4,1)} %bitcast.163), calls=%async_computation.9 | async-start | bytes 3145728
  194.1 13.8 %slice-start.4 = ((s8[5767168]{0:T(1024)(128)(4,1)}), s8[4194304]{0:T(1024)(128)(4,1)S(1)}, s32[]{:S(2)}) async-start(s8[5767168]{0:T(1024)(128)(4,1)} %bitcast.166), calls=%async_computation.10 | async-start | bytes 8388608
  200.7 7.1 %slice-start.5 = ((s8[5767168]{0:T(1024)(128)(4,1)}), s8[1572864]{0:T(1024)(128)(4,1)S(1)}, s32[]{:S(2)}) async-start(s8[5767168]{0:T(1024)(128)(4,1)} %bitcast.166), calls=%async_computation.11 | async-start | bytes 3145728
  207.9 3.7 %copy-start.17 = (bf16[1024,1408]{1,0:T(8,128)(2,1)}, bf16[1024,1408]{1,0:T(8,128)(2,1)S(1)}, u32[]{:S(2)}) copy-start(bf16[1024,1408]{1,0:T(8,128)(2,1)S(1)} %multiply_convert_fusion) | copy-start | bytes 8650756
  211.6 1.3 copy-start.15
  225.2 2.0 copy-start.7
  227.4 4.4 %collective-permute-start = (bf16[4,2,128,1024]{3,2,1,0:T(8,128)(2,1)S(1)}, bf16[4,2,128,1024]{3,2,1,0:T(8,128)(2,1)}, u32[]{:S(2)}, u32[]{:S(2)}) collective-permute-start(bf16[4,2,128,1024]{3,2,1,0:T(8,128)(2,1)S(1)} %dynamic-slice_bitcast_fusion), channel_id=1, source_target_pairs={{0,1},{1,0},{2,3},{3,2},{4,5},{5,4},{6,7},{7,6},{8,9},{9,8},{10,11... | collective-permute-start | bytes 6291464 | tf_op jit(solution)/shard_map/ppermute | solution.py:68
  235.6 1.4 copy-start.1
  237.8 13.2 %collective-permute-start.1 = (bf16[2,128,512]{2,1,0:T(8,128)(2,1)}, bf16[2,128,512]{2,1,0:T(8,128)(2,1)}, u32[]{:S(2)}, u32[]{:S(2)}) collective-permute-start(bf16[2,128,512]{2,1,0:T(8,128)(2,1)} %fusion.72), channel_id=1, source_target_pairs={{0,4},{1,5},{2,6},{3,7},{4,8},{5,9},{6,10},{7,11},{8,12},{9,13},{1... | collective-permute-start | bytes 786440 | tf_op jit(solution)/shard_map/ppermute | solution.py:80
  239.3 42.6 %copy-start.16 = (s32[16]{0:T(128)S(1)}, s32[16]{0:T(128)}, u32[]{:S(2)}) copy-start(s32[16]{0:T(128)} %param.37) | copy-start | bytes 196
  239.3 14.5 %collective-permute-start.4 = (bf16[2,128,512]{2,1,0:T(8,128)(2,1)S(1)}, bf16[2,128,512]{2,1,0:T(8,128)(2,1)}, u32[]{:S(2)}, u32[]{:S(2)}) collective-permute-start(bf16[2,128,512]{2,1,0:T(8,128)(2,1)S(1)} %fusion.73), channel_id=1, source_target_pairs={{0,12},{1,13},{2,14},{3,15},{4,0},{5,1},{6,2},{7,3},{8,4},{9,5},{1... | collective-permute-start | bytes 786440 | tf_op jit(solution)/shard_map/ppermute | solution.py:81
  252.9 12.7 %collective-permute-start.2 = (bf16[2,128,512]{2,1,0:T(8,128)(2,1)}, bf16[2,128,512]{2,1,0:T(8,128)(2,1)}, u32[]{:S(2)}, u32[]{:S(2)}) collective-permute-start(bf16[2,128,512]{2,1,0:T(8,128)(2,1)} %fusion.65), channel_id=1, source_target_pairs={{0,4},{1,5},{2,6},{3,7},{4,8},{5,9},{6,10},{7,11},{8,12},{9,13},{1... | collective-permute-start | bytes 786440 | tf_op jit(solution)/shard_map/ppermute | solution.py:80
  255.5 11.9 %collective-permute-start.5 = (bf16[2,128,512]{2,1,0:T(8,128)(2,1)}, bf16[2,128,512]{2,1,0:T(8,128)(2,1)}, u32[]{:S(2)}, u32[]{:S(2)}) collective-permute-start(bf16[2,128,512]{2,1,0:T(8,128)(2,1)} %fusion.63), channel_id=1, source_target_pairs={{0,12},{1,13},{2,14},{3,15},{4,0},{5,1},{6,2},{7,3},{8,4},{9,5},{1... | collective-permute-start | bytes 786440 | tf_op jit(solution)/shard_map/ppermute | solution.py:81
  267.4 11.3 %collective-permute-start.3 = (bf16[2,128,512]{2,1,0:T(8,128)(2,1)}, bf16[2,128,512]{2,1,0:T(8,128)(2,1)S(1)}, u32[]{:S(2)}, u32[]{:S(2)}) collective-permute-start(bf16[2,128,512]{2,1,0:T(8,128)(2,1)} %fusion.64), channel_id=1, source_target_pairs={{0,4},{1,5},{2,6},{3,7},{4,8},{5,9},{6,10},{7,11},{8,12},{9,13},{1... | collective-permute-start | bytes 786440 | tf_op jit(solution)/shard_map/ppermute | solution.py:80
  269.2 10.7 %collective-permute-start.6 = (bf16[2,128,512]{2,1,0:T(8,128)(2,1)}, bf16[2,128,512]{2,1,0:T(8,128)(2,1)}, u32[]{:S(2)}, u32[]{:S(2)}) collective-permute-start(bf16[2,128,512]{2,1,0:T(8,128)(2,1)} %fusion.62), channel_id=1, source_target_pairs={{0,12},{1,13},{2,14},{3,15},{4,0},{5,1},{6,2},{7,3},{8,4},{9,5},{1... | collective-permute-start | bytes 786440 | tf_op jit(solution)/shard_map/ppermute | solution.py:81
  272.4 9.5 %copy-start.8 = (bf16[2048,128]{1,0:T(8,128)(2,1)S(1)}, bf16[2048,128]{1,0:T(8,128)(2,1)}, u32[]{:S(2)}) copy-start(bf16[2048,128]{1,0:T(8,128)(2,1)} %get-tuple-element.112) | copy-start | bytes 1572868
  272.4 9.5 %copy-start.9 = (bf16[2048,128]{1,0:T(8,128)(2,1)S(1)}, bf16[2048,128]{1,0:T(8,128)(2,1)}, u32[]{:S(2)}) copy-start(bf16[2048,128]{1,0:T(8,128)(2,1)} %get-tuple-element.115) | copy-start | bytes 1572868
  279.8 1.2 copy-start.3
  281.1 0.8 copy-start.5
  281.9 6.5 %copy-start.4 = (f32[2,128,512]{2,1,0:T(8,128)S(1)}, f32[2,128,512]{2,1,0:T(8,128)}, u32[]{:S(2)}) copy-start(f32[2,128,512]{2,1,0:T(8,128)} %copy-done.3) | copy-start | bytes 1572868
  281.9 6.5 %collective-permute-start.7 = (bf16[128,1024]{1,0:T(8,128)(2,1)S(1)}, bf16[128,1024]{1,0:T(8,128)(2,1)}, u32[]{:S(2)}, u32[]{:S(2)}) collective-permute-start(bf16[128,1024]{1,0:T(8,128)(2,1)S(1)} %fusion.74), channel_id=1, source_target_pairs={{0,2},{1,3},{2,0},{3,1},{4,6},{5,7},{6,4},{7,5},{8,10},{9,11},{10,... | collective-permute-start | bytes 786440 | tf_op jit(solution)/shard_map/ppermute | solution.py:96
  281.9 6.5 %copy-start.6 = (f32[2,128,512]{2,1,0:T(8,128)S(1)}, f32[2,128,512]{2,1,0:T(8,128)}, u32[]{:S(2)}) copy-start(f32[2,128,512]{2,1,0:T(8,128)} %copy-done.5) | copy-start | bytes 1572868
Sparse Core Ops, SparseCore 0:
  10.6 54.5 all-gather.3
  66.9 58.6 all-gather.5
  132.5 52.2 all-gather.7
  216.2 70.7 reduce-scatter.1

commit v4 on v2

--- a/solution.py
+++ b/solution.py
@@ -53,7 +53,7 @@
     return jnp.dot(hidden, down_w, preferred_element_type=jnp.float32).astype(jnp.bfloat16)
 
 
-def ring_reduce_scatter(partial, groups, direction):
+def ring_reduce_scatter(partial, groups):
     ring = groups // 4
     rows = partial.shape[0] // groups
     width = partial.shape[1]
@@ -67,14 +67,25 @@
     give = lax.dynamic_index_in_dim(blocks, 1 - core, axis=2, keepdims=False)
     got = lax.ppermute(give, "tensor", core_pairs)
     summed = keep.astype(jnp.float32) + got.astype(jnp.float32)
-    ring_pairs = [(t, ((t // 4 + direction) % ring) * 4 + t % 4) for t in range(groups)]
-    carry = lax.dynamic_index_in_dim(summed, (y + ring - direction) % ring, 0, False)
-    carry = carry.astype(jnp.bfloat16)
-    for step in range(ring - 1):
-        received = lax.ppermute(carry, "tensor", ring_pairs)
-        index = (y + 2 * ring - direction * (step + 2)) % ring
-        acc = received.astype(jnp.float32) + lax.dynamic_index_in_dim(summed, index, 0, False)
-        carry = acc.astype(jnp.bfloat16)
+    forward_pairs = [(t, ((t // 4 + 1) % ring) * 4 + t % 4) for t in range(groups)]
+    backward_pairs = [(t, ((t // 4 + ring - 1) % ring) * 4 + t % 4) for t in range(groups)]
+    half = width // 2
+    own = lax.dynamic_index_in_dim(summed, y, 0, False)
+    to_next = lax.dynamic_index_in_dim(summed, (y + 1) % ring, 0, False)
+    to_prev = lax.dynamic_index_in_dim(summed, (y + ring - 1) % ring, 0, False)
+    far = lax.dynamic_index_in_dim(summed, (y + 2) % ring, 0, False)
+    send_f = jnp.concatenate([to_next, far[..., :half]], axis=-1).astype(jnp.bfloat16)
+    send_b = jnp.concatenate([to_prev, far[..., half:]], axis=-1).astype(jnp.bfloat16)
+    recv_f = lax.ppermute(send_f, "tensor", forward_pairs)
+    recv_b = lax.ppermute(send_b, "tensor", backward_pairs)
+    relay_f = lax.ppermute(recv_f[..., width:], "tensor", forward_pairs)
+    relay_b = lax.ppermute(recv_b[..., width:], "tensor", backward_pairs)
+    acc = (
+        own
+        + recv_f[..., :width].astype(jnp.float32)
+        + recv_b[..., :width].astype(jnp.float32)
+        + jnp.concatenate([relay_f, relay_b], axis=-1).astype(jnp.float32)
+    )
     side_pairs = [(t, t ^ 2) for t in range(groups)]
     keep_side = lax.dynamic_index_in_dim(acc, side, 0, False)
     give_side = lax.dynamic_index_in_dim(acc, 1 - side, 0, False).astype(jnp.bfloat16)
@@ -191,7 +202,7 @@
             term = term + weights[local].reshape(-1, 1) * back.reshape(-1, piece_width).astype(
                 jnp.float32
             )
-        outs.append(ring_reduce_scatter(term.astype(jnp.bfloat16), groups, 1 - 2 * (k % 2)))
+        outs.append(ring_reduce_scatter(term.astype(jnp.bfloat16), groups))
     ffn_out = jnp.concatenate(outs, axis=1)
     layer_out = (residual.astype(jnp.float32) + ffn_out).astype(jnp.bfloat16)
     return (layer_out, kv_pages)

time: 303 us -> 305 us (level)
  other arithmetic: 29.5 us -> 24.3 us
    convert_element_type x4 -> x0, other arithmetic: 5.59 us -> none  [ring_reduce_scatter(): carry = acc.astype(jnp.bfloat16)]
    dot_general x1, matrix products: 4.77 us -> 1.24 us  [shards(): jnp.einsum('bst,btd->bsd', onehots[local], token_blocks, preferred_elemen...]
    dot_general x1, matrix products: 3.17 us -> 6.53 us  [shards(): jnp.dot(normed_stream, shared_columns, preferred_element_type=jnp.float32)]
    ppermute x6 -> x8, starting transfers between devices: 10.7 us -> 13.4 us  [the longest x2 7.45 us: ring_reduce_scatter(): relay_b = lax.ppermute(recv_b[..., width:], 'tensor', backward_pairs)]
    ppermute x6 -> x8, waiting for transfers between devices: 28.5 us -> 28.4 us  [the longest x2 22.8 us: ring_reduce_scatter(): recv_b = lax.ppermute(send_b, 'tensor', backward_pairs)]
  transfers between devices with their start and end apart: 13 -> 15, of which waited for: 9 -> 10; matrix products, arithmetic and copies ran while one was open for 19% -> 20% of each run, Pallas kernels for 0% -> 0%
where the time goes in v4:
time: 305 us; the launch traced here: 304 us
  waiting for transfers between devices  138 us (45%)
  matrix products  66.8 us (22%)
  other arithmetic  24.3 us (8%)
  blocking collectives  20.6 us (7%)
  local copies, waits for them, and re-layouts  17.8 us (6%)
  starting transfers between devices  15.7 us (5%)
  between operations  14.4 us (5%)
  loops' own time  6.65 us (2%)
    all_gather x1, waiting for transfers between devices, shards(): lax.all_gather(rms_scale(tokens, attention_gain), 'tensor', axis=0, tiled...  52.3 us
    all_gather x1, waiting for transfers between devices, shards(): normed_stream = lax.all_gather(normed_ffn, 'tensor', axis=0, tiled=True)  52 us
    ppermute x2, waiting for transfers between devices, ring_reduce_scatter(): recv_b = lax.ppermute(send_b, 'tensor', backward_pairs)  22.8 us
    all_to_all x1, blocking collectives, shards(): lax.all_to_all(context.reshape(groups, tok_dev, inner), 'tensor', split_a...  20.6 us
    dot_general x4, matrix products, shards(): jnp.dot(rows, projection, preferred_element_type=jnp.float32)  14.6 us
    dot_general x1, matrix products, shards(): jnp.dot(picked, expert_up[local], preferred_element_type=jnp.float32)  8.96 us
    dot_general x1, matrix products, shards(): jnp.dot(picked, expert_gate[local], preferred_element_type=jnp.float32)  8.4 us
    ppermute x2, starting transfers between devices, ring_reduce_scatter(): relay_b = lax.ppermute(recv_b[..., width:], 'tensor', backward_pairs)  7.45 us
  transfers between devices with their start and end apart: 15, of which 10 were waited for; matrix products, arithmetic and copies ran while one was open for 20% of the time, Pallas kernels for 0%

profile of v4, /device:TPU:0, one launch (start us, length us, event | category | flops | bytes accessed | tf_op | source)
XLA Modules:
  0.0 303.8 jit_solution(3298814636839354001)
XLA Ops:
  7.2 1.2 fusion.53
  8.4 2.0 fusion.55
  10.6 0.7 all-gather.6.cloned.1.call-update
  11.3 1.6 pad_maximum_fusion
  12.9 52.3 %all-gather.4.cloned.1.call-done = bf16[2048,2048]{1,0:T(8,128)(2,1)} async-done(((bf16[128,2048]{1,0:T(8,128)(2,1)}), bf16[2048,2048]{1,0:T(8,128)(2,1)}) %all-gather.4.cloned.1.call-update) | async-done | bytes 8388624 | tf_op jit(solution)/shard_map/all_gather | solution.py:123
  65.2 14.6 %while.21 = (s32[]{:T(128)}, bf16[4,512,384]{2,1,0:T(8,128)(2,1)}, bf16[4,512,2048]{2,1,0:T(8,128)(2,1)}, bf16[2048,384]{1,0:T(8,128)(2,1)S(1)}, s32[]{:T(128)}) while((s32[]{:T(128)}, bf16[4,512,384]{2,1,0:T(8,128)(2,1)}, bf16[4,512,2048]{2,1,0:T(8,128)(2,1)}, bf16[2048,384]{1,0:T(8,128)(2,1)S(1)}, s32[]{:T(128)}) %tuple.66), condition=%wide.region_2.3_spmd, body=%wide.region_1.2_spmd.sunk | while | flops 805502976 | bytes 4064325 | solution.py:125
  65.2 3.6 %fusion.108 = bf16[4,512,384]{2,1,0:T(8,128)(2,1)} fusion(bf16[4,512,384]{2,1,0:T(8,128)(2,1)} %get-tuple-element.205, s32[]{:T(128)S(6)} %copy.34, bf16[2048,384]{1,0:T(8,128)(2,1)S(1)} %get-tuple-element.212, bf16[4,512,2048]{2,1,0:T(8,128)(2,1)} %get-tuple-element.211), kind=kOutput, calls=%fused_computation.7.clone.1 | convolution fusion | flops 805502976 | bytes 4064256 | tf_op jit(solution)/shard_map/while/body/eval_jaxpr/dot_general | solution.py:126
  68.8 3.6 %fusion.108 = bf16[4,512,384]{2,1,0:T(8,128)(2,1)} fusion(bf16[4,512,384]{2,1,0:T(8,128)(2,1)} %get-tuple-element.205, s32[]{:T(128)S(6)} %copy.34, bf16[2048,384]{1,0:T(8,128)(2,1)S(1)} %get-tuple-element.212, bf16[4,512,2048]{2,1,0:T(8,128)(2,1)} %get-tuple-element.211), kind=kOutput, calls=%fused_computation.7.clone.1 | convolution fusion | flops 805502976 | bytes 4064256 | tf_op jit(solution)/shard_map/while/body/eval_jaxpr/dot_general | solution.py:126
  72.4 3.6 %fusion.108 = bf16[4,512,384]{2,1,0:T(8,128)(2,1)} fusion(bf16[4,512,384]{2,1,0:T(8,128)(2,1)} %get-tuple-element.205, s32[]{:T(128)S(6)} %copy.34, bf16[2048,384]{1,0:T(8,128)(2,1)S(1)} %get-tuple-element.212, bf16[4,512,2048]{2,1,0:T(8,128)(2,1)} %get-tuple-element.211), kind=kOutput, calls=%fused_computation.7.clone.1 | convolution fusion | flops 805502976 | bytes 4064256 | tf_op jit(solution)/shard_map/while/body/eval_jaxpr/dot_general | solution.py:126
  76.0 3.8 %fusion.108 = bf16[4,512,384]{2,1,0:T(8,128)(2,1)} fusion(bf16[4,512,384]{2,1,0:T(8,128)(2,1)} %get-tuple-element.205, s32[]{:T(128)S(6)} %copy.34, bf16[2048,384]{1,0:T(8,128)(2,1)S(1)} %get-tuple-element.212, bf16[4,512,2048]{2,1,0:T(8,128)(2,1)} %get-tuple-element.211), kind=kOutput, calls=%fused_computation.7.clone.1 | convolution fusion | flops 805502976 | bytes 4064256 | tf_op jit(solution)/shard_map/while/body/eval_jaxpr/dot_general | solution.py:126
  79.8 2.7 fusion.83
  82.5 23.0 %while.22 = (s32[]{:T(128)}, bf16[4,512,1,128]{3,1,2,0:T(8,128)(2,1)S(1)}, s32[4]{0:T(128)S(1)}, s32[2048]{0:T(1024)S(1)}, bf16[2048,1,128]{2,0,1:T(8,128)(2,1)S...) while((s32[]{:T(128)}, ...), condition=%wide.region_6.7_spmd.clone, body=%wide.region_3.6_spmd.clone.sunk | while | flops 548470272 | bytes 13922475 | solution.py:45
  85.3 1.3 fusion.110
  86.6 0.7 fusion.111
  87.3 0.9 fusion.112
  91.1 1.3 fusion.110
  92.3 0.7 fusion.111
  93.0 0.9 fusion.112
  96.8 1.3 fusion.110
  98.1 0.7 fusion.111
  98.8 0.9 fusion.112
  102.6 1.3 fusion.110
  103.8 0.7 fusion.111
  104.5 0.9 fusion.112
  105.5 20.6 %all_to_all.5 = bf16[16,128,128]{2,1,0:T(8,128)(2,1)S(1)} all-to-all(bf16[16,128,128]{2,1,0:T(8,128)(2,1)S(1)} %bitcast.170), channel_id=1, replica_groups=mesh['dp'=8,'tensor'=16] {'tensor'}, dimensions={0} | all-to-all | bytes 1048576 | tf_op jit(solution)/shard_map/all_to_all | solution.py:135
  126.4 4.8 %multiply_reduce_fusion = (f32[128]{0:T(128)S(1)}, f32[128,2048]{1,0:T(8,128)S(1)}) fusion(bf16[128,2048]{0,1:T(8,128)(2,1)S(1)} %bitcast.163, bf16[2048,2048]{1,0:T(8,128)(2,1)} %all-gather.6.cloned.1.call-done, bf16[128,2048]{1,0:T(8,128)(2,1)S(1)} %copy-done.3), kind=kOutput, calls=%fused_computation.80 | convolution fusion | flops 1075314560 | bytes 10486272 | tf_op jit(solution)/shard_map/dot_general | solution.py:139
  131.3 1.0 multiply_convert_fusion.1
  132.7 52.0 %all-gather.8.cloned.1.call-done = bf16[2048,2048]{1,0:T(8,128)(2,1)} async-done(((bf16[128,2048]{1,0:T(8,128)(2,1)}), bf16[2048,2048]{1,0:T(8,128)(2,1)}) %all-gather.8.cloned.1.call-update) | async-done | bytes 8388624 | tf_op jit(solution)/shard_map/all_gather | solution.py:144
  184.7 6.5 %fusion.49 = f32[2048,352]{0,1:T(8,128)S(1)} fusion(bf16[2048,2048]{1,0:T(8,128)(2,1)} %all-gather.8.cloned.1.call-done, bf16[2048,176]{0,1:T(8,128)(2,1)S(1)} %copy-done.18, bf16[2048,176]{0,1:T(8,128)(2,1)} %param.29), kind=kOutput, calls=%fused_computation.57 | convolution fusion | flops 2955673600 | bytes 12713984 | tf_op jit(solution)/shard_map/dot_general | solution.py:168
  191.7 1.2 convolution_convert_fusion
  194.0 8.4 %fusion.32 = f32[1024,1408]{1,0:T(8,128)} fusion(bf16[1024,2048]{1,0:T(8,128)(2,1)S(1)} %bitcast.155, bf16[1,2048,1408]{2,1,0:T(8,128)(2,1)S(1)} %bitcast.174), kind=kOutput, calls=%fused_computation.33 | convolution fusion | flops 5905580032 | bytes 15728640 | tf_op jit(solution)/shard_map/dot_general | solution.py:177
  202.4 9.0 %multiply_convert_fusion = bf16[1024,1408]{1,0:T(8,128)(2,1)S(1)} fusion(f32[1024,1408]{1,0:T(8,128)} %fusion.32, bf16[1024,2048]{1,0:T(8,128)(2,1)S(1)} %bitcast.156, bf16[1,2048,1408]{2,1,0:T(8,128)(2,1)S(1)} %bitcast.176), kind=kOutput, calls=%fused_computation.35 | convolution fusion | flops 5914230784 | bytes 18612224 | tf_op jit(solution)/shard_map/dot_general | solution.py:179
  211.4 3.6 %fusion.45 = bf16[1024,1024]{1,0:T(8,128)(2,1)S(1)} fusion(bf16[1024,1408]{1,0:T(8,128)(2,1)S(1)} %multiply_convert_fusion, bf16[1408,2048]{1,0:T(8,128)(2,1)S(1)} %bitcast.179), kind=kOutput, calls=%fused_computation.51 | convolution fusion | flops 2953838592 | bytes 7864320 | tf_op jit(solution)/shard_map/dot_general | solution.py:193
  215.1 1.3 convolution_convert_fusion.1
  216.4 1.9 fusion.27
  218.4 1.8 dynamic-slice_bitcast_fusion
  220.4 3.6 %fusion.42 = bf16[1024,1024]{1,0:T(8,128)(2,1)S(1)} fusion(bf16[1024,1408]{1,0:T(8,128)(2,1)S(1)} %multiply_convert_fusion, bf16[1408,2048]{1,0:T(8,128)(2,1)S(1)} %bitcast.182), kind=kOutput, calls=%fused_computation.50 | convolution fusion | flops 2953838592 | bytes 7864320 | tf_op jit(solution)/shard_map/dot_general | solution.py:193
  224.1 1.3 convolution_convert_fusion.2
  225.4 1.7 fusion.29
  227.1 2.0 copy-done.5
  229.6 3.1 %convert_add_fusion = f32[4,2,128,1024]{3,2,1,0:T(8,128)S(1)} fusion(bf16[4,2,128,1024]{3,2,1,0:T(8,128)(2,1)} %collective-permute-done.6, bf16[4,2,2,128,1024]{4,3,2,1,0:T(8,128)(2,1)} %bitcast.162, s32[]{:T(128)S(6)} %select_n.96), kind=kLoop, calls=%fused_computation.36 | loop fusion | flops 3145728 | bytes 8388612 | tf_op jit(solution)/shard_map/add | solution.py:69
  233.2 2.8 collective-permute-start.8
  236.5 2.5 convert_add_fusion.1
  239.4 2.9 collective-permute-start.2
  242.4 11.4 %collective-permute-done.8 = bf16[2,128,1536]{2,1,0:T(8,128)(2,1)S(1)} collective-permute-done((bf16[2,128,1536]{2,1,0:T(8,128)(2,1)S(1)}, bf16[2,128,1536]{2,1,0:T(8,128)(2,1)S(1)}, u32[]{:S(2)}, u32[]{:S(2)}) %collective-permute-start.8) | collective-permute-done | bytes 786464 | tf_op jit(solution)/shard_map/ppermute | solution.py:80
  253.8 0.8 slice.106
  254.6 3.7 %collective-permute-start.10 = (bf16[2,128,512]{2,1,0:T(8,128)(2,1)}, bf16[2,128,512]{2,1,0:T(8,128)(2,1)}, u32[]{:S(2)}, u32[]{:S(2)}) collective-permute-start(bf16[2,128,512]{2,1,0:T(8,128)(2,1)} %slice.106), channel_id=1, source_target_pairs={{0,12},{1,13},{2,14},{3,15},{4,0},{5,1},{6,2},{7,3},{8,4},{9,5},{1... | collective-permute-start | bytes 786440 | tf_op jit(solution)/shard_map/ppermute | solution.py:82
  258.3 0.8 slice.105
  259.3 11.4 %collective-permute-done.2 = bf16[2,128,1536]{2,1,0:T(8,128)(2,1)S(1)} collective-permute-done((bf16[2,128,1536]{2,1,0:T(8,128)(2,1)S(1)}, bf16[2,128,1536]{2,1,0:T(8,128)(2,1)S(1)}, u32[]{:S(2)}, u32[]{:S(2)}) %collective-permute-start.2) | collective-permute-done | bytes 786464 | tf_op jit(solution)/shard_map/ppermute | solution.py:80
  270.7 3.8 %collective-permute-start.4 = (bf16[2,128,512]{2,1,0:T(8,128)(2,1)S(1)}, bf16[2,128,512]{2,1,0:T(8,128)(2,1)S(1)}, u32[]{:S(2)}, u32[]{:S(2)}) collective-permute-start(bf16[2,128,512]{2,1,0:T(8,128)(2,1)S(1)} %slice.99), channel_id=1, source_target_pairs={{0,12},{1,13},{2,14},{3,15},{4,0},{5,1},{6,2},{7,3},{8,4},{9,5},{1... | collective-permute-start | bytes 786440 | tf_op jit(solution)/shard_map/ppermute | solution.py:82
  274.6 1.0 slice.98
  276.4 3.9 %collective-permute-done.9 = bf16[2,128,512]{2,1,0:T(8,128)(2,1)} collective-permute-done((bf16[2,128,512]{2,1,0:T(8,128)(2,1)}, bf16[2,128,512]{2,1,0:T(8,128)(2,1)}, u32[]{:S(2)}, u32[]{:S(2)}) %collective-permute-start.9) | collective-permute-done | bytes 262176 | tf_op jit(solution)/shard_map/ppermute | solution.py:81
  280.3 1.9 fusion.58
  282.2 0.8 fusion.74
  283.0 0.9 collective-permute-start.11
  283.9 0.9 collective-permute-done.3
  284.8 1.6 fusion.60
  286.4 0.8 fusion.73
  287.3 0.8 collective-permute-start.5
  288.5 1.6 scatter_fusion
  290.5 1.2 bitcast_add_fusion.2
  291.7 3.6 %collective-permute-done.5 = bf16[128,1024]{1,0:T(8,128)(2,1)S(1)} collective-permute-done((bf16[128,1024]{1,0:T(8,128)(2,1)}, bf16[128,1024]{1,0:T(8,128)(2,1)S(1)}, u32[]{:S(2)}, u32[]{:S(2)}) %collective-permute-start.5) | collective-permute-done | bytes 262176 | tf_op jit(solution)/shard_map/ppermute | solution.py:92
  295.2 1.1 bitcast_add_fusion.3
  296.3 0.9 fusion.56
  (117 shorter events, 11.2 us)
Async XLA Ops:
  7.2 58.1 %all-gather.4.cloned.1.call-start = ((), (), s32[]{:S(2)}) async-start(), calls=%async_computation.1 | async-start | bytes 8912896 | tf_op jit(solution)/shard_map/all_gather | solution.py:123
  10.5 115.9 %all-gather.6.cloned.1.call-start = ((), (), s32[]{:S(2)}) async-start(), calls=%async_computation.2 | async-start | bytes 8912896 | tf_op jit(solution)/shard_map/all_gather | solution.py:124
  11.3 173.4 %all-gather.8.cloned.1.call-start = ((), (), s32[]{:S(2)}) async-start(), calls=%async_computation.3 | async-start | bytes 8912896 | tf_op jit(solution)/shard_map/all_gather | solution.py:144
  79.8 2.7 copy-start.16
  82.5 43.9 %copy-start.3 = (bf16[128,2048]{1,0:T(8,128)(2,1)S(1)}, bf16[128,2048]{1,0:T(8,128)(2,1)}, u32[]{:S(2)}) copy-start(bf16[128,2048]{1,0:T(8,128)(2,1)} %param.21) | copy-start | bytes 1572868
  126.4 4.9 %copy-start.17 = (f32[2048]{0:T(1024)S(1)}, f32[2048]{0:T(1024)}, u32[]{:S(2)}) copy-start(f32[2048]{0:T(1024)} %param.28) | copy-start | bytes 24580
  126.4 5.9 %copy-start.14 = (f32[2048,6]{0,1:T(8,128)S(1)}, f32[2048,6]{0,1:T(8,128)}, u32[]{:S(2)}) copy-start(f32[2048,6]{0,1:T(8,128)} %param.36) | copy-start | bytes 147460
  126.4 5.9 %copy-start.15 = (s32[2048,6]{0,1:T(8,128)S(1)}, s32[2048,6]{0,1:T(8,128)}, u32[]{:S(2)}) copy-start(s32[2048,6]{0,1:T(8,128)} %param.35) | copy-start | bytes 147460
  126.4 58.3 %copy-start.18 = (bf16[2048,176]{0,1:T(8,128)(2,1)S(1)}, bf16[2048,176]{0,1:T(8,128)(2,1)}, u32[]{:S(2)}) copy-start(bf16[2048,176]{0,1:T(8,128)(2,1)} %param.30) | copy-start | bytes 2162692
  184.7 7.0 %copy-start = (bf16[2048,2048]{1,0:T(8,128)(2,1)S(1)}, bf16[2048,2048]{1,0:T(8,128)(2,1)}, u32[]{:S(2)}) copy-start(bf16[2048,2048]{1,0:T(8,128)(2,1)} %all-gather.8.cloned.1.call-done) | copy-start | bytes 25165828
  191.2 2.2 slice-start
  191.7 2.4 slice-start.1
  191.7 10.7 %slice-start.2 = ((s8[5767168]{0:T(1024)(128)(4,1)}), s8[4194304]{0:T(1024)(128)(4,1)S(1)}, s32[]{:S(2)}) async-start(s8[5767168]{0:T(1024)(128)(4,1)} %bitcast.175), calls=%async_computation.6 | async-start | bytes 8388608
  194.0 8.4 %slice-start.3 = ((s8[5767168]{0:T(1024)(128)(4,1)}), s8[1572864]{0:T(1024)(128)(4,1)S(1)}, s32[]{:S(2)}) async-start(s8[5767168]{0:T(1024)(128)(4,1)} %bitcast.175), calls=%async_computation.7 | async-start | bytes 3145728
  194.0 17.4 %slice-start.4 = ((s8[5767168]{0:T(1024)(128)(4,1)}), s8[4194304]{0:T(1024)(128)(4,1)S(1)}, s32[]{:S(2)}) async-start(s8[5767168]{0:T(1024)(128)(4,1)} %bitcast.177), calls=%async_computation.8 | async-start | bytes 8388608
  202.4 9.0 %slice-start.5 = ((s8[5767168]{0:T(1024)(128)(4,1)}), s8[1572864]{0:T(1024)(128)(4,1)S(1)}, s32[]{:S(2)}) async-start(s8[5767168]{0:T(1024)(128)(4,1)} %bitcast.177), calls=%async_computation.9 | async-start | bytes 3145728
  215.1 1.3 copy-start.19
  215.1 5.3 %slice-start.6 = ((s8[5767168]{0:T(1024)(128)(4,1)}), s8[4194304]{0:T(1024)(128)(4,1)S(1)}, s32[]{:S(2)}) async-start(s8[5767168]{0:T(1024)(128)(4,1)} %bitcast.180), calls=%async_computation.10 | async-start | bytes 8388608
  216.4 4.0 %slice-start.7 = ((s8[5767168]{0:T(1024)(128)(4,1)}), s8[1572864]{0:T(1024)(128)(4,1)S(1)}, s32[]{:S(2)}) async-start(s8[5767168]{0:T(1024)(128)(4,1)} %bitcast.180), calls=%async_computation.11 | async-start | bytes 3145728
  218.4 5.7 %copy-start.7 = (bf16[2048,1024]{1,0:T(8,128)(2,1)}, bf16[2048,1024]{1,0:T(8,128)(2,1)S(1)}, u32[]{:S(2)}) copy-start(bf16[2048,1024]{1,0:T(8,128)(2,1)S(1)} %fusion.27) | copy-start | bytes 12582916
  220.2 9.5 %collective-permute-start.6 = (bf16[4,2,128,1024]{3,2,1,0:T(8,128)(2,1)}, bf16[4,2,128,1024]{3,2,1,0:T(8,128)(2,1)}, u32[]{:S(2)}, u32[]{:S(2)}) collective-permute-start(bf16[4,2,128,1024]{3,2,1,0:T(8,128)(2,1)} %dynamic-slice_bitcast_fusion), channel_id=1, source_target_pairs={{0,1},{1,0},{2,3},{3,2},{4,5},{5,4},{6,7},{7,6},{8,9},{9,8},{10,11... | collective-permute-start | bytes 6291464 | tf_op jit(solution)/shard_map/ppermute | solution.py:68
  227.1 2.0 copy-start.5
  229.3 6.8 %collective-permute-start = (bf16[4,2,128,1024]{3,2,1,0:T(8,128)(2,1)S(1)}, bf16[4,2,128,1024]{3,2,1,0:T(8,128)(2,1)}, u32[]{:S(2)}, u32[]{:S(2)}) collective-permute-start(bf16[4,2,128,1024]{3,2,1,0:T(8,128)(2,1)S(1)} %dynamic-slice_bitcast_fusion.1), channel_id=1, source_target_pairs={{0,1},{1,0},{2,3},{3,2},{4,5},{5,4},{6,7},{7,6},{8,9},{9,8},{10,11... | collective-permute-start | bytes 6291464 | tf_op jit(solution)/shard_map/ppermute | solution.py:68
  232.8 6.2 %copy-start.1 = (f32[4,2,128,1024]{3,2,1,0:T(8,128)}, f32[4,2,128,1024]{3,2,1,0:T(8,128)S(1)}, u32[]{:S(2)}) copy-start(f32[4,2,128,1024]{3,2,1,0:T(8,128)S(1)} %convert_add_fusion) | copy-start | bytes 12582916
  232.8 3.7 %copy-start.6 = (bf16[2048,1024]{1,0:T(8,128)(2,1)S(1)}, bf16[2048,1024]{1,0:T(8,128)(2,1)}, u32[]{:S(2)}) copy-start(bf16[2048,1024]{1,0:T(8,128)(2,1)} %copy-done.5) | copy-start | bytes 12582916
  233.2 20.7 %collective-permute-start.8 = (bf16[2,128,1536]{2,1,0:T(8,128)(2,1)S(1)}, bf16[2,128,1536]{2,1,0:T(8,128)(2,1)S(1)}, u32[]{:S(2)}, u32[]{:S(2)}) collective-permute-start(bf16[2,128,1536]{2,1,0:T(8,128)(2,1)S(1)} %pad_maximum_fusion.4), channel_id=1, source_target_pairs={{0,12},{1,13},{2,14},{3,15},{4,0},{5,1},{6,2},{7,3},{8,4},{9,5},{1... | collective-permute-start | bytes 2359304 | tf_op jit(solution)/shard_map/ppermute | solution.py:80
  236.0 22.3 %collective-permute-start.7 = (bf16[2,128,1536]{2,1,0:T(8,128)(2,1)S(1)}, bf16[2,128,1536]{2,1,0:T(8,128)(2,1)S(1)}, u32[]{:S(2)}, u32[]{:S(2)}) collective-permute-start(bf16[2,128,1536]{2,1,0:T(8,128)(2,1)S(1)} %pad_maximum_fusion.3), channel_id=1, source_target_pairs={{0,4},{1,5},{2,6},{3,7},{4,8},{5,9},{6,10},{7,11},{8,12},{9,13},{1... | collective-permute-start | bytes 2359304 | tf_op jit(solution)/shard_map/ppermute | solution.py:79
  239.0 20.1 %copy-start.2 = (f32[4,2,128,1024]{3,2,1,0:T(8,128)}, f32[4,2,128,1024]{3,2,1,0:T(8,128)S(1)}, u32[]{:S(2)}) copy-start(f32[4,2,128,1024]{3,2,1,0:T(8,128)S(1)} %convert_add_fusion.1) | copy-start | bytes 12582916
  239.0 20.3 %copy-start.20 = (s32[16]{0:T(128)S(1)}, s32[16]{0:T(128)}, u32[]{:S(2)}) copy-start(s32[16]{0:T(128)} %param.37) | copy-start | bytes 196
  239.4 31.3 %collective-permute-start.2 = (bf16[2,128,1536]{2,1,0:T(8,128)(2,1)S(1)}, bf16[2,128,1536]{2,1,0:T(8,128)(2,1)S(1)}, u32[]{:S(2)}, u32[]{:S(2)}) collective-permute-start(bf16[2,128,1536]{2,1,0:T(8,128)(2,1)S(1)} %pad_maximum_fusion.2), channel_id=1, source_target_pairs={{0,12},{1,13},{2,14},{3,15},{4,0},{5,1},{6,2},{7,3},{8,4},{9,5},{1... | collective-permute-start | bytes 2359304 | tf_op jit(solution)/shard_map/ppermute | solution.py:80
  242.3 32.3 %collective-permute-start.1 = (bf16[2,128,1536]{2,1,0:T(8,128)(2,1)S(1)}, bf16[2,128,1536]{2,1,0:T(8,128)(2,1)}, u32[]{:S(2)}, u32[]{:S(2)}) collective-permute-start(bf16[2,128,1536]{2,1,0:T(8,128)(2,1)S(1)} %pad_maximum_fusion.1), channel_id=1, source_target_pairs={{0,4},{1,5},{2,6},{3,7},{4,8},{5,9},{6,10},{7,11},{8,12},{9,13},{1... | collective-permute-start | bytes 2359304 | tf_op jit(solution)/shard_map/ppermute | solution.py:79
  253.8 4.5 %copy-start.12 = (bf16[2,128,1536]{2,1,0:T(8,128)(2,1)}, bf16[2,128,1536]{2,1,0:T(8,128)(2,1)S(1)}, u32[]{:S(2)}) copy-start(bf16[2,128,1536]{2,1,0:T(8,128)(2,1)S(1)} %collective-permute-done.8) | copy-start | bytes 2359300
  254.6 21.8 %collective-permute-start.10 = (bf16[2,128,512]{2,1,0:T(8,128)(2,1)}, bf16[2,128,512]{2,1,0:T(8,128)(2,1)}, u32[]{:S(2)}, u32[]{:S(2)}) collective-permute-start(bf16[2,128,512]{2,1,0:T(8,128)(2,1)} %slice.106), channel_id=1, source_target_pairs={{0,12},{1,13},{2,14},{3,15},{4,0},{5,1},{6,2},{7,3},{8,4},{9,5},{1... | collective-permute-start | bytes 786440 | tf_op jit(solution)/shard_map/ppermute | solution.py:82
  258.3 1.0 copy-start.13
  259.3 21.0 %collective-permute-start.9 = (bf16[2,128,512]{2,1,0:T(8,128)(2,1)}, bf16[2,128,512]{2,1,0:T(8,128)(2,1)}, u32[]{:S(2)}, u32[]{:S(2)}) collective-permute-start(bf16[2,128,512]{2,1,0:T(8,128)(2,1)} %slice.105), channel_id=1, source_target_pairs={{0,4},{1,5},{2,6},{3,7},{4,8},{5,9},{6,10},{7,11},{8,12},{9,13},{1... | collective-permute-start | bytes 786440 | tf_op jit(solution)/shard_map/ppermute | solution.py:81
  270.7 13.2 %collective-permute-start.4 = (bf16[2,128,512]{2,1,0:T(8,128)(2,1)S(1)}, bf16[2,128,512]{2,1,0:T(8,128)(2,1)S(1)}, u32[]{:S(2)}, u32[]{:S(2)}) collective-permute-start(bf16[2,128,512]{2,1,0:T(8,128)(2,1)S(1)} %slice.99), channel_id=1, source_target_pairs={{0,12},{1,13},{2,14},{3,15},{4,0},{5,1},{6,2},{7,3},{8,4},{9,5},{1... | collective-permute-start | bytes 786440 | tf_op jit(solution)/shard_map/ppermute | solution.py:82
  275.6 12.5 %copy-start.10 = (bf16[2048,128]{1,0:T(8,128)(2,1)S(1)}, bf16[2048,128]{1,0:T(8,128)(2,1)}, u32[]{:S(2)}) copy-start(bf16[2048,128]{1,0:T(8,128)(2,1)} %get-tuple-element.116) | copy-start | bytes 1572868
  275.6 12.5 %copy-start.11 = (bf16[2048,128]{1,0:T(8,128)(2,1)S(1)}, bf16[2048,128]{1,0:T(8,128)(2,1)}, u32[]{:S(2)}) copy-start(bf16[2048,128]{1,0:T(8,128)(2,1)} %get-tuple-element.119) | copy-start | bytes 1572868
  275.6 9.2 %collective-permute-start.3 = (bf16[2,128,512]{2,1,0:T(8,128)(2,1)S(1)}, bf16[2,128,512]{2,1,0:T(8,128)(2,1)S(1)}, u32[]{:S(2)}, u32[]{:S(2)}) collective-permute-start(bf16[2,128,512]{2,1,0:T(8,128)(2,1)S(1)} %slice.98), channel_id=1, source_target_pairs={{0,4},{1,5},{2,6},{3,7},{4,8},{5,9},{6,10},{7,11},{8,12},{9,13},{1... | collective-permute-start | bytes 786440 | tf_op jit(solution)/shard_map/ppermute | solution.py:81
  282.2 6.0 %copy-start.8 = (f32[2,128,1024]{2,1,0:T(8,128)}, f32[2,128,1024]{2,1,0:T(8,128)S(1)}, u32[]{:S(2)}) copy-start(f32[2,128,1024]{2,1,0:T(8,128)S(1)} %fusion.58) | copy-start | bytes 3145732
  283.0 7.4 %collective-permute-start.11 = (bf16[128,1024]{1,0:T(8,128)(2,1)}, bf16[128,1024]{1,0:T(8,128)(2,1)}, u32[]{:S(2)}, u32[]{:S(2)}) collective-permute-start(bf16[128,1024]{1,0:T(8,128)(2,1)} %fusion.74), channel_id=1, source_target_pairs={{0,2},{1,3},{2,0},{3,1},{4,6},{5,7},{6,4},{7,5},{8,10},{9,11},{10,... | collective-permute-start | bytes 786440 | tf_op jit(solution)/shard_map/ppermute | solution.py:92
  286.4 1.8 copy-start.9
  287.3 8.0 %collective-permute-start.5 = (bf16[128,1024]{1,0:T(8,128)(2,1)}, bf16[128,1024]{1,0:T(8,128)(2,1)S(1)}, u32[]{:S(2)}, u32[]{:S(2)}) collective-permute-start(bf16[128,1024]{1,0:T(8,128)(2,1)} %fusion.73), channel_id=1, source_target_pairs={{0,2},{1,3},{2,0},{3,1},{4,6},{5,7},{6,4},{7,5},{8,10},{9,11},{10,... | collective-permute-start | bytes 786440 | tf_op jit(solution)/shard_map/ppermute | solution.py:92
  290.1 7.2 %copy-start.4 = (bf16[2,16,128,128]{3,2,1,0:T(8,128)(2,1)}, bf16[2,16,128,128]{3,2,1,0:T(8,128)(2,1)S(1)}, u32[]{:S(2)}) copy-start(bf16[2,16,128,128]{3,2,1,0:T(8,128)(2,1)S(1)} %scatter_fusion) | copy-start | bytes 3145732
Sparse Core Ops, SparseCore 0:
  10.6 54.5 all-gather.3
  66.9 58.6 all-gather.5
  132.4 52.2 all-gather.7

commit v5 on v0

--- a/solution.py
+++ b/solution.py
@@ -53,7 +53,7 @@
     return jnp.dot(hidden, down_w, preferred_element_type=jnp.float32).astype(jnp.bfloat16)
 
 
-def ring_reduce_scatter(partial, groups):
+def ring_reduce_scatter(partial, groups, x_first):
     ring = groups // 4
     rows = partial.shape[0] // groups
     width = partial.shape[1]
@@ -63,10 +63,16 @@
     core = me % 2
     blocks = partial.reshape(ring, 2, 2, rows, width)
     core_pairs = [(t, t ^ 1) for t in range(groups)]
+    side_pairs = [(t, t ^ 2) for t in range(groups)]
     keep = lax.dynamic_index_in_dim(blocks, core, axis=2, keepdims=False)
     give = lax.dynamic_index_in_dim(blocks, 1 - core, axis=2, keepdims=False)
     got = lax.ppermute(give, "tensor", core_pairs)
     summed = keep.astype(jnp.float32) + got.astype(jnp.float32)
+    if x_first:
+        keep_side = lax.dynamic_index_in_dim(summed, side, 1, False)
+        give_side = lax.dynamic_index_in_dim(summed, 1 - side, 1, False).astype(jnp.bfloat16)
+        got_side = lax.ppermute(give_side, "tensor", side_pairs)
+        summed = keep_side + got_side.astype(jnp.float32)
     half = width // 2
     forward_part = summed[..., :half]
     backward_part = summed[..., half:]
@@ -90,7 +96,8 @@
         carry_f = acc_f.astype(jnp.bfloat16)
         carry_b = acc_b.astype(jnp.bfloat16)
     mine = jnp.concatenate([acc_f, acc_b], axis=-1)
-    side_pairs = [(t, t ^ 2) for t in range(groups)]
+    if x_first:
+        return mine
     keep_side = lax.dynamic_index_in_dim(mine, side, 0, False)
     give_side = lax.dynamic_index_in_dim(mine, 1 - side, 0, False).astype(jnp.bfloat16)
     got_side = lax.ppermute(give_side, "tensor", side_pairs)
@@ -206,7 +213,7 @@
             term = term + weights[local].reshape(-1, 1) * back.reshape(-1, piece_width).astype(
                 jnp.float32
             )
-        outs.append(ring_reduce_scatter(term.astype(jnp.bfloat16), groups))
+        outs.append(ring_reduce_scatter(term.astype(jnp.bfloat16), groups, k % 2 == 1))
     ffn_out = jnp.concatenate(outs, axis=1)
     layer_out = (residual.astype(jnp.float32) + ffn_out).astype(jnp.bfloat16)
     return (layer_out, kv_pages)

time: 288 us -> 305 us (1.059)
  waiting for transfers between devices: 118 us -> 136 us
    ppermute x2, waiting for transfers between devices: 0.01 us -> 9.28 us  [ring_reduce_scatter(): got_side = lax.ppermute(give_side, 'tensor', side_pairs)]
    ppermute x6, waiting for transfers between devices: 0.02 us -> 8.6 us  [ring_reduce_scatter(): recv_b = lax.ppermute(carry_b, 'tensor', backward_pairs)]
  transfers between devices with their start and end apart: 19 -> 19, of which waited for: 7 -> 10; matrix products, arithmetic and copies ran while one was open for 19% -> 19% of each run, Pallas kernels for 0% -> 0%
where the time goes in v5:
time: 305 us; the launch traced here: 304 us
  waiting for transfers between devices  136 us (45%)
  matrix products  66.1 us (22%)
  other arithmetic  25.4 us (8%)
  starting transfers between devices  22.2 us (7%)
  blocking collectives  17.9 us (6%)
  local copies, waits for them, and re-layouts  14.4 us (5%)
  between operations  14.4 us (5%)
  loops' own time  8.37 us (3%)
    all_gather x1, waiting for transfers between devices, shards(): lax.all_gather(rms_scale(tokens, attention_gain), 'tensor', axis=0, tiled...  52.3 us
    all_gather x1, waiting for transfers between devices, shards(): normed_stream = lax.all_gather(normed_ffn, 'tensor', axis=0, tiled=True)  51.9 us
    all_to_all x1, blocking collectives, shards(): lax.all_to_all(context.reshape(groups, tok_dev, inner), 'tensor', split_a...  17.9 us
    ppermute x6, starting transfers between devices, ring_reduce_scatter(): recv_b = lax.ppermute(carry_b, 'tensor', backward_pairs)  14.7 us
    dot_general x4, matrix products, shards(): jnp.dot(rows, projection, preferred_element_type=jnp.float32)  14.6 us
    ppermute x6, waiting for transfers between devices, ring_reduce_scatter(): recv_f = lax.ppermute(carry_f, 'tensor', forward_pairs)  12.7 us
    dot_general x1, matrix products, shards(): jnp.dot(picked, expert_gate[local], preferred_element_type=jnp.float32)  9.37 us
    ppermute x2, waiting for transfers between devices, ring_reduce_scatter(): got_side = lax.ppermute(give_side, 'tensor', side_pairs)  9.28 us
  transfers between devices with their start and end apart: 19, of which 10 were waited for; matrix products, arithmetic and copies ran while one was open for 19% of the time, Pallas kernels for 0%

profile of v5, /device:TPU:0, one launch (start us, length us, event | category | flops | bytes accessed | tf_op | source)
XLA Modules:
  0.0 304.4 jit_solution(4040330338063359977)
XLA Ops:
  7.2 1.2 fusion.53
  8.4 2.0 fusion.55
  11.3 1.6 pad_maximum_fusion
  12.9 52.3 %all-gather.4.cloned.1.call-done = bf16[2048,2048]{1,0:T(8,128)(2,1)} async-done(((bf16[128,2048]{1,0:T(8,128)(2,1)}), bf16[2048,2048]{1,0:T(8,128)(2,1)}) %all-gather.4.cloned.1.call-update) | async-done | bytes 8388624 | tf_op jit(solution)/shard_map/all_gather | solution.py:134
  65.2 14.6 %while.21 = (s32[]{:T(128)}, bf16[4,512,384]{2,1,0:T(8,128)(2,1)}, bf16[4,512,2048]{2,1,0:T(8,128)(2,1)}, bf16[2048,384]{1,0:T(8,128)(2,1)S(1)}, s32[]{:T(128)}) while((s32[]{:T(128)}, bf16[4,512,384]{2,1,0:T(8,128)(2,1)}, bf16[4,512,2048]{2,1,0:T(8,128)(2,1)}, bf16[2048,384]{1,0:T(8,128)(2,1)S(1)}, s32[]{:T(128)}) %tuple.63), condition=%wide.region_2.3_spmd, body=%wide.region_1.2_spmd.sunk | while | flops 805502976 | bytes 4064325 | solution.py:136
  65.2 3.6 %fusion.115 = bf16[4,512,384]{2,1,0:T(8,128)(2,1)} fusion(bf16[4,512,384]{2,1,0:T(8,128)(2,1)} %get-tuple-element.201, s32[]{:T(128)S(6)} %copy.41, bf16[2048,384]{1,0:T(8,128)(2,1)S(1)} %get-tuple-element.208, bf16[4,512,2048]{2,1,0:T(8,128)(2,1)} %get-tuple-element.207), kind=kOutput, calls=%fused_computation.7.clone.1 | convolution fusion | flops 805502976 | bytes 4064256 | tf_op jit(solution)/shard_map/while/body/eval_jaxpr/dot_general | solution.py:137
  68.8 3.6 %fusion.115 = bf16[4,512,384]{2,1,0:T(8,128)(2,1)} fusion(bf16[4,512,384]{2,1,0:T(8,128)(2,1)} %get-tuple-element.201, s32[]{:T(128)S(6)} %copy.41, bf16[2048,384]{1,0:T(8,128)(2,1)S(1)} %get-tuple-element.208, bf16[4,512,2048]{2,1,0:T(8,128)(2,1)} %get-tuple-element.207), kind=kOutput, calls=%fused_computation.7.clone.1 | convolution fusion | flops 805502976 | bytes 4064256 | tf_op jit(solution)/shard_map/while/body/eval_jaxpr/dot_general | solution.py:137
  72.4 3.6 %fusion.115 = bf16[4,512,384]{2,1,0:T(8,128)(2,1)} fusion(bf16[4,512,384]{2,1,0:T(8,128)(2,1)} %get-tuple-element.201, s32[]{:T(128)S(6)} %copy.41, bf16[2048,384]{1,0:T(8,128)(2,1)S(1)} %get-tuple-element.208, bf16[4,512,2048]{2,1,0:T(8,128)(2,1)} %get-tuple-element.207), kind=kOutput, calls=%fused_computation.7.clone.1 | convolution fusion | flops 805502976 | bytes 4064256 | tf_op jit(solution)/shard_map/while/body/eval_jaxpr/dot_general | solution.py:137
  76.0 3.9 %fusion.115 = bf16[4,512,384]{2,1,0:T(8,128)(2,1)} fusion(bf16[4,512,384]{2,1,0:T(8,128)(2,1)} %get-tuple-element.201, s32[]{:T(128)S(6)} %copy.41, bf16[2048,384]{1,0:T(8,128)(2,1)S(1)} %get-tuple-element.208, bf16[4,512,2048]{2,1,0:T(8,128)(2,1)} %get-tuple-element.207), kind=kOutput, calls=%fused_computation.7.clone.1 | convolution fusion | flops 805502976 | bytes 4064256 | tf_op jit(solution)/shard_map/while/body/eval_jaxpr/dot_general | solution.py:137
  79.9 2.6 fusion.92
  82.5 25.7 %while.22 = (s32[]{:T(128)}, bf16[4,512,1,128]{3,1,2,0:T(8,128)(2,1)S(1)}, s32[4]{0:T(128)S(1)}, s32[2048]{0:T(1024)S(1)}, bf16[2048,1,128]{2,0,1:T(8,128)(2,1)S...) while((s32[]{:T(128)}, ...), condition=%wide.region_6.7_spmd.clone, body=%wide.region_3.6_spmd.clone.sunk | while | flops 548470272 | bytes 13922475 | solution.py:45
  86.0 1.3 fusion.117
  87.3 0.7 fusion.118
  88.0 0.9 fusion.119
  92.5 1.3 fusion.117
  93.7 0.7 fusion.118
  94.4 0.9 fusion.119
  98.9 1.3 fusion.117
  100.8 0.9 fusion.119
  105.3 1.3 fusion.117
  107.3 0.9 fusion.119
  108.2 17.9 %all_to_all.5 = bf16[16,128,128]{2,1,0:T(8,128)(2,1)S(1)} all-to-all(bf16[16,128,128]{2,1,0:T(8,128)(2,1)S(1)} %bitcast.198), channel_id=1, replica_groups=mesh['dp'=8,'tensor'=16] {'tensor'}, dimensions={0} | all-to-all | bytes 1048576 | tf_op jit(solution)/shard_map/all_to_all | solution.py:146
  126.5 4.8 %multiply_reduce_fusion = (f32[128]{0:T(128)S(1)}, f32[128,2048]{1,0:T(8,128)S(1)}) fusion(bf16[128,2048]{0,1:T(8,128)(2,1)S(1)} %bitcast.191, bf16[2048,2048]{1,0:T(8,128)(2,1)} %all-gather.6.cloned.1.call-done, bf16[128,2048]{1,0:T(8,128)(2,1)S(1)} %copy-done.3), kind=kOutput, calls=%fused_computation.76 | convolution fusion | flops 1075314560 | bytes 10486272 | tf_op jit(solution)/shard_map/dot_general | solution.py:150
  131.3 1.0 multiply_convert_fusion.1
  132.7 51.9 %all-gather.8.cloned.1.call-done = bf16[2048,2048]{1,0:T(8,128)(2,1)} async-done(((bf16[128,2048]{1,0:T(8,128)(2,1)}), bf16[2048,2048]{1,0:T(8,128)(2,1)}) %all-gather.8.cloned.1.call-update) | async-done | bytes 8388624 | tf_op jit(solution)/shard_map/all_gather | solution.py:155
  184.6 4.8 %convolution_convert_fusion = bf16[16,64,2048]{2,1,0:T(8,128)(2,1)S(1)} fusion(bf16[16,128,2048]{2,1,0:T(8,128)(2,1)} %bitcast.181, s32[16,128]{1,0:T(8,128)S(1)} %bitcast_subtract_fusion, pred[16,128]{1,0:T(8,128)(4,1)S(1)} %broadcast_compare_fusion.1), kind=kOutput, calls=%fused_computation.38 | convolution fusion | flops 539230208 | bytes 12593152 | tf_op jit(solution)/shard_map/bst,btd->bsd/dot_general | solution.py:184
  189.4 9.4 %fusion.32 = f32[1024,1408]{1,0:T(8,128)S(1)} fusion(bf16[1024,2048]{1,0:T(8,128)(2,1)S(1)} %bitcast.184, bf16[1,2048,1408]{2,1,0:T(8,128)(2,1)} %param.32), kind=kOutput, calls=%fused_computation.33 | convolution fusion | flops 5905580032 | bytes 15728640 | tf_op jit(solution)/shard_map/dot_general | solution.py:188
  198.9 7.1 %multiply_convert_fusion = bf16[1024,1408]{1,0:T(8,128)(2,1)S(1)} fusion(f32[1024,1408]{1,0:T(8,128)S(1)} %fusion.32, bf16[1024,2048]{1,0:T(8,128)(2,1)S(1)} %bitcast.185, bf16[1,2048,1408]{2,1,0:T(8,128)(2,1)S(1)} %bitcast.202), kind=kOutput, calls=%fused_computation.35 | convolution fusion | flops 5914230784 | bytes 18612224 | tf_op jit(solution)/shard_map/dot_general | solution.py:190
  206.0 3.6 %fusion.45 = bf16[1024,1024]{1,0:T(8,128)(2,1)S(1)} fusion(bf16[1024,1408]{1,0:T(8,128)(2,1)S(1)} %multiply_convert_fusion, bf16[1408,2048]{1,0:T(8,128)(2,1)S(1)} %bitcast.205), kind=kOutput, calls=%fused_computation.54 | convolution fusion | flops 2953838592 | bytes 7864320 | tf_op jit(solution)/shard_map/dot_general | solution.py:204
  209.7 3.9 %fusion.42 = bf16[1024,1024]{1,0:T(8,128)(2,1)S(1)} fusion(bf16[1024,1408]{1,0:T(8,128)(2,1)S(1)} %multiply_convert_fusion, bf16[1408,2048]{1,0:T(8,128)(2,1)S(1)} %bitcast.206), kind=kOutput, calls=%fused_computation.53 | convolution fusion | flops 2953838592 | bytes 7864320 | tf_op jit(solution)/shard_map/dot_general | solution.py:204
  213.6 3.2 %fusion.49 = f32[2048,352]{0,1:T(8,128)S(1)} fusion(bf16[2048,2048]{1,0:T(8,128)(2,1)S(1)} %bitcast.183, bf16[2048,176]{0,1:T(8,128)(2,1)S(1)} %copy-done.12, bf16[2048,176]{0,1:T(8,128)(2,1)S(1)} %copy-done.13), kind=kOutput, calls=%fused_computation.60 | convolution fusion | flops 2955673600 | bytes 12713984 | tf_op jit(solution)/shard_map/dot_general | solution.py:179
  217.3 1.3 convolution_convert_fusion.2
  218.6 1.7 fusion.29
  220.3 1.8 dynamic-slice_bitcast_fusion
  223.0 1.3 convolution_convert_fusion.1
  224.3 1.7 fusion.27
  226.5 1.5 copy.36
  228.3 3.2 %convert_add_fusion.1 = f32[4,2,128,1024]{3,2,1,0:T(8,128)S(1)} fusion(bf16[4,2,128,1024]{3,2,1,0:T(8,128)(2,1)} %collective-permute-done, bf16[4,2,2,128,1024]{4,3,2,1,0:T(8,128)(2,1)} %bitcast.190, s32[]{:T(128)S(6)} %select_n.136), kind=kLoop, calls=%fused_computation.37 | loop fusion | flops 3145728 | bytes 8388612 | tf_op jit(solution)/shard_map/add | solution.py:70
  232.1 1.6 collective-permute-start.1
  233.7 1.8 collective-permute-start.4
  235.6 2.5 convert_add_fusion
  238.1 3.8 %collective-permute-done.1 = bf16[2,128,512]{2,1,0:T(8,128)(2,1)S(1)} collective-permute-done((bf16[2,128,512]{2,1,0:T(8,128)(2,1)S(1)}, bf16[2,128,512]{2,1,0:T(8,128)(2,1)S(1)}, u32[]{:S(2)}, u32[]{:S(2)}) %collective-permute-start.1) | collective-permute-done | bytes 262176 | tf_op jit(solution)/shard_map/ppermute | solution.py:86
  242.6 3.0 collective-permute-start.5
  245.7 1.2 fusion.56
  246.8 1.4 collective-permute-start.9
  248.2 2.9 collective-permute-done.2
  251.2 0.8 fusion.65
  252.0 0.8 fusion.63
  252.8 3.2 %collective-permute-start.6 = (bf16[2,128,512]{2,1,0:T(8,128)(2,1)}, bf16[2,128,512]{2,1,0:T(8,128)(2,1)}, u32[]{:S(2)}, u32[]{:S(2)}) collective-permute-start(bf16[2,128,512]{2,1,0:T(8,128)(2,1)} %fusion.63), channel_id=1, source_target_pairs={{0,12},{1,13},{2,14},{3,15},{4,0},{5,1},{6,2},{7,3},{8,4},{9,5},{1... | collective-permute-start | bytes 786440 | tf_op jit(solution)/shard_map/ppermute | solution.py:87
  256.4 1.6 scatter_fusion
  258.0 2.2 collective-permute-done.3
  260.1 1.1 bitcast_add_fusion.4
  261.3 1.2 bitcast_add_fusion.1
  262.5 1.5 collective-permute-start.7
  264.0 9.3 %collective-permute-done.9 = bf16[4,128,1024]{2,1,0:T(8,128)(2,1)} collective-permute-done((bf16[4,128,1024]{2,1,0:T(8,128)(2,1)}, bf16[4,128,1024]{2,1,0:T(8,128)(2,1)}, u32[]{:S(2)}, u32[]{:S(2)}) %collective-permute-start.9) | collective-permute-done | bytes 1048608 | tf_op jit(solution)/shard_map/ppermute | solution.py:74
  273.3 2.2 bitcast_add_fusion
  276.2 1.8 collective-permute-start.10
  278.0 3.3 %collective-permute-done.13 = bf16[128,512]{1,0:T(8,128)(2,1)S(1)} collective-permute-done((bf16[128,512]{1,0:T(8,128)(2,1)S(1)}, bf16[128,512]{1,0:T(8,128)(2,1)S(1)}, u32[]{:S(2)}, u32[]{:S(2)}) %collective-permute-start.13) | collective-permute-done | bytes 131104 | tf_op jit(solution)/shard_map/ppermute | solution.py:87
  281.3 2.5 collective-permute-start.14
  283.9 2.9 collective-permute-done.14
  286.9 3.8 %collective-permute-start.15 = (bf16[128,512]{1,0:T(8,128)(2,1)S(1)}, bf16[128,512]{1,0:T(8,128)(2,1)S(1)}, u32[]{:S(2)}, u32[]{:S(2)}) collective-permute-start(bf16[128,512]{1,0:T(8,128)(2,1)S(1)} %fusion.76), channel_id=1, source_target_pairs={{0,12},{1,13},{2,14},{3,15},{4,0},{5,1},{6,2},{7,3},{8,4},{9,5},{1... | collective-permute-start | bytes 393224 | tf_op jit(solution)/shard_map/ppermute | solution.py:87
  290.8 2.4 collective-permute-done.15
  293.2 3.7 %collective-permute-done.12 = bf16[128,512]{1,0:T(8,128)(2,1)S(1)} collective-permute-done((bf16[128,512]{1,0:T(8,128)(2,1)S(1)}, bf16[128,512]{1,0:T(8,128)(2,1)S(1)}, u32[]{:S(2)}, u32[]{:S(2)}) %collective-permute-start.12) | collective-permute-done | bytes 131104 | tf_op jit(solution)/shard_map/ppermute | solution.py:86
  297.0 0.9 fusion.57
  (115 shorter events, 13.7 us)
Async XLA Ops:
  7.2 58.1 %all-gather.4.cloned.1.call-start = ((), (), s32[]{:S(2)}) async-start(), calls=%async_computation.1 | async-start | bytes 8912896 | tf_op jit(solution)/shard_map/all_gather | solution.py:134
  10.5 116.0 %all-gather.6.cloned.1.call-start = ((), (), s32[]{:S(2)}) async-start(), calls=%async_computation.2 | async-start | bytes 8912896 | tf_op jit(solution)/shard_map/all_gather | solution.py:135
  11.3 173.4 %all-gather.8.cloned.1.call-start = ((), (), s32[]{:S(2)}) async-start(), calls=%async_computation.3 | async-start | bytes 8912896 | tf_op jit(solution)/shard_map/all_gather | solution.py:155
  79.9 2.6 copy-start.10
  82.5 44.0 %copy-start.3 = (bf16[128,2048]{1,0:T(8,128)(2,1)S(1)}, bf16[128,2048]{1,0:T(8,128)(2,1)}, u32[]{:S(2)}) copy-start(bf16[128,2048]{1,0:T(8,128)(2,1)} %param.21) | copy-start | bytes 1572868
  126.5 4.8 %copy-start.11 = (f32[2048]{0:T(1024)S(1)}, f32[2048]{0:T(1024)}, u32[]{:S(2)}) copy-start(f32[2048]{0:T(1024)} %param.28) | copy-start | bytes 24580
  126.5 5.9 %copy-start.8 = (f32[2048,6]{0,1:T(8,128)S(1)}, f32[2048,6]{0,1:T(8,128)}, u32[]{:S(2)}) copy-start(f32[2048,6]{0,1:T(8,128)} %param.36) | copy-start | bytes 147460
  126.5 5.9 %copy-start.9 = (s32[2048,6]{0,1:T(8,128)S(1)}, s32[2048,6]{0,1:T(8,128)}, u32[]{:S(2)}) copy-start(s32[2048,6]{0,1:T(8,128)} %param.35) | copy-start | bytes 147460
  184.6 14.2 %slice-start.2 = ((s8[5767168]{0:T(1024)(128)(4,1)}), s8[4194304]{0:T(1024)(128)(4,1)S(1)}, s32[]{:S(2)}) async-start(s8[5767168]{0:T(1024)(128)(4,1)} %bitcast.201), calls=%async_computation.6 | async-start | bytes 8388608
  189.4 9.4 %slice-start.3 = ((s8[5767168]{0:T(1024)(128)(4,1)}), s8[1572864]{0:T(1024)(128)(4,1)S(1)}, s32[]{:S(2)}) async-start(s8[5767168]{0:T(1024)(128)(4,1)} %bitcast.201), calls=%async_computation.7 | async-start | bytes 3145728
  189.4 16.5 %slice-start.4 = ((s8[5767168]{0:T(1024)(128)(4,1)}), s8[4194304]{0:T(1024)(128)(4,1)S(1)}, s32[]{:S(2)}) async-start(s8[5767168]{0:T(1024)(128)(4,1)} %bitcast.203), calls=%async_computation.8 | async-start | bytes 8388608
  198.8 7.1 %slice-start.5 = ((s8[5767168]{0:T(1024)(128)(4,1)}), s8[1572864]{0:T(1024)(128)(4,1)S(1)}, s32[]{:S(2)}) async-start(s8[5767168]{0:T(1024)(128)(4,1)} %bitcast.203), calls=%async_computation.9 | async-start | bytes 3145728
  206.0 7.5 %slice-start = ((s8[8388608]{0:T(1024)(128)(4,1)}), s8[4194304]{0:T(1024)(128)(4,1)S(1)}, s32[]{:S(2)}) async-start(s8[8388608]{0:T(1024)(128)(4,1)} %bitcast.182), calls=%async_computation.4 | async-start | bytes 8388608
  209.6 3.9 %slice-start.1 = ((s8[8388608]{0:T(1024)(128)(4,1)}), s8[4194304]{0:T(1024)(128)(4,1)S(1)}, s32[]{:S(2)}) async-start(s8[8388608]{0:T(1024)(128)(4,1)} %bitcast.182), calls=%async_computation.5 | async-start | bytes 8388608
  209.7 3.9 %copy-start.12 = (bf16[2048,176]{0,1:T(8,128)(2,1)S(1)}, bf16[2048,176]{0,1:T(8,128)(2,1)}, u32[]{:S(2)}) copy-start(bf16[2048,176]{0,1:T(8,128)(2,1)} %param.30) | copy-start | bytes 2162692
  209.7 3.9 %copy-start.13 = (bf16[2048,176]{0,1:T(8,128)(2,1)S(1)}, bf16[2048,176]{0,1:T(8,128)(2,1)}, u32[]{:S(2)}) copy-start(bf16[2048,176]{0,1:T(8,128)(2,1)} %param.29) | copy-start | bytes 2162692
  216.8 1.7 copy-start.14
  220.3 2.7 copy-start.5
  222.1 6.2 %collective-permute-start = (bf16[4,2,128,1024]{3,2,1,0:T(8,128)(2,1)}, bf16[4,2,128,1024]{3,2,1,0:T(8,128)(2,1)}, u32[]{:S(2)}, u32[]{:S(2)}) collective-permute-start(bf16[4,2,128,1024]{3,2,1,0:T(8,128)(2,1)} %dynamic-slice_bitcast_fusion), channel_id=1, source_target_pairs={{0,1},{1,0},{2,3},{3,2},{4,5},{5,4},{6,7},{7,6},{8,9},{9,8},{10,11... | collective-permute-start | bytes 6291464 | tf_op jit(solution)/shard_map/ppermute | solution.py:69
  226.5 1.8 copy-start.15
  228.0 7.5 %collective-permute-start.8 = (bf16[4,2,128,1024]{3,2,0,1:T(8,128)(2,1)}, bf16[4,2,128,1024]{3,2,0,1:T(8,128)(2,1)}, u32[]{:S(2)}, u32[]{:S(2)}) collective-permute-start(bf16[4,2,128,1024]{3,2,0,1:T(8,128)(2,1)} %bitcast.163), channel_id=1, source_target_pairs={{0,1},{1,0},{2,3},{3,2},{4,5},{5,4},{6,7},{7,6},{8,9},{9,8},{10,11... | collective-permute-start | bytes 6291464 | tf_op jit(solution)/shard_map/ppermute | solution.py:69
  232.1 19.1 %copy-start.2 = (f32[4,2,128,512]{3,2,1,0:T(8,128)}, f32[4,2,128,512]{3,2,1,0:T(8,128)S(1)}, u32[]{:S(2)}) copy-start(f32[4,2,128,512]{3,2,1,0:T(8,128)S(1)} %get-tuple-element.111) | copy-start | bytes 6291460
  232.1 19.9 %copy-start.1 = (f32[4,2,128,512]{3,2,1,0:T(8,128)}, f32[4,2,128,512]{3,2,1,0:T(8,128)S(1)}, u32[]{:S(2)}) copy-start(f32[4,2,128,512]{3,2,1,0:T(8,128)S(1)} %get-tuple-element.110) | copy-start | bytes 6291460
  232.1 9.8 %collective-permute-start.1 = (bf16[2,128,512]{2,1,0:T(8,128)(2,1)S(1)}, bf16[2,128,512]{2,1,0:T(8,128)(2,1)S(1)}, u32[]{:S(2)}, u32[]{:S(2)}) collective-permute-start(bf16[2,128,512]{2,1,0:T(8,128)(2,1)S(1)} %fusion.73), channel_id=1, source_target_pairs={{0,4},{1,5},{2,6},{3,7},{4,8},{5,9},{6,10},{7,11},{8,12},{9,13},{1... | collective-permute-start | bytes 786440 | tf_op jit(solution)/shard_map/ppermute | solution.py:86
  233.7 8.8 %collective-permute-start.4 = (bf16[2,128,512]{2,1,0:T(8,128)(2,1)S(1)}, bf16[2,128,512]{2,1,0:T(8,128)(2,1)S(1)}, u32[]{:S(2)}, u32[]{:S(2)}) collective-permute-start(bf16[2,128,512]{2,1,0:T(8,128)(2,1)S(1)} %fusion.74), channel_id=1, source_target_pairs={{0,12},{1,13},{2,14},{3,15},{4,0},{5,1},{6,2},{7,3},{8,4},{9,5},{1... | collective-permute-start | bytes 786440 | tf_op jit(solution)/shard_map/ppermute | solution.py:87
  238.1 18.1 %copy-start = (f32[4,2,128,1024]{3,2,0,1:T(8,128)}, f32[4,2,128,1024]{3,2,0,1:T(8,128)S(1)}, u32[]{:S(2)}) copy-start(f32[4,2,128,1024]{3,2,0,1:T(8,128)S(1)} %convert_add_fusion) | copy-start | bytes 12582916
  238.1 17.9 %copy-start.6 = (bf16[2048,128]{1,0:T(8,128)(2,1)S(1)}, bf16[2048,128]{1,0:T(8,128)(2,1)}, u32[]{:S(2)}) copy-start(bf16[2048,128]{1,0:T(8,128)(2,1)} %get-tuple-element.116) | copy-start | bytes 1572868
  238.1 17.9 %copy-start.7 = (bf16[2048,128]{1,0:T(8,128)(2,1)S(1)}, bf16[2048,128]{1,0:T(8,128)(2,1)}, u32[]{:S(2)}) copy-start(bf16[2048,128]{1,0:T(8,128)(2,1)} %get-tuple-element.119) | copy-start | bytes 1572868
  242.0 9.2 %collective-permute-start.2 = (bf16[2,128,512]{2,1,0:T(8,128)(2,1)S(1)}, bf16[2,128,512]{2,1,0:T(8,128)(2,1)S(1)}, u32[]{:S(2)}, u32[]{:S(2)}) collective-permute-start(bf16[2,128,512]{2,1,0:T(8,128)(2,1)S(1)} %fusion.66), channel_id=1, source_target_pairs={{0,4},{1,5},{2,6},{3,7},{4,8},{5,9},{6,10},{7,11},{8,12},{9,13},{1... | collective-permute-start | bytes 786440 | tf_op jit(solution)/shard_map/ppermute | solution.py:86
  242.6 9.3 %collective-permute-start.5 = (bf16[2,128,512]{2,1,0:T(8,128)(2,1)S(1)}, bf16[2,128,512]{2,1,0:T(8,128)(2,1)S(1)}, u32[]{:S(2)}, u32[]{:S(2)}) collective-permute-start(bf16[2,128,512]{2,1,0:T(8,128)(2,1)S(1)} %fusion.64), channel_id=1, source_target_pairs={{0,12},{1,13},{2,14},{3,15},{4,0},{5,1},{6,2},{7,3},{8,4},{9,5},{1... | collective-permute-start | bytes 786440 | tf_op jit(solution)/shard_map/ppermute | solution.py:87
  246.8 26.4 %collective-permute-start.9 = (bf16[4,128,1024]{2,1,0:T(8,128)(2,1)}, bf16[4,128,1024]{2,1,0:T(8,128)(2,1)}, u32[]{:S(2)}, u32[]{:S(2)}) collective-permute-start(bf16[4,128,1024]{2,1,0:T(8,128)(2,1)} %fusion.56), channel_id=1, source_target_pairs={{0,2},{1,3},{2,0},{3,1},{4,6},{5,7},{6,4},{7,5},{8,10},{9,11},{10,... | collective-permute-start | bytes 3145736 | tf_op jit(solution)/shard_map/ppermute | solution.py:74
  252.0 8.2 %collective-permute-start.3 = (bf16[2,128,512]{2,1,0:T(8,128)(2,1)}, bf16[2,128,512]{2,1,0:T(8,128)(2,1)S(1)}, u32[]{:S(2)}, u32[]{:S(2)}) collective-permute-start(bf16[2,128,512]{2,1,0:T(8,128)(2,1)} %fusion.65), channel_id=1, source_target_pairs={{0,4},{1,5},{2,6},{3,7},{4,8},{5,9},{6,10},{7,11},{8,12},{9,13},{1... | collective-permute-start | bytes 786440 | tf_op jit(solution)/shard_map/ppermute | solution.py:86
  252.8 8.5 %collective-permute-start.6 = (bf16[2,128,512]{2,1,0:T(8,128)(2,1)}, bf16[2,128,512]{2,1,0:T(8,128)(2,1)}, u32[]{:S(2)}, u32[]{:S(2)}) collective-permute-start(bf16[2,128,512]{2,1,0:T(8,128)(2,1)} %fusion.63), channel_id=1, source_target_pairs={{0,12},{1,13},{2,14},{3,15},{4,0},{5,1},{6,2},{7,3},{8,4},{9,5},{1... | collective-permute-start | bytes 786440 | tf_op jit(solution)/shard_map/ppermute | solution.py:87
  257.9 17.5 %copy-start.4 = (bf16[2,16,128,128]{3,2,1,0:T(8,128)(2,1)}, bf16[2,16,128,128]{3,2,1,0:T(8,128)(2,1)S(1)}, u32[]{:S(2)}) copy-start(bf16[2,16,128,128]{3,2,1,0:T(8,128)(2,1)S(1)} %scatter_fusion) | copy-start | bytes 3145732
  262.5 15.5 %collective-permute-start.7 = (bf16[128,1024]{1,0:T(8,128)(2,1)S(1)}, bf16[128,1024]{1,0:T(8,128)(2,1)S(1)}, u32[]{:S(2)}, u32[]{:S(2)}) collective-permute-start(bf16[128,1024]{1,0:T(8,128)(2,1)S(1)} %fusion.75), channel_id=1, source_target_pairs={{0,2},{1,3},{2,0},{3,1},{4,6},{5,7},{6,4},{7,5},{8,10},{9,11},{10,... | collective-permute-start | bytes 786440 | tf_op jit(solution)/shard_map/ppermute | solution.py:103
  275.8 5.5 %collective-permute-start.13 = (bf16[128,512]{1,0:T(8,128)(2,1)S(1)}, bf16[128,512]{1,0:T(8,128)(2,1)S(1)}, u32[]{:S(2)}, u32[]{:S(2)}) collective-permute-start(bf16[128,512]{1,0:T(8,128)(2,1)S(1)} %fusion.87), channel_id=1, source_target_pairs={{0,12},{1,13},{2,14},{3,15},{4,0},{5,1},{6,2},{7,3},{8,4},{9,5},{1... | collective-permute-start | bytes 393224 | tf_op jit(solution)/shard_map/ppermute | solution.py:87
  276.2 7.6 %collective-permute-start.10 = (bf16[128,512]{1,0:T(8,128)(2,1)S(1)}, bf16[128,512]{1,0:T(8,128)(2,1)S(1)}, u32[]{:S(2)}, u32[]{:S(2)}) collective-permute-start(bf16[128,512]{1,0:T(8,128)(2,1)S(1)} %fusion.86), channel_id=1, source_target_pairs={{0,4},{1,5},{2,6},{3,7},{4,8},{5,9},{6,10},{7,11},{8,12},{9,13},{1... | collective-permute-start | bytes 393224 | tf_op jit(solution)/shard_map/ppermute | solution.py:86
  281.3 5.5 %collective-permute-start.14 = (bf16[128,512]{1,0:T(8,128)(2,1)S(1)}, bf16[128,512]{1,0:T(8,128)(2,1)S(1)}, u32[]{:S(2)}, u32[]{:S(2)}) collective-permute-start(bf16[128,512]{1,0:T(8,128)(2,1)S(1)} %fusion.77), channel_id=1, source_target_pairs={{0,12},{1,13},{2,14},{3,15},{4,0},{5,1},{6,2},{7,3},{8,4},{9,5},{1... | collective-permute-start | bytes 393224 | tf_op jit(solution)/shard_map/ppermute | solution.py:87
  283.8 6.8 %collective-permute-start.11 = (bf16[128,512]{1,0:T(8,128)(2,1)S(1)}, bf16[128,512]{1,0:T(8,128)(2,1)S(1)}, u32[]{:S(2)}, u32[]{:S(2)}) collective-permute-start(bf16[128,512]{1,0:T(8,128)(2,1)S(1)} %fusion.79), channel_id=1, source_target_pairs={{0,4},{1,5},{2,6},{3,7},{4,8},{5,9},{6,10},{7,11},{8,12},{9,13},{1... | collective-permute-start | bytes 393224 | tf_op jit(solution)/shard_map/ppermute | solution.py:86
  286.9 6.3 %collective-permute-start.15 = (bf16[128,512]{1,0:T(8,128)(2,1)S(1)}, bf16[128,512]{1,0:T(8,128)(2,1)S(1)}, u32[]{:S(2)}, u32[]{:S(2)}) collective-permute-start(bf16[128,512]{1,0:T(8,128)(2,1)S(1)} %fusion.76), channel_id=1, source_target_pairs={{0,12},{1,13},{2,14},{3,15},{4,0},{5,1},{6,2},{7,3},{8,4},{9,5},{1... | collective-permute-start | bytes 393224 | tf_op jit(solution)/shard_map/ppermute | solution.py:87
  290.7 6.2 %collective-permute-start.12 = (bf16[128,512]{1,0:T(8,128)(2,1)S(1)}, bf16[128,512]{1,0:T(8,128)(2,1)S(1)}, u32[]{:S(2)}, u32[]{:S(2)}) collective-permute-start(bf16[128,512]{1,0:T(8,128)(2,1)S(1)} %fusion.78), channel_id=1, source_target_pairs={{0,4},{1,5},{2,6},{3,7},{4,8},{5,9},{6,10},{7,11},{8,12},{9,13},{1... | collective-permute-start | bytes 393224 | tf_op jit(solution)/shard_map/ppermute | solution.py:86
Sparse Core Ops, SparseCore 0:
  10.6 54.5 all-gather.3
  66.9 58.4 all-gather.5
  132.4 52.1 all-gather.7

commit v6 on v0

--- a/solution.py
+++ b/solution.py
@@ -171,23 +171,27 @@
     shared_width = shared_gate.shape[1]
     joined = jnp.dot(normed_stream, shared_columns, preferred_element_type=jnp.float32)
     token_blocks = normed_stream.reshape(groups, tok_dev, model_width)
-    expert_gate_parts = []
-    expert_up_parts = []
+    hidden_all = (jax.nn.silu(joined[:, :shared_width]) * joined[:, shared_width:]).astype(
+        jnp.bfloat16
+    )
+    expert_hidden = []
     for local in range(local_experts):
         picked = jnp.einsum(
             "bst,btd->bsd", onehots[local], token_blocks, preferred_element_type=jnp.float32
-        ).astype(jnp.bfloat16).reshape(-1, model_width)
-        expert_gate_parts.append(
-            jnp.dot(picked, expert_gate[local], preferred_element_type=jnp.float32)
-        )
-        expert_up_parts.append(jnp.dot(picked, expert_up[local], preferred_element_type=jnp.float32))
-    hidden_all = (jax.nn.silu(joined[:, :shared_width]) * joined[:, shared_width:]).astype(
-        jnp.bfloat16
-    )
-    expert_hidden = [
-        (jax.nn.silu(expert_gate_parts[local]) * expert_up_parts[local]).astype(jnp.bfloat16)
-        for local in range(local_experts)
-    ]
+        ).astype(jnp.bfloat16)
+        gate_w = expert_gate[local]
+        up_w = expert_up[local]
+
+        def hidden_rows(rows):
+            gate_part = jnp.dot(rows, gate_w, preferred_element_type=jnp.float32)
+            upward = jnp.dot(rows, up_w, preferred_element_type=jnp.float32)
+            return (jax.nn.silu(gate_part) * upward).astype(jnp.bfloat16)
+
+        expert_hidden.append(
+            lax.map(hidden_rows, picked.reshape(4, -1, model_width)).reshape(
+                groups * capacity, -1
+            )
+        )
 
     outs = []
     for k in range(pieces):

time: 288 us -> 317 us (1.10)
  matrix products: 66 us -> 92.2 us
    dot_general x2 -> x8, matrix products: 16.4 us -> 35.6 us  [the longest x4 19.6 us: hidden_rows(): gate_part = jnp.dot(rows, gate_w, preferred_element_type=jnp.float32)]
    ppermute x6, waiting for transfers between devices: 0.02 us -> 7.94 us  [ring_reduce_scatter(): recv_b = lax.ppermute(carry_b, 'tensor', backward_pairs)]
    ppermute x6, waiting for transfers between devices: 12.5 us -> 6.61 us  [ring_reduce_scatter(): recv_f = lax.ppermute(carry_f, 'tensor', forward_pairs)]
    dot_general x2, matrix products: 7.49 us -> 12.5 us  [shards(): jnp.dot(expert_hidden[local], expert_down[local][:, columns], preferred_e...]
  transfers between devices with their start and end apart: 19 -> 19, of which waited for: 7 -> 8; matrix products, arithmetic and copies ran while one was open for 19% -> 17% of each run, Pallas kernels for 0% -> 0%
where the time goes in v6:
time: 317 us; the launch traced here: 316 us
  waiting for transfers between devices  120 us (38%)
  matrix products  92.2 us (29%)
  starting transfers between devices  23.7 us (7%)
  other arithmetic  23.1 us (7%)
  blocking collectives  18.9 us (6%)
  local copies, waits for them, and re-layouts  16.5 us (5%)
  between operations  14.3 us (5%)
  loops' own time  7.7 us (2%)
    all_gather x1, waiting for transfers between devices, shards(): lax.all_gather(rms_scale(tokens, attention_gain), 'tensor', axis=0, tiled...  52.6 us
    all_gather x1, waiting for transfers between devices, shards(): normed_stream = lax.all_gather(normed_ffn, 'tensor', axis=0, tiled=True)  52 us
    ppermute x6, starting transfers between devices, ring_reduce_scatter(): recv_b = lax.ppermute(carry_b, 'tensor', backward_pairs)  20.6 us
    dot_general x4, matrix products, hidden_rows(): gate_part = jnp.dot(rows, gate_w, preferred_element_type=jnp.float32)  19.6 us
    all_to_all x1, blocking collectives, shards(): lax.all_to_all(context.reshape(groups, tok_dev, inner), 'tensor', split_a...  18.9 us
    dot_general x4, matrix products, hidden_rows(): upward = jnp.dot(rows, up_w, preferred_element_type=jnp.float32)  16.1 us
    dot_general x4, matrix products, shards(): jnp.dot(rows, projection, preferred_element_type=jnp.float32)  14.7 us
    dot_general x2, matrix products, shards(): jnp.dot(expert_hidden[local], expert_down[local][:, columns], preferred_e...  12.5 us
  transfers between devices with their start and end apart: 19, of which 8 were waited for; matrix products, arithmetic and copies ran while one was open for 17% of the time, Pallas kernels for 0%

profile of v6, /device:TPU:0, one launch (start us, length us, event | category | flops | bytes accessed | tf_op | source)
XLA Modules:
  0.0 316.4 jit_solution(9224875074730707214)
XLA Ops:
  7.2 1.3 fusion.57
  8.5 2.0 fusion.59
  11.4 1.3 pad_maximum_fusion
  12.7 52.6 %all-gather.4.cloned.1.call-done = bf16[2048,2048]{1,0:T(8,128)(2,1)} async-done(((bf16[128,2048]{1,0:T(8,128)(2,1)}), bf16[2048,2048]{1,0:T(8,128)(2,1)}) %all-gather.4.cloned.1.call-update) | async-done | bytes 8388624 | tf_op jit(solution)/shard_map/all_gather | solution.py:127
  65.3 14.7 %while.31 = (s32[]{:T(128)}, bf16[4,512,384]{2,1,0:T(8,128)(2,1)}, bf16[4,512,2048]{2,1,0:T(8,128)(2,1)}, bf16[2048,384]{1,0:T(8,128)(2,1)S(1)}, s32[]{:T(128)}) while((s32[]{:T(128)}, bf16[4,512,384]{2,1,0:T(8,128)(2,1)}, bf16[4,512,2048]{2,1,0:T(8,128)(2,1)}, bf16[2048,384]{1,0:T(8,128)(2,1)S(1)}, s32[]{:T(128)}) %tuple.79), condition=%wide.region_2.3_spmd, body=%wide.region_1.2_spmd.sunk | while | flops 805502976 | bytes 4064317 | solution.py:129
  65.3 3.6 %fusion.130 = bf16[4,512,384]{2,1,0:T(8,128)(2,1)} fusion(bf16[4,512,384]{2,1,0:T(8,128)(2,1)} %get-tuple-element.268, s32[]{:T(128)} %get-tuple-element.267, bf16[2048,384]{1,0:T(8,128)(2,1)S(1)} %get-tuple-element.275, bf16[4,512,2048]{2,1,0:T(8,128)(2,1)} %get-tuple-element.274), kind=kOutput, calls=%fused_computation.7.clone.1 | convolution fusion | flops 805502976 | bytes 4064256 | tf_op jit(solution)/shard_map/while/body/eval_jaxpr/dot_general | solution.py:130
  68.9 3.6 %fusion.130 = bf16[4,512,384]{2,1,0:T(8,128)(2,1)} fusion(bf16[4,512,384]{2,1,0:T(8,128)(2,1)} %get-tuple-element.268, s32[]{:T(128)} %get-tuple-element.267, bf16[2048,384]{1,0:T(8,128)(2,1)S(1)} %get-tuple-element.275, bf16[4,512,2048]{2,1,0:T(8,128)(2,1)} %get-tuple-element.274), kind=kOutput, calls=%fused_computation.7.clone.1 | convolution fusion | flops 805502976 | bytes 4064256 | tf_op jit(solution)/shard_map/while/body/eval_jaxpr/dot_general | solution.py:130
  72.5 3.6 %fusion.130 = bf16[4,512,384]{2,1,0:T(8,128)(2,1)} fusion(bf16[4,512,384]{2,1,0:T(8,128)(2,1)} %get-tuple-element.268, s32[]{:T(128)} %get-tuple-element.267, bf16[2048,384]{1,0:T(8,128)(2,1)S(1)} %get-tuple-element.275, bf16[4,512,2048]{2,1,0:T(8,128)(2,1)} %get-tuple-element.274), kind=kOutput, calls=%fused_computation.7.clone.1 | convolution fusion | flops 805502976 | bytes 4064256 | tf_op jit(solution)/shard_map/while/body/eval_jaxpr/dot_general | solution.py:130
  76.1 3.9 %fusion.130 = bf16[4,512,384]{2,1,0:T(8,128)(2,1)} fusion(bf16[4,512,384]{2,1,0:T(8,128)(2,1)} %get-tuple-element.268, s32[]{:T(128)} %get-tuple-element.267, bf16[2048,384]{1,0:T(8,128)(2,1)S(1)} %get-tuple-element.275, bf16[4,512,2048]{2,1,0:T(8,128)(2,1)} %get-tuple-element.274), kind=kOutput, calls=%fused_computation.7.clone.1 | convolution fusion | flops 805502976 | bytes 4064256 | tf_op jit(solution)/shard_map/while/body/eval_jaxpr/dot_general | solution.py:130
  80.0 2.6 fusion.101
  82.6 24.6 %while.33 = (s32[]{:T(128)}, bf16[4,512,1,128]{3,1,2,0:T(8,128)(2,1)S(1)}, s32[4]{0:T(128)S(1)}, s32[2048]{0:T(1024)S(1)}, bf16[2048,1,128]{2,0,1:T(8,128)(2,1)S...) while((s32[]{:T(128)}, ...), condition=%wide.region_6.7_spmd.clone, body=%wide.region_3.6_spmd.clone.sunk | while | flops 548470272 | bytes 13922467 | solution.py:45
  85.9 1.3 fusion.138
  87.8 0.9 fusion.140
  92.0 1.3 fusion.138
  94.0 0.9 fusion.140
  98.2 1.3 fusion.138
  100.2 0.9 fusion.140
  104.4 1.3 fusion.138
  106.3 0.9 fusion.140
  107.3 18.9 %all_to_all.5 = bf16[16,128,128]{2,1,0:T(8,128)(2,1)S(1)} all-to-all(bf16[16,128,128]{2,1,0:T(8,128)(2,1)S(1)} %bitcast.212), channel_id=1, replica_groups=mesh['dp'=8,'tensor'=16] {'tensor'}, dimensions={0} | all-to-all | bytes 1048576 | tf_op jit(solution)/shard_map/all_to_all | solution.py:139
  126.5 4.8 %multiply_reduce_fusion = (f32[128]{0:T(128)S(1)}, f32[128,2048]{1,0:T(8,128)S(1)}) fusion(bf16[128,2048]{0,1:T(8,128)(2,1)S(1)} %bitcast.205, bf16[2048,2048]{1,0:T(8,128)(2,1)} %all-gather.6.cloned.1.call-done, bf16[128,2048]{1,0:T(8,128)(2,1)S(1)} %copy-done), kind=kOutput, calls=%fused_computation.82 | convolution fusion | flops 1075314560 | bytes 10486272 | tf_op jit(solution)/shard_map/dot_general | solution.py:143
  131.3 1.0 multiply_convert_fusion
  132.8 52.0 %all-gather.8.cloned.1.call-done = bf16[2048,2048]{1,0:T(8,128)(2,1)} async-done(((bf16[128,2048]{1,0:T(8,128)(2,1)}), bf16[2048,2048]{1,0:T(8,128)(2,1)}) %all-gather.8.cloned.1.call-update) | async-done | bytes 8388624 | tf_op jit(solution)/shard_map/all_gather | solution.py:148
  184.8 6.6 %convolution_convert_fusion = bf16[16,64,2048]{2,1,0:T(8,128)(2,1)} fusion(bf16[16,128,2048]{2,1,0:T(8,128)(2,1)} %bitcast.195, s32[16,128]{1,0:T(8,128)S(1)} %bitcast_subtract_fusion, pred[16,128]{1,0:T(8,128)(4,1)S(1)} %broadcast_compare_fusion.1), kind=kOutput, calls=%fused_computation.44 | convolution fusion | flops 539230208 | bytes 12593152 | tf_op jit(solution)/shard_map/bst,btd->bsd/dot_general | solution.py:179
  191.4 35.7 %while.32 = (s32[]{:T(128)}, bf16[4,256,1408]{2,1,0:T(8,128)(2,1)}, bf16[4,256,2048]{2,1,0:T(8,128)(2,1)}, bf16[2048,1408]{1,0:T(8,128)(2,1)}, bf16[2048,1408]{1,0:T(8,128)(2,1)}, /*index=5*/s32[]{:T(128)}) while((s32[]{:T(128)}, bf16[4,256,1408]{2,1,0:T(8,128)(2,1)}, bf16[4,256,2048]{2,1,0:T(8,128)(2,1)}, bf16[2048,1408]{1,0:T(8,128)(2,1)}, ...), condition=%wide.region_12.13_spmd, body=%wide.region_11.12_spmd.sunk | while | flops 2954952704 | bytes 40306272 | solution.py:191
  191.5 4.9 %fusion.135 = f32[256,1408]{1,0:T(8,128)S(1)} fusion(bf16[2048,1408]{1,0:T(8,128)(2,1)} %get-tuple-element.322, bf16[4,256,2048]{2,1,0:T(8,128)(2,1)} %get-tuple-element.321, s32[]{:T(128)} %get-tuple-element.313), kind=kOutput, calls=%fused_computation.14.clone.1 | convolution fusion | flops 1476395008 | bytes 8258048 | tf_op jit(solution)/shard_map/while/body/eval_jaxpr/dot_general | solution.py:186
  196.4 4.1 %fusion.136 = bf16[4,256,1408]{2,1,0:T(8,128)(2,1)} fusion(bf16[4,256,1408]{2,1,0:T(8,128)(2,1)} %get-tuple-element.314, s32[]{:T(128)} %get-tuple-element.313, bf16[2048,1408]{1,0:T(8,128)(2,1)S(1)} %copy-done.12, f32[256,1408]{1,0:T(8,128)S(1)} %fusion.135, bf16[4,256,2048]{2,1,0:T(8,128)(2,1)} %get-tuple-element.321), kind=kOutput, calls=%fused_computation.12.clone.1 | convolution fusion | flops 1478557696 | bytes 8979456 | tf_op jit(solution)/shard_map/while/body/eval_jaxpr/dot_general | solution.py:187
  200.4 4.9 %fusion.135 = f32[256,1408]{1,0:T(8,128)S(1)} fusion(bf16[2048,1408]{1,0:T(8,128)(2,1)} %get-tuple-element.322, bf16[4,256,2048]{2,1,0:T(8,128)(2,1)} %get-tuple-element.321, s32[]{:T(128)} %get-tuple-element.313), kind=kOutput, calls=%fused_computation.14.clone.1 | convolution fusion | flops 1476395008 | bytes 8258048 | tf_op jit(solution)/shard_map/while/body/eval_jaxpr/dot_general | solution.py:186
  205.3 4.0 %fusion.136 = bf16[4,256,1408]{2,1,0:T(8,128)(2,1)} fusion(bf16[4,256,1408]{2,1,0:T(8,128)(2,1)} %get-tuple-element.314, s32[]{:T(128)} %get-tuple-element.313, bf16[2048,1408]{1,0:T(8,128)(2,1)S(1)} %copy-done.12, f32[256,1408]{1,0:T(8,128)S(1)} %fusion.135, bf16[4,256,2048]{2,1,0:T(8,128)(2,1)} %get-tuple-element.321), kind=kOutput, calls=%fused_computation.12.clone.1 | convolution fusion | flops 1478557696 | bytes 8979456 | tf_op jit(solution)/shard_map/while/body/eval_jaxpr/dot_general | solution.py:187
  209.3 4.9 %fusion.135 = f32[256,1408]{1,0:T(8,128)S(1)} fusion(bf16[2048,1408]{1,0:T(8,128)(2,1)} %get-tuple-element.322, bf16[4,256,2048]{2,1,0:T(8,128)(2,1)} %get-tuple-element.321, s32[]{:T(128)} %get-tuple-element.313), kind=kOutput, calls=%fused_computation.14.clone.1 | convolution fusion | flops 1476395008 | bytes 8258048 | tf_op jit(solution)/shard_map/while/body/eval_jaxpr/dot_general | solution.py:186
  214.2 4.0 %fusion.136 = bf16[4,256,1408]{2,1,0:T(8,128)(2,1)} fusion(bf16[4,256,1408]{2,1,0:T(8,128)(2,1)} %get-tuple-element.314, s32[]{:T(128)} %get-tuple-element.313, bf16[2048,1408]{1,0:T(8,128)(2,1)S(1)} %copy-done.12, f32[256,1408]{1,0:T(8,128)S(1)} %fusion.135, bf16[4,256,2048]{2,1,0:T(8,128)(2,1)} %get-tuple-element.321), kind=kOutput, calls=%fused_computation.12.clone.1 | convolution fusion | flops 1478557696 | bytes 8979456 | tf_op jit(solution)/shard_map/while/body/eval_jaxpr/dot_general | solution.py:187
  218.3 4.9 %fusion.135 = f32[256,1408]{1,0:T(8,128)S(1)} fusion(bf16[2048,1408]{1,0:T(8,128)(2,1)} %get-tuple-element.322, bf16[4,256,2048]{2,1,0:T(8,128)(2,1)} %get-tuple-element.321, s32[]{:T(128)} %get-tuple-element.313), kind=kOutput, calls=%fused_computation.14.clone.1 | convolution fusion | flops 1476395008 | bytes 8258048 | tf_op jit(solution)/shard_map/while/body/eval_jaxpr/dot_general | solution.py:186
  223.2 4.0 %fusion.136 = bf16[4,256,1408]{2,1,0:T(8,128)(2,1)} fusion(bf16[4,256,1408]{2,1,0:T(8,128)(2,1)} %get-tuple-element.314, s32[]{:T(128)} %get-tuple-element.313, bf16[2048,1408]{1,0:T(8,128)(2,1)S(1)} %copy-done.12, f32[256,1408]{1,0:T(8,128)S(1)} %fusion.135, bf16[4,256,2048]{2,1,0:T(8,128)(2,1)} %get-tuple-element.321), kind=kOutput, calls=%fused_computation.12.clone.1 | convolution fusion | flops 1478557696 | bytes 8979456 | tf_op jit(solution)/shard_map/while/body/eval_jaxpr/dot_general | solution.py:187
  227.2 6.2 %fusion.46 = bf16[1024,1024]{1,0:T(8,128)(2,1)S(1)} fusion(bf16[1024,1408]{1,0:T(8,128)(2,1)} %bitcast.17, bf16[1408,2048]{1,0:T(8,128)(2,1)} %bitcast.217), kind=kOutput, calls=%fused_computation.56 | convolution fusion | flops 2953838592 | bytes 7864320 | tf_op jit(solution)/shard_map/dot_general | solution.py:201
  233.4 6.2 %fusion.49 = bf16[1024,1024]{1,0:T(8,128)(2,1)S(1)} fusion(bf16[1024,1408]{1,0:T(8,128)(2,1)} %bitcast.17, bf16[1408,2048]{1,0:T(8,128)(2,1)} %bitcast.218), kind=kOutput, calls=%fused_computation.57 | convolution fusion | flops 2953838592 | bytes 7864320 | tf_op jit(solution)/shard_map/dot_general | solution.py:201
  239.7 1.3 convolution_convert_fusion.2
  241.1 3.2 %fusion.53 = f32[2048,352]{0,1:T(8,128)S(1)} fusion(bf16[2048,2048]{1,0:T(8,128)(2,1)S(1)} %bitcast.197, bf16[2048,176]{0,1:T(8,128)(2,1)S(1)} %copy-done.13, bf16[2048,176]{0,1:T(8,128)(2,1)S(1)} %copy-done.14), kind=kOutput, calls=%fused_computation.63 | convolution fusion | flops 2955673600 | bytes 12713984 | tf_op jit(solution)/shard_map/dot_general | solution.py:172
  245.4 1.7 fusion.39
  247.1 1.8 dynamic-slice_bitcast_fusion.1
  249.1 1.3 convolution_convert_fusion.1
  250.4 1.7 fusion.37
  252.1 2.0 copy-done.1
  254.9 3.2 convert_add_fusion.1
  258.7 2.8 collective-permute-start.4
  261.7 2.5 convert_add_fusion
  264.9 3.3 %collective-permute-start.12 = (bf16[2,128,512]{2,1,0:T(8,128)(2,1)S(1)}, bf16[2,128,512]{2,1,0:T(8,128)(2,1)S(1)}, u32[]{:S(2)}, u32[]{:S(2)}) collective-permute-start(bf16[2,128,512]{2,1,0:T(8,128)(2,1)S(1)} %fusion.88), channel_id=1, source_target_pairs={{0,12},{1,13},{2,14},{3,15},{4,0},{5,1},{6,2},{7,3},{8,4},{9,5},{1... | collective-permute-start | bytes 786440 | tf_op jit(solution)/shard_map/ppermute | solution.py:81
  268.3 3.3 %collective-permute-start.5 = (bf16[2,128,512]{2,1,0:T(8,128)(2,1)S(1)}, bf16[2,128,512]{2,1,0:T(8,128)(2,1)S(1)}, u32[]{:S(2)}, u32[]{:S(2)}) collective-permute-start(bf16[2,128,512]{2,1,0:T(8,128)(2,1)S(1)} %fusion.76), channel_id=1, source_target_pairs={{0,12},{1,13},{2,14},{3,15},{4,0},{5,1},{6,2},{7,3},{8,4},{9,5},{1... | collective-permute-start | bytes 786440 | tf_op jit(solution)/shard_map/ppermute | solution.py:81
  271.8 3.1 collective-permute-done.12
  274.9 3.8 %collective-permute-start.13 = (bf16[2,128,512]{2,1,0:T(8,128)(2,1)S(1)}, bf16[2,128,512]{2,1,0:T(8,128)(2,1)S(1)}, u32[]{:S(2)}, u32[]{:S(2)}) collective-permute-start(bf16[2,128,512]{2,1,0:T(8,128)(2,1)S(1)} %fusion.72), channel_id=1, source_target_pairs={{0,12},{1,13},{2,14},{3,15},{4,0},{5,1},{6,2},{7,3},{8,4},{9,5},{1... | collective-permute-start | bytes 786440 | tf_op jit(solution)/shard_map/ppermute | solution.py:81
  278.9 1.6 collective-permute-done.5
  280.6 3.8 %collective-permute-start.6 = (bf16[2,128,512]{2,1,0:T(8,128)(2,1)S(1)}, bf16[2,128,512]{2,1,0:T(8,128)(2,1)S(1)}, u32[]{:S(2)}, u32[]{:S(2)}) collective-permute-start(bf16[2,128,512]{2,1,0:T(8,128)(2,1)S(1)} %fusion.75), channel_id=1, source_target_pairs={{0,12},{1,13},{2,14},{3,15},{4,0},{5,1},{6,2},{7,3},{8,4},{9,5},{1... | collective-permute-start | bytes 786440 | tf_op jit(solution)/shard_map/ppermute | solution.py:81
  284.5 1.6 collective-permute-done.13
  286.2 3.8 %collective-permute-start.14 = (bf16[2,128,512]{2,1,0:T(8,128)(2,1)S(1)}, bf16[2,128,512]{2,1,0:T(8,128)(2,1)S(1)}, u32[]{:S(2)}, u32[]{:S(2)}) collective-permute-start(bf16[2,128,512]{2,1,0:T(8,128)(2,1)S(1)} %fusion.71), channel_id=1, source_target_pairs={{0,12},{1,13},{2,14},{3,15},{4,0},{5,1},{6,2},{7,3},{8,4},{9,5},{1... | collective-permute-start | bytes 786440 | tf_op jit(solution)/shard_map/ppermute | solution.py:81
  290.1 1.6 collective-permute-done.6
  291.8 3.7 %collective-permute-done.3 = bf16[2,128,512]{2,1,0:T(8,128)(2,1)S(1)} collective-permute-done((bf16[2,128,512]{2,1,0:T(8,128)(2,1)S(1)}, bf16[2,128,512]{2,1,0:T(8,128)(2,1)S(1)}, u32[]{:S(2)}, u32[]{:S(2)}) %collective-permute-start.3) | collective-permute-done | bytes 262176 | tf_op jit(solution)/shard_map/ppermute | solution.py:80
  295.7 0.9 collective-permute-start.7
  296.7 2.9 collective-permute-done.11
  300.4 0.8 collective-permute-start.15
  301.2 1.1 maximum_bitcast_fusion
  302.3 1.2 broadcast_in_dim.53
  303.5 3.4 %scatter_fusion = bf16[2,16,128,128]{3,2,1,0:T(8,128)(2,1)} fusion(bf16[2,16,128,128]{3,2,1,0:T(8,128)(2,1)} %broadcast_in_dim.53, s32[16]{0:T(128)S(1)} %compare_select_fusion, bf16[16,2,128,128]{3,2,1,0:T(8,128)(2,1)} %maximum_bitcast_fusion), kind=kCustom, calls=%fused_computation | custom fusion | bytes 3145792 | tf_op jit(solution)/shard_map/scatter | solution.py:137
  306.9 1.0 fusion.70
  307.9 1.0 fusion.65
  308.9 0.9 fusion.60
  (120 shorter events, 15.5 us)
Async XLA Ops:
  7.2 4.3 %copy-start.7 = (bf16[2048,128]{1,0:T(8,128)(2,1)S(1)}, bf16[2048,128]{1,0:T(8,128)(2,1)}, u32[]{:S(2)}) copy-start(bf16[2048,128]{1,0:T(8,128)(2,1)} %param.27) | copy-start | bytes 1572868
  7.2 4.3 %copy-start.6 = (bf16[2048,128]{1,0:T(8,128)(2,1)S(1)}, bf16[2048,128]{1,0:T(8,128)(2,1)}, u32[]{:S(2)}) copy-start(bf16[2048,128]{1,0:T(8,128)(2,1)} %param.28) | copy-start | bytes 1572868
  7.2 58.1 %all-gather.4.cloned.1.call-start = ((), (), s32[]{:S(2)}) async-start(), calls=%async_computation.1 | async-start | bytes 8912896 | tf_op jit(solution)/shard_map/all_gather | solution.py:127
  10.6 115.9 %all-gather.6.cloned.1.call-start = ((), (), s32[]{:S(2)}) async-start(), calls=%async_computation.2 | async-start | bytes 8912896 | tf_op jit(solution)/shard_map/all_gather | solution.py:128
  11.4 173.5 %all-gather.8.cloned.1.call-start = ((), (), s32[]{:S(2)}) async-start(), calls=%async_computation.3 | async-start | bytes 8912896 | tf_op jit(solution)/shard_map/all_gather | solution.py:148
  80.0 2.6 copy-start.10
  82.6 43.9 %copy-start = (bf16[128,2048]{1,0:T(8,128)(2,1)S(1)}, bf16[128,2048]{1,0:T(8,128)(2,1)}, u32[]{:S(2)}) copy-start(bf16[128,2048]{1,0:T(8,128)(2,1)} %param.23) | copy-start | bytes 1572868
  126.5 4.8 %copy-start.11 = (f32[2048]{0:T(1024)S(1)}, f32[2048]{0:T(1024)}, u32[]{:S(2)}) copy-start(f32[2048]{0:T(1024)} %param.30) | copy-start | bytes 24580
  126.5 5.9 %copy-start.8 = (f32[2048,6]{0,1:T(8,128)S(1)}, f32[2048,6]{0,1:T(8,128)}, u32[]{:S(2)}) copy-start(f32[2048,6]{0,1:T(8,128)} %param.38) | copy-start | bytes 147460
  126.5 5.9 %copy-start.9 = (s32[2048,6]{0,1:T(8,128)S(1)}, s32[2048,6]{0,1:T(8,128)}, u32[]{:S(2)}) copy-start(s32[2048,6]{0,1:T(8,128)} %param.37) | copy-start | bytes 147460
  191.4 4.9 %copy-start.12 = (bf16[2048,1408]{1,0:T(8,128)(2,1)S(1)}, bf16[2048,1408]{1,0:T(8,128)(2,1)}, u32[]{:S(2)}) copy-start(bf16[2048,1408]{1,0:T(8,128)(2,1)} %get-tuple-element.323) | copy-start | bytes 17301508 | tf_op jit(solution)/shard_map/while
  200.4 4.9 %copy-start.12 = (bf16[2048,1408]{1,0:T(8,128)(2,1)S(1)}, bf16[2048,1408]{1,0:T(8,128)(2,1)}, u32[]{:S(2)}) copy-start(bf16[2048,1408]{1,0:T(8,128)(2,1)} %get-tuple-element.323) | copy-start | bytes 17301508 | tf_op jit(solution)/shard_map/while
  209.3 4.9 %copy-start.12 = (bf16[2048,1408]{1,0:T(8,128)(2,1)S(1)}, bf16[2048,1408]{1,0:T(8,128)(2,1)}, u32[]{:S(2)}) copy-start(bf16[2048,1408]{1,0:T(8,128)(2,1)} %get-tuple-element.323) | copy-start | bytes 17301508 | tf_op jit(solution)/shard_map/while
  218.3 4.9 %copy-start.12 = (bf16[2048,1408]{1,0:T(8,128)(2,1)S(1)}, bf16[2048,1408]{1,0:T(8,128)(2,1)}, u32[]{:S(2)}) copy-start(bf16[2048,1408]{1,0:T(8,128)(2,1)} %get-tuple-element.323) | copy-start | bytes 17301508 | tf_op jit(solution)/shard_map/while
  227.2 13.8 %slice-start = ((s8[8388608]{0:T(1024)(128)(4,1)}), s8[4194304]{0:T(1024)(128)(4,1)S(1)}, s32[]{:S(2)}) async-start(s8[8388608]{0:T(1024)(128)(4,1)} %bitcast.196), calls=%async_computation.4 | async-start | bytes 8388608
  233.4 7.6 %slice-start.1 = ((s8[8388608]{0:T(1024)(128)(4,1)}), s8[4194304]{0:T(1024)(128)(4,1)S(1)}, s32[]{:S(2)}) async-start(s8[8388608]{0:T(1024)(128)(4,1)} %bitcast.196), calls=%async_computation.5 | async-start | bytes 8388608
  239.7 1.4 copy-start.13
  239.7 1.3 copy-start.14
  244.3 1.1 copy-start.15
  247.1 3.3 %copy-start.3 = (bf16[2048,1024]{1,0:T(8,128)(2,1)}, bf16[2048,1024]{1,0:T(8,128)(2,1)S(1)}, u32[]{:S(2)}) copy-start(bf16[2048,1024]{1,0:T(8,128)(2,1)S(1)} %fusion.39) | copy-start | bytes 12582916
  248.9 6.0 %collective-permute-start = (bf16[4,2,128,1024]{3,2,1,0:T(8,128)(2,1)}, bf16[4,2,128,1024]{3,2,1,0:T(8,128)(2,1)}, u32[]{:S(2)}, u32[]{:S(2)}) collective-permute-start(bf16[4,2,128,1024]{3,2,1,0:T(8,128)(2,1)} %dynamic-slice_bitcast_fusion.1), channel_id=1, source_target_pairs={{0,1},{1,0},{2,3},{3,2},{4,5},{5,4},{6,7},{7,6},{8,9},{9,8},{10,11... | collective-permute-start | bytes 6291464 | tf_op jit(solution)/shard_map/ppermute | solution.py:68
  252.1 2.0 copy-start.1
  252.1 2.7 copy-start.16
  254.3 7.3 %collective-permute-start.8 = (bf16[4,2,128,1024]{3,2,1,0:T(8,128)(2,1)S(1)}, bf16[4,2,128,1024]{3,2,1,0:T(8,128)(2,1)}, u32[]{:S(2)}, u32[]{:S(2)}) collective-permute-start(bf16[4,2,128,1024]{3,2,1,0:T(8,128)(2,1)S(1)} %dynamic-slice_bitcast_fusion), channel_id=1, source_target_pairs={{0,1},{1,0},{2,3},{3,2},{4,5},{5,4},{6,7},{7,6},{8,9},{9,8},{10,11... | collective-permute-start | bytes 6291464 | tf_op jit(solution)/shard_map/ppermute | solution.py:68
  258.0 3.6 %copy-start.2 = (bf16[2048,1024]{1,0:T(8,128)(2,1)S(1)}, bf16[2048,1024]{1,0:T(8,128)(2,1)}, u32[]{:S(2)}) copy-start(bf16[2048,1024]{1,0:T(8,128)(2,1)} %copy-done.1) | copy-start | bytes 12582916
  258.7 9.5 %collective-permute-start.4 = (bf16[2,128,512]{2,1,0:T(8,128)(2,1)S(1)}, bf16[2,128,512]{2,1,0:T(8,128)(2,1)S(1)}, u32[]{:S(2)}, u32[]{:S(2)}) collective-permute-start(bf16[2,128,512]{2,1,0:T(8,128)(2,1)S(1)} %fusion.86), channel_id=1, source_target_pairs={{0,12},{1,13},{2,14},{3,15},{4,0},{5,1},{6,2},{7,3},{8,4},{9,5},{1... | collective-permute-start | bytes 786440 | tf_op jit(solution)/shard_map/ppermute | solution.py:81
  261.6 10.1 %collective-permute-start.1 = (bf16[2,128,512]{2,1,0:T(8,128)(2,1)S(1)}, bf16[2,128,512]{2,1,0:T(8,128)(2,1)S(1)}, u32[]{:S(2)}, u32[]{:S(2)}) collective-permute-start(bf16[2,128,512]{2,1,0:T(8,128)(2,1)S(1)} %fusion.85), channel_id=1, source_target_pairs={{0,4},{1,5},{2,6},{3,7},{4,8},{5,9},{6,10},{7,11},{8,12},{9,13},{1... | collective-permute-start | bytes 786440 | tf_op jit(solution)/shard_map/ppermute | solution.py:80
  264.9 10.0 %collective-permute-start.12 = (bf16[2,128,512]{2,1,0:T(8,128)(2,1)S(1)}, bf16[2,128,512]{2,1,0:T(8,128)(2,1)S(1)}, u32[]{:S(2)}, u32[]{:S(2)}) collective-permute-start(bf16[2,128,512]{2,1,0:T(8,128)(2,1)S(1)} %fusion.88), channel_id=1, source_target_pairs={{0,12},{1,13},{2,14},{3,15},{4,0},{5,1},{6,2},{7,3},{8,4},{9,5},{1... | collective-permute-start | bytes 786440 | tf_op jit(solution)/shard_map/ppermute | solution.py:81
  268.2 10.5 %collective-permute-start.9 = (bf16[2,128,512]{2,1,0:T(8,128)(2,1)S(1)}, bf16[2,128,512]{2,1,0:T(8,128)(2,1)S(1)}, u32[]{:S(2)}, u32[]{:S(2)}) collective-permute-start(bf16[2,128,512]{2,1,0:T(8,128)(2,1)S(1)} %fusion.87), channel_id=1, source_target_pairs={{0,4},{1,5},{2,6},{3,7},{4,8},{5,9},{6,10},{7,11},{8,12},{9,13},{1... | collective-permute-start | bytes 786440 | tf_op jit(solution)/shard_map/ppermute | solution.py:80
  268.3 12.1 %collective-permute-start.5 = (bf16[2,128,512]{2,1,0:T(8,128)(2,1)S(1)}, bf16[2,128,512]{2,1,0:T(8,128)(2,1)S(1)}, u32[]{:S(2)}, u32[]{:S(2)}) collective-permute-start(bf16[2,128,512]{2,1,0:T(8,128)(2,1)S(1)} %fusion.76), channel_id=1, source_target_pairs={{0,12},{1,13},{2,14},{3,15},{4,0},{5,1},{6,2},{7,3},{8,4},{9,5},{1... | collective-permute-start | bytes 786440 | tf_op jit(solution)/shard_map/ppermute | solution.py:81
  271.7 12.6 %collective-permute-start.2 = (bf16[2,128,512]{2,1,0:T(8,128)(2,1)S(1)}, bf16[2,128,512]{2,1,0:T(8,128)(2,1)S(1)}, u32[]{:S(2)}, u32[]{:S(2)}) collective-permute-start(bf16[2,128,512]{2,1,0:T(8,128)(2,1)S(1)} %fusion.78), channel_id=1, source_target_pairs={{0,4},{1,5},{2,6},{3,7},{4,8},{5,9},{6,10},{7,11},{8,12},{9,13},{1... | collective-permute-start | bytes 786440 | tf_op jit(solution)/shard_map/ppermute | solution.py:80
  274.9 11.2 %collective-permute-start.13 = (bf16[2,128,512]{2,1,0:T(8,128)(2,1)S(1)}, bf16[2,128,512]{2,1,0:T(8,128)(2,1)S(1)}, u32[]{:S(2)}, u32[]{:S(2)}) collective-permute-start(bf16[2,128,512]{2,1,0:T(8,128)(2,1)S(1)} %fusion.72), channel_id=1, source_target_pairs={{0,12},{1,13},{2,14},{3,15},{4,0},{5,1},{6,2},{7,3},{8,4},{9,5},{1... | collective-permute-start | bytes 786440 | tf_op jit(solution)/shard_map/ppermute | solution.py:81
  278.8 11.2 %collective-permute-start.10 = (bf16[2,128,512]{2,1,0:T(8,128)(2,1)S(1)}, bf16[2,128,512]{2,1,0:T(8,128)(2,1)S(1)}, u32[]{:S(2)}, u32[]{:S(2)}) collective-permute-start(bf16[2,128,512]{2,1,0:T(8,128)(2,1)S(1)} %fusion.74), channel_id=1, source_target_pairs={{0,4},{1,5},{2,6},{3,7},{4,8},{5,9},{6,10},{7,11},{8,12},{9,13},{1... | collective-permute-start | bytes 786440 | tf_op jit(solution)/shard_map/ppermute | solution.py:80
  280.6 11.2 %collective-permute-start.6 = (bf16[2,128,512]{2,1,0:T(8,128)(2,1)S(1)}, bf16[2,128,512]{2,1,0:T(8,128)(2,1)S(1)}, u32[]{:S(2)}, u32[]{:S(2)}) collective-permute-start(bf16[2,128,512]{2,1,0:T(8,128)(2,1)S(1)} %fusion.75), channel_id=1, source_target_pairs={{0,12},{1,13},{2,14},{3,15},{4,0},{5,1},{6,2},{7,3},{8,4},{9,5},{1... | collective-permute-start | bytes 786440 | tf_op jit(solution)/shard_map/ppermute | solution.py:81
  284.4 11.1 %collective-permute-start.3 = (bf16[2,128,512]{2,1,0:T(8,128)(2,1)S(1)}, bf16[2,128,512]{2,1,0:T(8,128)(2,1)S(1)}, u32[]{:S(2)}, u32[]{:S(2)}) collective-permute-start(bf16[2,128,512]{2,1,0:T(8,128)(2,1)S(1)} %fusion.77), channel_id=1, source_target_pairs={{0,4},{1,5},{2,6},{3,7},{4,8},{5,9},{6,10},{7,11},{8,12},{9,13},{1... | collective-permute-start | bytes 786440 | tf_op jit(solution)/shard_map/ppermute | solution.py:80
  286.2 10.4 %collective-permute-start.14 = (bf16[2,128,512]{2,1,0:T(8,128)(2,1)S(1)}, bf16[2,128,512]{2,1,0:T(8,128)(2,1)S(1)}, u32[]{:S(2)}, u32[]{:S(2)}) collective-permute-start(bf16[2,128,512]{2,1,0:T(8,128)(2,1)S(1)} %fusion.71), channel_id=1, source_target_pairs={{0,12},{1,13},{2,14},{3,15},{4,0},{5,1},{6,2},{7,3},{8,4},{9,5},{1... | collective-permute-start | bytes 786440 | tf_op jit(solution)/shard_map/ppermute | solution.py:81
  290.0 9.5 %collective-permute-start.11 = (bf16[2,128,512]{2,1,0:T(8,128)(2,1)S(1)}, bf16[2,128,512]{2,1,0:T(8,128)(2,1)S(1)}, u32[]{:S(2)}, u32[]{:S(2)}) collective-permute-start(bf16[2,128,512]{2,1,0:T(8,128)(2,1)S(1)} %fusion.73), channel_id=1, source_target_pairs={{0,4},{1,5},{2,6},{3,7},{4,8},{5,9},{6,10},{7,11},{8,12},{9,13},{1... | collective-permute-start | bytes 786440 | tf_op jit(solution)/shard_map/ppermute | solution.py:80
  295.6 5.6 %copy-start.4 = (bf16[2048,128]{1,0:T(8,128)(2,1)S(1)}, bf16[2048,128]{1,0:T(8,128)(2,1)}, u32[]{:S(2)}) copy-start(bf16[2048,128]{1,0:T(8,128)(2,1)} %get-tuple-element.152) | copy-start | bytes 1572868
  295.6 5.6 %copy-start.5 = (bf16[2048,128]{1,0:T(8,128)(2,1)S(1)}, bf16[2048,128]{1,0:T(8,128)(2,1)}, u32[]{:S(2)}) copy-start(bf16[2048,128]{1,0:T(8,128)(2,1)} %get-tuple-element.155) | copy-start | bytes 1572868
  295.7 11.2 %collective-permute-start.7 = (bf16[128,1024]{1,0:T(8,128)(2,1)S(1)}, bf16[128,1024]{1,0:T(8,128)(2,1)}, u32[]{:S(2)}, u32[]{:S(2)}) collective-permute-start(bf16[128,1024]{1,0:T(8,128)(2,1)S(1)} %fusion.89), channel_id=1, source_target_pairs={{0,2},{1,3},{2,0},{3,1},{4,6},{5,7},{6,4},{7,5},{8,10},{9,11},{10,... | collective-permute-start | bytes 786440 | tf_op jit(solution)/shard_map/ppermute | solution.py:96
  300.4 7.5 %collective-permute-start.15 = (bf16[128,1024]{1,0:T(8,128)(2,1)}, bf16[128,1024]{1,0:T(8,128)(2,1)}, u32[]{:S(2)}, u32[]{:S(2)}) collective-permute-start(bf16[128,1024]{1,0:T(8,128)(2,1)} %fusion.90), channel_id=1, source_target_pairs={{0,2},{1,3},{2,0},{3,1},{4,6},{5,7},{6,4},{7,5},{8,10},{9,11},{10,... | collective-permute-start | bytes 786440 | tf_op jit(solution)/shard_map/ppermute | solution.py:96
Sparse Core Ops, SparseCore 0:
  10.7 54.5 all-gather.3
  67.0 58.6 all-gather.5
  132.5 52.2 all-gather.7

commit v7 on v0

--- a/solution.py
+++ b/solution.py
@@ -143,8 +143,7 @@
     attention = jnp.dot(context_rows, out_weight_all, preferred_element_type=jnp.float32)
     residual = (tokens.astype(jnp.float32) + attention).astype(jnp.bfloat16)
     normed_ffn = rms_scale(residual, ffn_gain)
-    pieces = 2
-    piece_width = model_width // pieces
+    piece_edges = [0, model_width * 5 // 8, model_width]
     normed_stream = lax.all_gather(normed_ffn, "tensor", axis=0, tiled=True)
 
     local_experts = expert_gate.shape[0]
@@ -190,8 +189,9 @@
     ]
 
     outs = []
-    for k in range(pieces):
-        columns = slice(k * piece_width, (k + 1) * piece_width)
+    for k in range(len(piece_edges) - 1):
+        columns = slice(piece_edges[k], piece_edges[k + 1])
+        piece_width = piece_edges[k + 1] - piece_edges[k]
         term = jnp.dot(hidden_all, shared_down[:, columns], preferred_element_type=jnp.float32)
         for local in range(local_experts):
             rows = jnp.dot(

time: 288 us -> 302 us (1.049)
  waiting for transfers between devices: 118 us -> 126 us
    ppermute x6, waiting for transfers between devices: 12.5 us -> 20.8 us  [ring_reduce_scatter(): recv_f = lax.ppermute(carry_f, 'tensor', forward_pairs)]
  transfers between devices with their start and end apart: 19 -> 19, of which waited for: 7 -> 8; matrix products, arithmetic and copies ran while one was open for 19% -> 19% of each run, Pallas kernels for 0% -> 0%
where the time goes in v7:
time: 302 us; the launch traced here: 301 us
  waiting for transfers between devices  126 us (42%)
  matrix products  65.7 us (22%)
  other arithmetic  25.2 us (8%)
  starting transfers between devices  24.2 us (8%)
  blocking collectives  18.9 us (6%)
  local copies, waits for them, and re-layouts  18.1 us (6%)
  between operations  14.4 us (5%)
  loops' own time  7.7 us (3%)
    all_gather x1, waiting for transfers between devices, shards(): lax.all_gather(rms_scale(tokens, attention_gain), 'tensor', axis=0, tiled...  52.3 us
    all_gather x1, waiting for transfers between devices, shards(): normed_stream = lax.all_gather(normed_ffn, 'tensor', axis=0, tiled=True)  52 us
    ppermute x6, waiting for transfers between devices, ring_reduce_scatter(): recv_f = lax.ppermute(carry_f, 'tensor', forward_pairs)  20.8 us
    all_to_all x1, blocking collectives, shards(): lax.all_to_all(context.reshape(groups, tok_dev, inner), 'tensor', split_a...  18.9 us
    ppermute x6, starting transfers between devices, ring_reduce_scatter(): recv_b = lax.ppermute(carry_b, 'tensor', backward_pairs)  18.5 us
    dot_general x4, matrix products, shards(): jnp.dot(rows, projection, preferred_element_type=jnp.float32)  14.7 us
    dot_general x1, matrix products, shards(): jnp.dot(picked, expert_gate[local], preferred_element_type=jnp.float32)  9.36 us
    another operation x1, loops' own time, attend(): context = lax.map(one_block, starts).reshape(total_tokens, inner)  7.7 us
  transfers between devices with their start and end apart: 19, of which 8 were waited for; matrix products, arithmetic and copies ran while one was open for 19% of the time, Pallas kernels for 0%

profile of v7, /device:TPU:0, one launch (start us, length us, event | category | flops | bytes accessed | tf_op | source)
XLA Modules:
  0.0 300.6 jit_solution(12890776957076383150)
XLA Ops:
  7.2 1.2 fusion.49
  8.4 2.0 fusion.51
  11.3 1.6 pad_maximum_fusion
  12.9 52.3 %all-gather.4.cloned.1.call-done = bf16[2048,2048]{1,0:T(8,128)(2,1)} async-done(((bf16[128,2048]{1,0:T(8,128)(2,1)}), bf16[2048,2048]{1,0:T(8,128)(2,1)}) %all-gather.4.cloned.1.call-update) | async-done | bytes 8388624 | tf_op jit(solution)/shard_map/all_gather | solution.py:127
  65.2 14.7 %while.21 = (s32[]{:T(128)}, bf16[4,512,384]{2,1,0:T(8,128)(2,1)}, bf16[4,512,2048]{2,1,0:T(8,128)(2,1)}, bf16[2048,384]{1,0:T(8,128)(2,1)S(1)}, s32[]{:T(128)}) while((s32[]{:T(128)}, bf16[4,512,384]{2,1,0:T(8,128)(2,1)}, bf16[4,512,2048]{2,1,0:T(8,128)(2,1)}, bf16[2048,384]{1,0:T(8,128)(2,1)S(1)}, s32[]{:T(128)}) %tuple.62), condition=%wide.region_2.3_spmd, body=%wide.region_1.2_spmd.sunk | while | flops 805502976 | bytes 4064325 | solution.py:129
  65.2 3.6 %fusion.116 = bf16[4,512,384]{2,1,0:T(8,128)(2,1)} fusion(bf16[4,512,384]{2,1,0:T(8,128)(2,1)} %get-tuple-element.199, s32[]{:T(128)S(6)} %copy.34, bf16[2048,384]{1,0:T(8,128)(2,1)S(1)} %get-tuple-element.206, bf16[4,512,2048]{2,1,0:T(8,128)(2,1)} %get-tuple-element.205), kind=kOutput, calls=%fused_computation.7.clone.1 | convolution fusion | flops 805502976 | bytes 4064256 | tf_op jit(solution)/shard_map/while/body/eval_jaxpr/dot_general | solution.py:130
  68.8 3.6 %fusion.116 = bf16[4,512,384]{2,1,0:T(8,128)(2,1)} fusion(bf16[4,512,384]{2,1,0:T(8,128)(2,1)} %get-tuple-element.199, s32[]{:T(128)S(6)} %copy.34, bf16[2048,384]{1,0:T(8,128)(2,1)S(1)} %get-tuple-element.206, bf16[4,512,2048]{2,1,0:T(8,128)(2,1)} %get-tuple-element.205), kind=kOutput, calls=%fused_computation.7.clone.1 | convolution fusion | flops 805502976 | bytes 4064256 | tf_op jit(solution)/shard_map/while/body/eval_jaxpr/dot_general | solution.py:130
  72.4 3.6 %fusion.116 = bf16[4,512,384]{2,1,0:T(8,128)(2,1)} fusion(bf16[4,512,384]{2,1,0:T(8,128)(2,1)} %get-tuple-element.199, s32[]{:T(128)S(6)} %copy.34, bf16[2048,384]{1,0:T(8,128)(2,1)S(1)} %get-tuple-element.206, bf16[4,512,2048]{2,1,0:T(8,128)(2,1)} %get-tuple-element.205), kind=kOutput, calls=%fused_computation.7.clone.1 | convolution fusion | flops 805502976 | bytes 4064256 | tf_op jit(solution)/shard_map/while/body/eval_jaxpr/dot_general | solution.py:130
  76.0 3.9 %fusion.116 = bf16[4,512,384]{2,1,0:T(8,128)(2,1)} fusion(bf16[4,512,384]{2,1,0:T(8,128)(2,1)} %get-tuple-element.199, s32[]{:T(128)S(6)} %copy.34, bf16[2048,384]{1,0:T(8,128)(2,1)S(1)} %get-tuple-element.206, bf16[4,512,2048]{2,1,0:T(8,128)(2,1)} %get-tuple-element.205), kind=kOutput, calls=%fused_computation.7.clone.1 | convolution fusion | flops 805502976 | bytes 4064256 | tf_op jit(solution)/shard_map/while/body/eval_jaxpr/dot_general | solution.py:130
  79.9 2.6 fusion.93
  82.5 24.6 %while.22 = (s32[]{:T(128)}, bf16[4,512,1,128]{3,1,2,0:T(8,128)(2,1)S(1)}, s32[4]{0:T(128)S(1)}, s32[2048]{0:T(1024)S(1)}, bf16[2048,1,128]{2,0,1:T(8,128)(2,1)S...) while((s32[]{:T(128)}, ...), condition=%wide.region_6.7_spmd.clone, body=%wide.region_3.6_spmd.clone.sunk | while | flops 548470272 | bytes 13922475 | solution.py:45
  85.8 1.3 fusion.118
  87.0 0.7 fusion.119
  87.7 0.9 fusion.120
  91.9 1.3 fusion.118
  93.2 0.7 fusion.119
  93.9 0.9 fusion.120
  98.1 1.3 fusion.118
  100.0 0.9 fusion.120
  104.2 1.3 fusion.118
  106.2 0.9 fusion.120
  107.2 18.9 %all_to_all.5 = bf16[16,128,128]{2,1,0:T(8,128)(2,1)S(1)} all-to-all(bf16[16,128,128]{2,1,0:T(8,128)(2,1)S(1)} %bitcast.200), channel_id=1, replica_groups=mesh['dp'=8,'tensor'=16] {'tensor'}, dimensions={0} | all-to-all | bytes 1048576 | tf_op jit(solution)/shard_map/all_to_all | solution.py:139
  126.4 4.8 %multiply_reduce_fusion = (f32[128]{0:T(128)S(1)}, f32[128,2048]{1,0:T(8,128)S(1)}) fusion(bf16[128,2048]{0,1:T(8,128)(2,1)S(1)} %bitcast.190, bf16[2048,2048]{1,0:T(8,128)(2,1)} %all-gather.6.cloned.1.call-done, bf16[128,2048]{1,0:T(8,128)(2,1)S(1)} %copy-done.2), kind=kOutput, calls=%fused_computation.71 | convolution fusion | flops 1075314560 | bytes 10486272 | tf_op jit(solution)/shard_map/dot_general | solution.py:143
  131.2 1.0 multiply_convert_fusion.1
  132.7 52.0 %all-gather.8.cloned.1.call-done = bf16[2048,2048]{1,0:T(8,128)(2,1)} async-done(((bf16[128,2048]{1,0:T(8,128)(2,1)}), bf16[2048,2048]{1,0:T(8,128)(2,1)}) %all-gather.8.cloned.1.call-update) | async-done | bytes 8388624 | tf_op jit(solution)/shard_map/all_gather | solution.py:147
  184.7 4.8 %convolution_convert_fusion.1 = bf16[16,64,2048]{2,1,0:T(8,128)(2,1)S(1)} fusion(bf16[16,128,2048]{2,1,0:T(8,128)(2,1)} %bitcast.182, s32[16,128]{1,0:T(8,128)S(1)} %bitcast_subtract_fusion, pred[16,128]{1,0:T(8,128)(4,1)S(1)} %broadcast_compare_fusion.1), kind=kOutput, calls=%fused_computation.38 | convolution fusion | flops 539230208 | bytes 12593152 | tf_op jit(solution)/shard_map/bst,btd->bsd/dot_general | solution.py:176
  189.5 9.4 %fusion.32 = f32[1024,1408]{1,0:T(8,128)S(1)} fusion(bf16[1024,2048]{1,0:T(8,128)(2,1)S(1)} %bitcast.185, bf16[1,2048,1408]{2,1,0:T(8,128)(2,1)} %param.32), kind=kOutput, calls=%fused_computation.33 | convolution fusion | flops 5905580032 | bytes 15728640 | tf_op jit(solution)/shard_map/dot_general | solution.py:180
  198.9 7.1 %multiply_convert_fusion = bf16[1024,1408]{1,0:T(8,128)(2,1)S(1)} fusion(f32[1024,1408]{1,0:T(8,128)S(1)} %fusion.32, bf16[1024,2048]{1,0:T(8,128)(2,1)S(1)} %bitcast.186, bf16[1,2048,1408]{2,1,0:T(8,128)(2,1)S(1)} %bitcast.204), kind=kOutput, calls=%fused_computation.35 | convolution fusion | flops 5914230784 | bytes 18612224 | tf_op jit(solution)/shard_map/dot_general | solution.py:182
  206.0 2.6 fusion.41
  208.7 4.7 %convolution_convert_fusion.2 = bf16[1024,1280]{1,0:T(8,128)(2,1)S(1)} fusion(bf16[1024,1408]{1,0:T(8,128)(2,1)S(1)} %multiply_convert_fusion, bf16[1408,2048]{1,0:T(8,128)(2,1)S(1)} %bitcast.208), kind=kOutput, calls=%fused_computation.39 | convolution fusion | flops 3692298240 | bytes 9109504 | tf_op jit(solution)/shard_map/dot_general | solution.py:197
  213.4 3.2 %fusion.45 = f32[2048,352]{0,1:T(8,128)S(1)} fusion(bf16[2048,2048]{1,0:T(8,128)(2,1)S(1)} %bitcast.184, bf16[2048,176]{0,1:T(8,128)(2,1)S(1)} %copy-done.12, bf16[2048,176]{0,1:T(8,128)(2,1)S(1)} %copy-done.13), kind=kOutput, calls=%fused_computation.60 | convolution fusion | flops 2955673600 | bytes 12713984 | tf_op jit(solution)/shard_map/dot_general | solution.py:171
  217.0 1.0 convolution_convert_fusion.3
  218.1 1.2 fusion.29
  219.4 1.4 dynamic-slice_bitcast_fusion.1
  221.5 1.6 convolution_convert_fusion
  223.1 2.0 fusion.27
  225.1 2.3 copy-done.1
  227.4 1.8 dynamic-slice_bitcast_fusion
  229.4 1.7 convert_add_fusion.1
  231.4 1.2 copy-done
  232.6 1.6 collective-permute-start.9
  234.2 1.8 collective-permute-start.12
  236.0 4.9 %collective-permute-done.9 = bf16[2,128,384]{2,1,0:T(8,128)(2,1)S(1)} collective-permute-done((bf16[2,128,384]{2,1,0:T(8,128)(2,1)S(1)}, bf16[2,128,384]{2,1,0:T(8,128)(2,1)S(1)}, u32[]{:S(2)}, u32[]{:S(2)}) %collective-permute-start.9) | collective-permute-done | bytes 196640 | tf_op jit(solution)/shard_map/ppermute | solution.py:80
  240.9 1.0 fusion.75
  242.4 3.0 %collective-permute-start.13 = (bf16[2,128,384]{2,1,0:T(8,128)(2,1)S(1)}, bf16[2,128,384]{2,1,0:T(8,128)(2,1)S(1)}, u32[]{:S(2)}, u32[]{:S(2)}) collective-permute-start(bf16[2,128,384]{2,1,0:T(8,128)(2,1)S(1)} %fusion.73), channel_id=1, source_target_pairs={{0,12},{1,13},{2,14},{3,15},{4,0},{5,1},{6,2},{7,3},{8,4},{9,5},{1... | collective-permute-start | bytes 589832 | tf_op jit(solution)/shard_map/ppermute | solution.py:81
  245.4 4.1 %collective-permute-done.10 = bf16[2,128,384]{2,1,0:T(8,128)(2,1)S(1)} collective-permute-done((bf16[2,128,384]{2,1,0:T(8,128)(2,1)S(1)}, bf16[2,128,384]{2,1,0:T(8,128)(2,1)S(1)}, u32[]{:S(2)}, u32[]{:S(2)}) %collective-permute-start.10) | collective-permute-done | bytes 196640 | tf_op jit(solution)/shard_map/ppermute | solution.py:80
  249.5 1.0 fusion.74
  250.7 3.5 %collective-permute-start.14 = (bf16[2,128,384]{2,1,0:T(8,128)(2,1)S(1)}, bf16[2,128,384]{2,1,0:T(8,128)(2,1)S(1)}, u32[]{:S(2)}, u32[]{:S(2)}) collective-permute-start(bf16[2,128,384]{2,1,0:T(8,128)(2,1)S(1)} %fusion.72), channel_id=1, source_target_pairs={{0,12},{1,13},{2,14},{3,15},{4,0},{5,1},{6,2},{7,3},{8,4},{9,5},{1... | collective-permute-start | bytes 589832 | tf_op jit(solution)/shard_map/ppermute | solution.py:81
  254.2 3.1 %convert_add_fusion = f32[4,2,128,1280]{3,2,1,0:T(8,128)S(1)} fusion(bf16[4,2,128,1280]{3,2,1,0:T(8,128)(2,1)} %collective-permute-done, bf16[4,2,2,128,1280]{4,3,2,1,0:T(8,128)(2,1)} %bitcast.189, s32[]{:T(128)S(6)} %select_n.137), kind=kLoop, calls=%fused_computation.37 | loop fusion | flops 3932160 | bytes 10485764 | tf_op jit(solution)/shard_map/add | solution.py:69
  258.1 3.3 %collective-permute-start.4 = (bf16[2,128,640]{2,1,0:T(8,128)(2,1)S(1)}, bf16[2,128,640]{2,1,0:T(8,128)(2,1)S(1)}, u32[]{:S(2)}, u32[]{:S(2)}) collective-permute-start(bf16[2,128,640]{2,1,0:T(8,128)(2,1)S(1)} %fusion.77), channel_id=1, source_target_pairs={{0,12},{1,13},{2,14},{3,15},{4,0},{5,1},{6,2},{7,3},{8,4},{9,5},{1... | collective-permute-start | bytes 983048 | tf_op jit(solution)/shard_map/ppermute | solution.py:81
  261.4 1.0 bitcast_add_fusion.9
  262.4 4.4 %collective-permute-done.1 = bf16[2,128,640]{2,1,0:T(8,128)(2,1)S(1)} collective-permute-done((bf16[2,128,640]{2,1,0:T(8,128)(2,1)S(1)}, bf16[2,128,640]{2,1,0:T(8,128)(2,1)S(1)}, u32[]{:S(2)}, u32[]{:S(2)}) %collective-permute-start.1) | collective-permute-done | bytes 327712 | tf_op jit(solution)/shard_map/ppermute | solution.py:80
  267.1 3.3 %collective-permute-start.5 = (bf16[2,128,640]{2,1,0:T(8,128)(2,1)S(1)}, bf16[2,128,640]{2,1,0:T(8,128)(2,1)S(1)}, u32[]{:S(2)}, u32[]{:S(2)}) collective-permute-start(bf16[2,128,640]{2,1,0:T(8,128)(2,1)S(1)} %fusion.59), channel_id=1, source_target_pairs={{0,12},{1,13},{2,14},{3,15},{4,0},{5,1},{6,2},{7,3},{8,4},{9,5},{1... | collective-permute-start | bytes 983048 | tf_op jit(solution)/shard_map/ppermute | solution.py:81
  270.4 5.0 %collective-permute-done.2 = bf16[2,128,640]{2,1,0:T(8,128)(2,1)S(1)} collective-permute-done((bf16[2,128,640]{2,1,0:T(8,128)(2,1)S(1)}, bf16[2,128,640]{2,1,0:T(8,128)(2,1)S(1)}, u32[]{:S(2)}, u32[]{:S(2)}) %collective-permute-start.2) | collective-permute-done | bytes 327712 | tf_op jit(solution)/shard_map/ppermute | solution.py:80
  275.6 3.5 %collective-permute-start.6 = (bf16[2,128,640]{2,1,0:T(8,128)(2,1)S(1)}, bf16[2,128,640]{2,1,0:T(8,128)(2,1)S(1)}, u32[]{:S(2)}, u32[]{:S(2)}) collective-permute-start(bf16[2,128,640]{2,1,0:T(8,128)(2,1)S(1)} %fusion.58), channel_id=1, source_target_pairs={{0,12},{1,13},{2,14},{3,15},{4,0},{5,1},{6,2},{7,3},{8,4},{9,5},{1... | collective-permute-start | bytes 983048 | tf_op jit(solution)/shard_map/ppermute | solution.py:81
  279.9 1.4 collective-permute-start.15
  281.3 2.5 collective-permute-done.3
  283.9 0.8 fusion.78
  284.7 1.4 collective-permute-start.7
  286.3 1.2 broadcast_in_dim.45
  287.5 3.0 scatter_fusion
  290.4 1.1 fusion.71
  292.1 1.0 fusion.57
  293.1 0.9 fusion.52
  (114 shorter events, 13.4 us)
Async XLA Ops:
  7.2 58.1 %all-gather.4.cloned.1.call-start = ((), (), s32[]{:S(2)}) async-start(), calls=%async_computation.1 | async-start | bytes 8912896 | tf_op jit(solution)/shard_map/all_gather | solution.py:127
  10.5 115.9 %all-gather.6.cloned.1.call-start = ((), (), s32[]{:S(2)}) async-start(), calls=%async_computation.2 | async-start | bytes 8912896 | tf_op jit(solution)/shard_map/all_gather | solution.py:128
  11.3 173.4 %all-gather.8.cloned.1.call-start = ((), (), s32[]{:S(2)}) async-start(), calls=%async_computation.3 | async-start | bytes 8912896 | tf_op jit(solution)/shard_map/all_gather | solution.py:147
  79.9 2.6 copy-start.10
  82.5 43.9 %copy-start.2 = (bf16[128,2048]{1,0:T(8,128)(2,1)S(1)}, bf16[128,2048]{1,0:T(8,128)(2,1)}, u32[]{:S(2)}) copy-start(bf16[128,2048]{1,0:T(8,128)(2,1)} %param.21) | copy-start | bytes 1572868
  126.4 4.8 %copy-start.11 = (f32[2048]{0:T(1024)S(1)}, f32[2048]{0:T(1024)}, u32[]{:S(2)}) copy-start(f32[2048]{0:T(1024)} %param.28) | copy-start | bytes 24580
  126.4 5.9 %copy-start.8 = (f32[2048,6]{0,1:T(8,128)S(1)}, f32[2048,6]{0,1:T(8,128)}, u32[]{:S(2)}) copy-start(f32[2048,6]{0,1:T(8,128)} %param.36) | copy-start | bytes 147460
  126.4 5.9 %copy-start.9 = (s32[2048,6]{0,1:T(8,128)S(1)}, s32[2048,6]{0,1:T(8,128)}, u32[]{:S(2)}) copy-start(s32[2048,6]{0,1:T(8,128)} %param.35) | copy-start | bytes 147460
  184.7 14.2 %slice-start.2 = ((s8[5767168]{0:T(1024)(128)(4,1)}), s8[4194304]{0:T(1024)(128)(4,1)S(1)}, s32[]{:S(2)}) async-start(s8[5767168]{0:T(1024)(128)(4,1)} %bitcast.203), calls=%async_computation.6 | async-start | bytes 8388608
  189.5 9.4 %slice-start.3 = ((s8[5767168]{0:T(1024)(128)(4,1)}), s8[1572864]{0:T(1024)(128)(4,1)S(1)}, s32[]{:S(2)}) async-start(s8[5767168]{0:T(1024)(128)(4,1)} %bitcast.203), calls=%async_computation.7 | async-start | bytes 3145728
  189.5 16.5 %slice-start.4 = ((s8[5767168]{0:T(1024)(128)(4,1)}), s8[4194304]{0:T(1024)(128)(4,1)S(1)}, s32[]{:S(2)}) async-start(s8[5767168]{0:T(1024)(128)(4,1)} %bitcast.205), calls=%async_computation.8 | async-start | bytes 8388608
  198.9 7.1 %slice-start.5 = ((s8[5767168]{0:T(1024)(128)(4,1)}), s8[1572864]{0:T(1024)(128)(4,1)S(1)}, s32[]{:S(2)}) async-start(s8[5767168]{0:T(1024)(128)(4,1)} %bitcast.205), calls=%async_computation.9 | async-start | bytes 3145728
  206.0 7.3 %slice-start = ((s8[8388608]{0:T(1024)(128)(4,1)}), s8[4194304]{0:T(1024)(128)(4,1)S(1)}, s32[]{:S(2)}) async-start(s8[8388608]{0:T(1024)(128)(4,1)} %bitcast.183), calls=%async_computation.4 | async-start | bytes 8388608
  208.6 4.7 %slice-start.1 = ((s8[8388608]{0:T(1024)(128)(4,1)}), s8[4194304]{0:T(1024)(128)(4,1)S(1)}, s32[]{:S(2)}) async-start(s8[8388608]{0:T(1024)(128)(4,1)} %bitcast.183), calls=%async_computation.5 | async-start | bytes 8388608
  208.7 4.7 %copy-start.12 = (bf16[2048,176]{0,1:T(8,128)(2,1)S(1)}, bf16[2048,176]{0,1:T(8,128)(2,1)}, u32[]{:S(2)}) copy-start(bf16[2048,176]{0,1:T(8,128)(2,1)} %param.30) | copy-start | bytes 2162692
  208.7 4.7 %copy-start.13 = (bf16[2048,176]{0,1:T(8,128)(2,1)S(1)}, bf16[2048,176]{0,1:T(8,128)(2,1)}, u32[]{:S(2)}) copy-start(bf16[2048,176]{0,1:T(8,128)(2,1)} %param.29) | copy-start | bytes 2162692
  217.0 1.1 copy-start.14
  219.4 2.2 copy-start.5
  220.7 8.7 %collective-permute-start.8 = (bf16[4,2,128,768]{3,2,1,0:T(8,128)(2,1)}, bf16[4,2,128,768]{3,2,1,0:T(8,128)(2,1)S(1)}, u32[]{:S(2)}, u32[]{:S(2)}) collective-permute-start(bf16[4,2,128,768]{3,2,1,0:T(8,128)(2,1)} %dynamic-slice_bitcast_fusion.1), channel_id=1, source_target_pairs={{0,1},{1,0},{2,3},{3,2},{4,5},{5,4},{6,7},{7,6},{8,9},{9,8},{10,11... | collective-permute-start | bytes 4718600 | tf_op jit(solution)/shard_map/ppermute | solution.py:68
  225.1 2.3 copy-start.1
  229.2 25.1 %collective-permute-start = (bf16[4,2,128,1280]{3,2,1,0:T(8,128)(2,1)}, bf16[4,2,128,1280]{3,2,1,0:T(8,128)(2,1)}, u32[]{:S(2)}, u32[]{:S(2)}) collective-permute-start(bf16[4,2,128,1280]{3,2,1,0:T(8,128)(2,1)} %dynamic-slice_bitcast_fusion), channel_id=1, source_target_pairs={{0,1},{1,0},{2,3},{3,2},{4,5},{5,4},{6,7},{7,6},{8,9},{9,8},{10,11... | collective-permute-start | bytes 7864328 | tf_op jit(solution)/shard_map/ppermute | solution.py:68
  231.2 3.0 copy-start.15
  231.4 1.2 copy-start
  232.6 8.3 %collective-permute-start.9 = (bf16[2,128,384]{2,1,0:T(8,128)(2,1)S(1)}, bf16[2,128,384]{2,1,0:T(8,128)(2,1)S(1)}, u32[]{:S(2)}, u32[]{:S(2)}) collective-permute-start(bf16[2,128,384]{2,1,0:T(8,128)(2,1)S(1)} %fusion.86), channel_id=1, source_target_pairs={{0,4},{1,5},{2,6},{3,7},{4,8},{5,9},{6,10},{7,11},{8,12},{9,13},{1... | collective-permute-start | bytes 589832 | tf_op jit(solution)/shard_map/ppermute | solution.py:80
  234.2 8.1 %collective-permute-start.12 = (bf16[2,128,384]{2,1,0:T(8,128)(2,1)S(1)}, bf16[2,128,384]{2,1,0:T(8,128)(2,1)S(1)}, u32[]{:S(2)}, u32[]{:S(2)}) collective-permute-start(bf16[2,128,384]{2,1,0:T(8,128)(2,1)S(1)} %fusion.87), channel_id=1, source_target_pairs={{0,12},{1,13},{2,14},{3,15},{4,0},{5,1},{6,2},{7,3},{8,4},{9,5},{1... | collective-permute-start | bytes 589832 | tf_op jit(solution)/shard_map/ppermute | solution.py:81
  242.0 7.5 %collective-permute-start.10 = (bf16[2,128,384]{2,1,0:T(8,128)(2,1)S(1)}, bf16[2,128,384]{2,1,0:T(8,128)(2,1)S(1)}, u32[]{:S(2)}, u32[]{:S(2)}) collective-permute-start(bf16[2,128,384]{2,1,0:T(8,128)(2,1)S(1)} %fusion.75), channel_id=1, source_target_pairs={{0,4},{1,5},{2,6},{3,7},{4,8},{5,9},{6,10},{7,11},{8,12},{9,13},{1... | collective-permute-start | bytes 589832 | tf_op jit(solution)/shard_map/ppermute | solution.py:80
  242.4 8.2 %collective-permute-start.13 = (bf16[2,128,384]{2,1,0:T(8,128)(2,1)S(1)}, bf16[2,128,384]{2,1,0:T(8,128)(2,1)S(1)}, u32[]{:S(2)}, u32[]{:S(2)}) collective-permute-start(bf16[2,128,384]{2,1,0:T(8,128)(2,1)S(1)} %fusion.73), channel_id=1, source_target_pairs={{0,12},{1,13},{2,14},{3,15},{4,0},{5,1},{6,2},{7,3},{8,4},{9,5},{1... | collective-permute-start | bytes 589832 | tf_op jit(solution)/shard_map/ppermute | solution.py:81
  250.5 10.8 %collective-permute-start.11 = (bf16[2,128,384]{2,1,0:T(8,128)(2,1)S(1)}, bf16[2,128,384]{2,1,0:T(8,128)(2,1)S(1)}, u32[]{:S(2)}, u32[]{:S(2)}) collective-permute-start(bf16[2,128,384]{2,1,0:T(8,128)(2,1)S(1)} %fusion.74), channel_id=1, source_target_pairs={{0,4},{1,5},{2,6},{3,7},{4,8},{5,9},{6,10},{7,11},{8,12},{9,13},{1... | collective-permute-start | bytes 589832 | tf_op jit(solution)/shard_map/ppermute | solution.py:80
  250.7 19.7 %collective-permute-start.14 = (bf16[2,128,384]{2,1,0:T(8,128)(2,1)S(1)}, bf16[2,128,384]{2,1,0:T(8,128)(2,1)S(1)}, u32[]{:S(2)}, u32[]{:S(2)}) collective-permute-start(bf16[2,128,384]{2,1,0:T(8,128)(2,1)S(1)} %fusion.72), channel_id=1, source_target_pairs={{0,12},{1,13},{2,14},{3,15},{4,0},{5,1},{6,2},{7,3},{8,4},{9,5},{1... | collective-permute-start | bytes 589832 | tf_op jit(solution)/shard_map/ppermute | solution.py:81
  258.0 8.8 %collective-permute-start.1 = (bf16[2,128,640]{2,1,0:T(8,128)(2,1)S(1)}, bf16[2,128,640]{2,1,0:T(8,128)(2,1)S(1)}, u32[]{:S(2)}, u32[]{:S(2)}) collective-permute-start(bf16[2,128,640]{2,1,0:T(8,128)(2,1)S(1)} %fusion.76), channel_id=1, source_target_pairs={{0,4},{1,5},{2,6},{3,7},{4,8},{5,9},{6,10},{7,11},{8,12},{9,13},{1... | collective-permute-start | bytes 983048 | tf_op jit(solution)/shard_map/ppermute | solution.py:80
  258.1 8.9 %collective-permute-start.4 = (bf16[2,128,640]{2,1,0:T(8,128)(2,1)S(1)}, bf16[2,128,640]{2,1,0:T(8,128)(2,1)S(1)}, u32[]{:S(2)}, u32[]{:S(2)}) collective-permute-start(bf16[2,128,640]{2,1,0:T(8,128)(2,1)S(1)} %fusion.77), channel_id=1, source_target_pairs={{0,12},{1,13},{2,14},{3,15},{4,0},{5,1},{6,2},{7,3},{8,4},{9,5},{1... | collective-permute-start | bytes 983048 | tf_op jit(solution)/shard_map/ppermute | solution.py:81
  262.4 17.4 %copy-start.3 = (f32[2,128,384]{2,1,0:T(8,128)}, f32[2,128,384]{2,1,0:T(8,128)S(1)}, u32[]{:S(2)}) copy-start(f32[2,128,384]{2,1,0:T(8,128)S(1)} %bitcast_add_fusion.9) | copy-start | bytes 1179652
  266.9 8.5 %collective-permute-start.2 = (bf16[2,128,640]{2,1,0:T(8,128)(2,1)S(1)}, bf16[2,128,640]{2,1,0:T(8,128)(2,1)S(1)}, u32[]{:S(2)}, u32[]{:S(2)}) collective-permute-start(bf16[2,128,640]{2,1,0:T(8,128)(2,1)S(1)} %fusion.61), channel_id=1, source_target_pairs={{0,4},{1,5},{2,6},{3,7},{4,8},{5,9},{6,10},{7,11},{8,12},{9,13},{1... | collective-permute-start | bytes 983048 | tf_op jit(solution)/shard_map/ppermute | solution.py:80
  267.1 8.5 %collective-permute-start.5 = (bf16[2,128,640]{2,1,0:T(8,128)(2,1)S(1)}, bf16[2,128,640]{2,1,0:T(8,128)(2,1)S(1)}, u32[]{:S(2)}, u32[]{:S(2)}) collective-permute-start(bf16[2,128,640]{2,1,0:T(8,128)(2,1)S(1)} %fusion.59), channel_id=1, source_target_pairs={{0,12},{1,13},{2,14},{3,15},{4,0},{5,1},{6,2},{7,3},{8,4},{9,5},{1... | collective-permute-start | bytes 983048 | tf_op jit(solution)/shard_map/ppermute | solution.py:81
  270.4 13.6 %copy-start.4 = (f32[2,128,384]{2,1,0:T(8,128)}, f32[2,128,384]{2,1,0:T(8,128)S(1)}, u32[]{:S(2)}) copy-start(f32[2,128,384]{2,1,0:T(8,128)S(1)} %bitcast_add_fusion.6) | copy-start | bytes 1179652
  275.4 8.4 %collective-permute-start.3 = (bf16[2,128,640]{2,1,0:T(8,128)(2,1)S(1)}, bf16[2,128,640]{2,1,0:T(8,128)(2,1)S(1)}, u32[]{:S(2)}, u32[]{:S(2)}) collective-permute-start(bf16[2,128,640]{2,1,0:T(8,128)(2,1)S(1)} %fusion.60), channel_id=1, source_target_pairs={{0,4},{1,5},{2,6},{3,7},{4,8},{5,9},{6,10},{7,11},{8,12},{9,13},{1... | collective-permute-start | bytes 983048 | tf_op jit(solution)/shard_map/ppermute | solution.py:80
  275.6 10.6 %copy-start.6 = (bf16[2048,128]{1,0:T(8,128)(2,1)S(1)}, bf16[2048,128]{1,0:T(8,128)(2,1)}, u32[]{:S(2)}) copy-start(bf16[2048,128]{1,0:T(8,128)(2,1)} %get-tuple-element.114) | copy-start | bytes 1572868
  275.6 10.5 %copy-start.7 = (bf16[2048,128]{1,0:T(8,128)(2,1)S(1)}, bf16[2048,128]{1,0:T(8,128)(2,1)}, u32[]{:S(2)}) copy-start(bf16[2048,128]{1,0:T(8,128)(2,1)} %get-tuple-element.117) | copy-start | bytes 1572868
  275.6 8.2 %collective-permute-start.6 = (bf16[2,128,640]{2,1,0:T(8,128)(2,1)S(1)}, bf16[2,128,640]{2,1,0:T(8,128)(2,1)S(1)}, u32[]{:S(2)}, u32[]{:S(2)}) collective-permute-start(bf16[2,128,640]{2,1,0:T(8,128)(2,1)S(1)} %fusion.58), channel_id=1, source_target_pairs={{0,12},{1,13},{2,14},{3,15},{4,0},{5,1},{6,2},{7,3},{8,4},{9,5},{1... | collective-permute-start | bytes 983048 | tf_op jit(solution)/shard_map/ppermute | solution.py:81
  279.9 10.6 %collective-permute-start.15 = (bf16[128,768]{1,0:T(8,128)(2,1)}, bf16[128,768]{1,0:T(8,128)(2,1)}, u32[]{:S(2)}, u32[]{:S(2)}) collective-permute-start(bf16[128,768]{1,0:T(8,128)(2,1)} %fusion.88), channel_id=1, source_target_pairs={{0,2},{1,3},{2,0},{3,1},{4,6},{5,7},{6,4},{7,5},{8,10},{9,11},{10,... | collective-permute-start | bytes 589832 | tf_op jit(solution)/shard_map/ppermute | solution.py:96
  284.7 7.4 %collective-permute-start.7 = (bf16[128,1280]{1,0:T(8,128)(2,1)}, bf16[128,1280]{1,0:T(8,128)(2,1)}, u32[]{:S(2)}, u32[]{:S(2)}) collective-permute-start(bf16[128,1280]{1,0:T(8,128)(2,1)} %fusion.78), channel_id=1, source_target_pairs={{0,2},{1,3},{2,0},{3,1},{4,6},{5,7},{6,4},{7,5},{8,10},{9,11},{10,... | collective-permute-start | bytes 983048 | tf_op jit(solution)/shard_map/ppermute | solution.py:96
Sparse Core Ops, SparseCore 0:
  10.6 54.5 all-gather.3
  66.9 58.6 all-gather.5
  132.4 52.2 all-gather.7

commit v8 on v7

--- a/solution.py
+++ b/solution.py
@@ -143,7 +143,7 @@
     attention = jnp.dot(context_rows, out_weight_all, preferred_element_type=jnp.float32)
     residual = (tokens.astype(jnp.float32) + attention).astype(jnp.bfloat16)
     normed_ffn = rms_scale(residual, ffn_gain)
-    piece_edges = [0, model_width * 5 // 8, model_width]
+    piece_edges = [0, model_width * 3 // 8, model_width]
     normed_stream = lax.all_gather(normed_ffn, "tensor", axis=0, tiled=True)
 
     local_experts = expert_gate.shape[0]

time: 302 us -> 302 us (level)
  no operation moved by 1% of the time
where the time goes in v8:
time: 302 us; the launch traced here: 300 us
  waiting for transfers between devices  126 us (42%)
  matrix products  65.7 us (22%)
  other arithmetic  25.2 us (8%)
  starting transfers between devices  24.2 us (8%)
  blocking collectives  18.9 us (6%)
  local copies, waits for them, and re-layouts  18.1 us (6%)
  between operations  14.4 us (5%)
  loops' own time  7.7 us (3%)
    all_gather x1, waiting for transfers between devices, shards(): lax.all_gather(rms_scale(tokens, attention_gain), 'tensor', axis=0, tiled...  52.3 us
    all_gather x1, waiting for transfers between devices, shards(): normed_stream = lax.all_gather(normed_ffn, 'tensor', axis=0, tiled=True)  52 us
    ppermute x6, waiting for transfers between devices, ring_reduce_scatter(): recv_f = lax.ppermute(carry_f, 'tensor', forward_pairs)  20.6 us
    all_to_all x1, blocking collectives, shards(): lax.all_to_all(context.reshape(groups, tok_dev, inner), 'tensor', split_a...  18.9 us
    ppermute x6, starting transfers between devices, ring_reduce_scatter(): recv_b = lax.ppermute(carry_b, 'tensor', backward_pairs)  18.5 us
    dot_general x4, matrix products, shards(): jnp.dot(rows, projection, preferred_element_type=jnp.float32)  14.7 us
    dot_general x1, matrix products, shards(): jnp.dot(picked, expert_gate[local], preferred_element_type=jnp.float32)  9.36 us
    another operation x1, loops' own time, attend(): context = lax.map(one_block, starts).reshape(total_tokens, inner)  7.7 us
  transfers between devices with their start and end apart: 19, of which 8 were waited for; matrix products, arithmetic and copies ran while one was open for 19% of the time, Pallas kernels for 0%

profile of v8, /device:TPU:0, one launch (start us, length us, event | category | flops | bytes accessed | tf_op | source)
XLA Modules:
  0.0 300.4 jit_solution(4785191260126668803)
XLA Ops:
  7.2 1.2 fusion.49
  8.4 2.0 fusion.51
  11.3 1.6 pad_maximum_fusion
  12.9 52.3 %all-gather.4.cloned.1.call-done = bf16[2048,2048]{1,0:T(8,128)(2,1)} async-done(((bf16[128,2048]{1,0:T(8,128)(2,1)}), bf16[2048,2048]{1,0:T(8,128)(2,1)}) %all-gather.4.cloned.1.call-update) | async-done | bytes 8388624 | tf_op jit(solution)/shard_map/all_gather | solution.py:127
  65.2 14.7 %while.21 = (s32[]{:T(128)}, bf16[4,512,384]{2,1,0:T(8,128)(2,1)}, bf16[4,512,2048]{2,1,0:T(8,128)(2,1)}, bf16[2048,384]{1,0:T(8,128)(2,1)S(1)}, s32[]{:T(128)}) while((s32[]{:T(128)}, bf16[4,512,384]{2,1,0:T(8,128)(2,1)}, bf16[4,512,2048]{2,1,0:T(8,128)(2,1)}, bf16[2048,384]{1,0:T(8,128)(2,1)S(1)}, s32[]{:T(128)}) %tuple.62), condition=%wide.region_2.3_spmd, body=%wide.region_1.2_spmd.sunk | while | flops 805502976 | bytes 4064325 | solution.py:129
  65.2 3.6 %fusion.116 = bf16[4,512,384]{2,1,0:T(8,128)(2,1)} fusion(bf16[4,512,384]{2,1,0:T(8,128)(2,1)} %get-tuple-element.199, s32[]{:T(128)S(6)} %copy.34, bf16[2048,384]{1,0:T(8,128)(2,1)S(1)} %get-tuple-element.206, bf16[4,512,2048]{2,1,0:T(8,128)(2,1)} %get-tuple-element.205), kind=kOutput, calls=%fused_computation.7.clone.1 | convolution fusion | flops 805502976 | bytes 4064256 | tf_op jit(solution)/shard_map/while/body/eval_jaxpr/dot_general | solution.py:130
  68.8 3.6 %fusion.116 = bf16[4,512,384]{2,1,0:T(8,128)(2,1)} fusion(bf16[4,512,384]{2,1,0:T(8,128)(2,1)} %get-tuple-element.199, s32[]{:T(128)S(6)} %copy.34, bf16[2048,384]{1,0:T(8,128)(2,1)S(1)} %get-tuple-element.206, bf16[4,512,2048]{2,1,0:T(8,128)(2,1)} %get-tuple-element.205), kind=kOutput, calls=%fused_computation.7.clone.1 | convolution fusion | flops 805502976 | bytes 4064256 | tf_op jit(solution)/shard_map/while/body/eval_jaxpr/dot_general | solution.py:130
  72.4 3.6 %fusion.116 = bf16[4,512,384]{2,1,0:T(8,128)(2,1)} fusion(bf16[4,512,384]{2,1,0:T(8,128)(2,1)} %get-tuple-element.199, s32[]{:T(128)S(6)} %copy.34, bf16[2048,384]{1,0:T(8,128)(2,1)S(1)} %get-tuple-element.206, bf16[4,512,2048]{2,1,0:T(8,128)(2,1)} %get-tuple-element.205), kind=kOutput, calls=%fused_computation.7.clone.1 | convolution fusion | flops 805502976 | bytes 4064256 | tf_op jit(solution)/shard_map/while/body/eval_jaxpr/dot_general | solution.py:130
  76.0 3.9 %fusion.116 = bf16[4,512,384]{2,1,0:T(8,128)(2,1)} fusion(bf16[4,512,384]{2,1,0:T(8,128)(2,1)} %get-tuple-element.199, s32[]{:T(128)S(6)} %copy.34, bf16[2048,384]{1,0:T(8,128)(2,1)S(1)} %get-tuple-element.206, bf16[4,512,2048]{2,1,0:T(8,128)(2,1)} %get-tuple-element.205), kind=kOutput, calls=%fused_computation.7.clone.1 | convolution fusion | flops 805502976 | bytes 4064256 | tf_op jit(solution)/shard_map/while/body/eval_jaxpr/dot_general | solution.py:130
  79.9 2.6 fusion.93
  82.5 24.6 %while.22 = (s32[]{:T(128)}, bf16[4,512,1,128]{3,1,2,0:T(8,128)(2,1)S(1)}, s32[4]{0:T(128)S(1)}, s32[2048]{0:T(1024)S(1)}, bf16[2048,1,128]{2,0,1:T(8,128)(2,1)S...) while((s32[]{:T(128)}, ...), condition=%wide.region_6.7_spmd.clone, body=%wide.region_3.6_spmd.clone.sunk | while | flops 548470272 | bytes 13922475 | solution.py:45
  85.8 1.3 fusion.118
  87.0 0.7 fusion.119
  87.7 0.9 fusion.120
  91.9 1.3 fusion.118
  93.9 0.9 fusion.120
  98.1 1.3 fusion.118
  99.3 0.7 fusion.119
  100.0 0.9 fusion.120
  104.2 1.3 fusion.118
  106.2 0.9 fusion.120
  107.2 18.9 %all_to_all.5 = bf16[16,128,128]{2,1,0:T(8,128)(2,1)S(1)} all-to-all(bf16[16,128,128]{2,1,0:T(8,128)(2,1)S(1)} %bitcast.200), channel_id=1, replica_groups=mesh['dp'=8,'tensor'=16] {'tensor'}, dimensions={0} | all-to-all | bytes 1048576 | tf_op jit(solution)/shard_map/all_to_all | solution.py:139
  126.4 4.8 %multiply_reduce_fusion = (f32[128]{0:T(128)S(1)}, f32[128,2048]{1,0:T(8,128)S(1)}) fusion(bf16[128,2048]{0,1:T(8,128)(2,1)S(1)} %bitcast.190, bf16[2048,2048]{1,0:T(8,128)(2,1)} %all-gather.6.cloned.1.call-done, bf16[128,2048]{1,0:T(8,128)(2,1)S(1)} %copy-done.2), kind=kOutput, calls=%fused_computation.71 | convolution fusion | flops 1075314560 | bytes 10486272 | tf_op jit(solution)/shard_map/dot_general | solution.py:143
  131.2 1.0 multiply_convert_fusion.1
  132.7 52.0 %all-gather.8.cloned.1.call-done = bf16[2048,2048]{1,0:T(8,128)(2,1)} async-done(((bf16[128,2048]{1,0:T(8,128)(2,1)}), bf16[2048,2048]{1,0:T(8,128)(2,1)}) %all-gather.8.cloned.1.call-update) | async-done | bytes 8388624 | tf_op jit(solution)/shard_map/all_gather | solution.py:147
  184.7 4.8 %convolution_convert_fusion.1 = bf16[16,64,2048]{2,1,0:T(8,128)(2,1)S(1)} fusion(bf16[16,128,2048]{2,1,0:T(8,128)(2,1)} %bitcast.182, s32[16,128]{1,0:T(8,128)S(1)} %bitcast_subtract_fusion, pred[16,128]{1,0:T(8,128)(4,1)S(1)} %broadcast_compare_fusion.1), kind=kOutput, calls=%fused_computation.38 | convolution fusion | flops 539230208 | bytes 12593152 | tf_op jit(solution)/shard_map/bst,btd->bsd/dot_general | solution.py:176
  189.5 9.4 %fusion.32 = f32[1024,1408]{1,0:T(8,128)S(1)} fusion(bf16[1024,2048]{1,0:T(8,128)(2,1)S(1)} %bitcast.185, bf16[1,2048,1408]{2,1,0:T(8,128)(2,1)} %param.32), kind=kOutput, calls=%fused_computation.33 | convolution fusion | flops 5905580032 | bytes 15728640 | tf_op jit(solution)/shard_map/dot_general | solution.py:180
  198.9 7.1 %multiply_convert_fusion = bf16[1024,1408]{1,0:T(8,128)(2,1)S(1)} fusion(f32[1024,1408]{1,0:T(8,128)S(1)} %fusion.32, bf16[1024,2048]{1,0:T(8,128)(2,1)S(1)} %bitcast.186, bf16[1,2048,1408]{2,1,0:T(8,128)(2,1)S(1)} %bitcast.204), kind=kOutput, calls=%fused_computation.35 | convolution fusion | flops 5914230784 | bytes 18612224 | tf_op jit(solution)/shard_map/dot_general | solution.py:182
  206.0 2.6 fusion.41
  208.7 4.7 %convolution_convert_fusion.2 = bf16[1024,1280]{1,0:T(8,128)(2,1)S(1)} fusion(bf16[1024,1408]{1,0:T(8,128)(2,1)S(1)} %multiply_convert_fusion, bf16[1408,2048]{1,0:T(8,128)(2,1)S(1)} %bitcast.208), kind=kOutput, calls=%fused_computation.39 | convolution fusion | flops 3692298240 | bytes 9109504 | tf_op jit(solution)/shard_map/dot_general | solution.py:197
  213.4 3.2 %fusion.45 = f32[2048,352]{0,1:T(8,128)S(1)} fusion(bf16[2048,2048]{1,0:T(8,128)(2,1)S(1)} %bitcast.184, bf16[2048,176]{0,1:T(8,128)(2,1)S(1)} %copy-done.12, bf16[2048,176]{0,1:T(8,128)(2,1)S(1)} %copy-done.13), kind=kOutput, calls=%fused_computation.60 | convolution fusion | flops 2955673600 | bytes 12713984 | tf_op jit(solution)/shard_map/dot_general | solution.py:171
  217.0 1.0 convolution_convert_fusion.3
  218.1 1.2 fusion.29
  219.4 1.4 dynamic-slice_bitcast_fusion.1
  221.5 1.6 convolution_convert_fusion
  223.1 2.0 fusion.27
  225.1 2.3 copy-done.1
  227.4 1.8 dynamic-slice_bitcast_fusion
  229.5 1.7 convert_add_fusion.1
  231.5 1.2 copy-done
  232.7 1.6 collective-permute-start.1
  234.2 1.8 collective-permute-start.4
  236.1 4.9 %collective-permute-done.1 = bf16[2,128,384]{2,1,0:T(8,128)(2,1)S(1)} collective-permute-done((bf16[2,128,384]{2,1,0:T(8,128)(2,1)S(1)}, bf16[2,128,384]{2,1,0:T(8,128)(2,1)S(1)}, u32[]{:S(2)}, u32[]{:S(2)}) %collective-permute-start.1) | collective-permute-done | bytes 196640 | tf_op jit(solution)/shard_map/ppermute | solution.py:80
  241.0 1.0 fusion.75
  242.4 3.3 %collective-permute-start.5 = (bf16[2,128,384]{2,1,0:T(8,128)(2,1)S(1)}, bf16[2,128,384]{2,1,0:T(8,128)(2,1)S(1)}, u32[]{:S(2)}, u32[]{:S(2)}) collective-permute-start(bf16[2,128,384]{2,1,0:T(8,128)(2,1)S(1)} %fusion.73), channel_id=1, source_target_pairs={{0,12},{1,13},{2,14},{3,15},{4,0},{5,1},{6,2},{7,3},{8,4},{9,5},{1... | collective-permute-start | bytes 589832 | tf_op jit(solution)/shard_map/ppermute | solution.py:81
  245.7 3.8 %collective-permute-done.2 = bf16[2,128,384]{2,1,0:T(8,128)(2,1)S(1)} collective-permute-done((bf16[2,128,384]{2,1,0:T(8,128)(2,1)S(1)}, bf16[2,128,384]{2,1,0:T(8,128)(2,1)S(1)}, u32[]{:S(2)}, u32[]{:S(2)}) %collective-permute-start.2) | collective-permute-done | bytes 196640 | tf_op jit(solution)/shard_map/ppermute | solution.py:80
  249.5 1.0 fusion.74
  250.7 3.3 %collective-permute-start.6 = (bf16[2,128,384]{2,1,0:T(8,128)(2,1)S(1)}, bf16[2,128,384]{2,1,0:T(8,128)(2,1)S(1)}, u32[]{:S(2)}, u32[]{:S(2)}) collective-permute-start(bf16[2,128,384]{2,1,0:T(8,128)(2,1)S(1)} %fusion.72), channel_id=1, source_target_pairs={{0,12},{1,13},{2,14},{3,15},{4,0},{5,1},{6,2},{7,3},{8,4},{9,5},{1... | collective-permute-start | bytes 589832 | tf_op jit(solution)/shard_map/ppermute | solution.py:81
  254.0 3.1 %convert_add_fusion = f32[4,2,128,1280]{3,2,1,0:T(8,128)S(1)} fusion(bf16[4,2,128,1280]{3,2,1,0:T(8,128)(2,1)} %collective-permute-done.8, bf16[4,2,2,128,1280]{4,3,2,1,0:T(8,128)(2,1)} %bitcast.189, s32[]{:T(128)S(6)} %select_n.137), kind=kLoop, calls=%fused_computation.37 | loop fusion | flops 3932160 | bytes 10485764 | tf_op jit(solution)/shard_map/add | solution.py:69
  257.9 3.3 %collective-permute-start.12 = (bf16[2,128,640]{2,1,0:T(8,128)(2,1)S(1)}, bf16[2,128,640]{2,1,0:T(8,128)(2,1)S(1)}, u32[]{:S(2)}, u32[]{:S(2)}) collective-permute-start(bf16[2,128,640]{2,1,0:T(8,128)(2,1)S(1)} %fusion.77), channel_id=1, source_target_pairs={{0,12},{1,13},{2,14},{3,15},{4,0},{5,1},{6,2},{7,3},{8,4},{9,5},{1... | collective-permute-start | bytes 983048 | tf_op jit(solution)/shard_map/ppermute | solution.py:81
  261.2 1.0 bitcast_add_fusion.9
  262.2 4.4 %collective-permute-done.9 = bf16[2,128,640]{2,1,0:T(8,128)(2,1)S(1)} collective-permute-done((bf16[2,128,640]{2,1,0:T(8,128)(2,1)S(1)}, bf16[2,128,640]{2,1,0:T(8,128)(2,1)S(1)}, u32[]{:S(2)}, u32[]{:S(2)}) %collective-permute-start.9) | collective-permute-done | bytes 327712 | tf_op jit(solution)/shard_map/ppermute | solution.py:80
  266.8 3.3 %collective-permute-start.13 = (bf16[2,128,640]{2,1,0:T(8,128)(2,1)S(1)}, bf16[2,128,640]{2,1,0:T(8,128)(2,1)S(1)}, u32[]{:S(2)}, u32[]{:S(2)}) collective-permute-start(bf16[2,128,640]{2,1,0:T(8,128)(2,1)S(1)} %fusion.59), channel_id=1, source_target_pairs={{0,12},{1,13},{2,14},{3,15},{4,0},{5,1},{6,2},{7,3},{8,4},{9,5},{1... | collective-permute-start | bytes 983048 | tf_op jit(solution)/shard_map/ppermute | solution.py:81
  270.2 5.0 %collective-permute-done.10 = bf16[2,128,640]{2,1,0:T(8,128)(2,1)S(1)} collective-permute-done((bf16[2,128,640]{2,1,0:T(8,128)(2,1)S(1)}, bf16[2,128,640]{2,1,0:T(8,128)(2,1)S(1)}, u32[]{:S(2)}, u32[]{:S(2)}) %collective-permute-start.10) | collective-permute-done | bytes 327712 | tf_op jit(solution)/shard_map/ppermute | solution.py:80
  275.4 3.5 %collective-permute-start.14 = (bf16[2,128,640]{2,1,0:T(8,128)(2,1)S(1)}, bf16[2,128,640]{2,1,0:T(8,128)(2,1)S(1)}, u32[]{:S(2)}, u32[]{:S(2)}) collective-permute-start(bf16[2,128,640]{2,1,0:T(8,128)(2,1)S(1)} %fusion.58), channel_id=1, source_target_pairs={{0,12},{1,13},{2,14},{3,15},{4,0},{5,1},{6,2},{7,3},{8,4},{9,5},{1... | collective-permute-start | bytes 983048 | tf_op jit(solution)/shard_map/ppermute | solution.py:81
  279.6 1.4 collective-permute-start.7
  281.1 2.5 collective-permute-done.11
  283.7 0.8 fusion.78
  284.5 1.4 collective-permute-start.15
  286.0 1.2 broadcast_in_dim.45
  287.3 3.0 scatter_fusion
  290.2 1.1 fusion.71
  291.9 1.0 fusion.57
  292.9 0.9 fusion.52
  (114 shorter events, 13.4 us)
Async XLA Ops:
  7.2 58.1 %all-gather.4.cloned.1.call-start = ((), (), s32[]{:S(2)}) async-start(), calls=%async_computation.1 | async-start | bytes 8912896 | tf_op jit(solution)/shard_map/all_gather | solution.py:127
  10.5 115.9 %all-gather.6.cloned.1.call-start = ((), (), s32[]{:S(2)}) async-start(), calls=%async_computation.2 | async-start | bytes 8912896 | tf_op jit(solution)/shard_map/all_gather | solution.py:128
  11.3 173.4 %all-gather.8.cloned.1.call-start = ((), (), s32[]{:S(2)}) async-start(), calls=%async_computation.3 | async-start | bytes 8912896 | tf_op jit(solution)/shard_map/all_gather | solution.py:147
  79.9 2.6 copy-start.10
  82.5 43.9 %copy-start.2 = (bf16[128,2048]{1,0:T(8,128)(2,1)S(1)}, bf16[128,2048]{1,0:T(8,128)(2,1)}, u32[]{:S(2)}) copy-start(bf16[128,2048]{1,0:T(8,128)(2,1)} %param.21) | copy-start | bytes 1572868
  126.4 4.8 %copy-start.11 = (f32[2048]{0:T(1024)S(1)}, f32[2048]{0:T(1024)}, u32[]{:S(2)}) copy-start(f32[2048]{0:T(1024)} %param.28) | copy-start | bytes 24580
  126.4 5.9 %copy-start.8 = (f32[2048,6]{0,1:T(8,128)S(1)}, f32[2048,6]{0,1:T(8,128)}, u32[]{:S(2)}) copy-start(f32[2048,6]{0,1:T(8,128)} %param.36) | copy-start | bytes 147460
  126.4 5.9 %copy-start.9 = (s32[2048,6]{0,1:T(8,128)S(1)}, s32[2048,6]{0,1:T(8,128)}, u32[]{:S(2)}) copy-start(s32[2048,6]{0,1:T(8,128)} %param.35) | copy-start | bytes 147460
  184.7 14.2 %slice-start.2 = ((s8[5767168]{0:T(1024)(128)(4,1)}), s8[4194304]{0:T(1024)(128)(4,1)S(1)}, s32[]{:S(2)}) async-start(s8[5767168]{0:T(1024)(128)(4,1)} %bitcast.203), calls=%async_computation.6 | async-start | bytes 8388608
  189.5 9.4 %slice-start.3 = ((s8[5767168]{0:T(1024)(128)(4,1)}), s8[1572864]{0:T(1024)(128)(4,1)S(1)}, s32[]{:S(2)}) async-start(s8[5767168]{0:T(1024)(128)(4,1)} %bitcast.203), calls=%async_computation.7 | async-start | bytes 3145728
  189.5 16.5 %slice-start.4 = ((s8[5767168]{0:T(1024)(128)(4,1)}), s8[4194304]{0:T(1024)(128)(4,1)S(1)}, s32[]{:S(2)}) async-start(s8[5767168]{0:T(1024)(128)(4,1)} %bitcast.205), calls=%async_computation.8 | async-start | bytes 8388608
  198.9 7.1 %slice-start.5 = ((s8[5767168]{0:T(1024)(128)(4,1)}), s8[1572864]{0:T(1024)(128)(4,1)S(1)}, s32[]{:S(2)}) async-start(s8[5767168]{0:T(1024)(128)(4,1)} %bitcast.205), calls=%async_computation.9 | async-start | bytes 3145728
  206.0 7.3 %slice-start = ((s8[8388608]{0:T(1024)(128)(4,1)}), s8[4194304]{0:T(1024)(128)(4,1)S(1)}, s32[]{:S(2)}) async-start(s8[8388608]{0:T(1024)(128)(4,1)} %bitcast.183), calls=%async_computation.4 | async-start | bytes 8388608
  208.6 4.7 %slice-start.1 = ((s8[8388608]{0:T(1024)(128)(4,1)}), s8[4194304]{0:T(1024)(128)(4,1)S(1)}, s32[]{:S(2)}) async-start(s8[8388608]{0:T(1024)(128)(4,1)} %bitcast.183), calls=%async_computation.5 | async-start | bytes 8388608
  208.7 4.7 %copy-start.12 = (bf16[2048,176]{0,1:T(8,128)(2,1)S(1)}, bf16[2048,176]{0,1:T(8,128)(2,1)}, u32[]{:S(2)}) copy-start(bf16[2048,176]{0,1:T(8,128)(2,1)} %param.30) | copy-start | bytes 2162692
  208.7 4.7 %copy-start.13 = (bf16[2048,176]{0,1:T(8,128)(2,1)S(1)}, bf16[2048,176]{0,1:T(8,128)(2,1)}, u32[]{:S(2)}) copy-start(bf16[2048,176]{0,1:T(8,128)(2,1)} %param.29) | copy-start | bytes 2162692
  217.0 1.1 copy-start.14
  219.4 2.2 copy-start.5
  220.7 8.8 %collective-permute-start = (bf16[4,2,128,768]{3,2,1,0:T(8,128)(2,1)}, bf16[4,2,128,768]{3,2,1,0:T(8,128)(2,1)S(1)}, u32[]{:S(2)}, u32[]{:S(2)}) collective-permute-start(bf16[4,2,128,768]{3,2,1,0:T(8,128)(2,1)} %dynamic-slice_bitcast_fusion.1), channel_id=1, source_target_pairs={{0,1},{1,0},{2,3},{3,2},{4,5},{5,4},{6,7},{7,6},{8,9},{9,8},{10,11... | collective-permute-start | bytes 4718600 | tf_op jit(solution)/shard_map/ppermute | solution.py:68
  225.1 2.3 copy-start.1
  229.2 24.8 %collective-permute-start.8 = (bf16[4,2,128,1280]{3,2,1,0:T(8,128)(2,1)}, bf16[4,2,128,1280]{3,2,1,0:T(8,128)(2,1)}, u32[]{:S(2)}, u32[]{:S(2)}) collective-permute-start(bf16[4,2,128,1280]{3,2,1,0:T(8,128)(2,1)} %dynamic-slice_bitcast_fusion), channel_id=1, source_target_pairs={{0,1},{1,0},{2,3},{3,2},{4,5},{5,4},{6,7},{7,6},{8,9},{9,8},{10,11... | collective-permute-start | bytes 7864328 | tf_op jit(solution)/shard_map/ppermute | solution.py:68
  231.2 3.0 copy-start.15
  231.5 1.2 copy-start
  232.7 8.3 %collective-permute-start.1 = (bf16[2,128,384]{2,1,0:T(8,128)(2,1)S(1)}, bf16[2,128,384]{2,1,0:T(8,128)(2,1)S(1)}, u32[]{:S(2)}, u32[]{:S(2)}) collective-permute-start(bf16[2,128,384]{2,1,0:T(8,128)(2,1)S(1)} %fusion.86), channel_id=1, source_target_pairs={{0,4},{1,5},{2,6},{3,7},{4,8},{5,9},{6,10},{7,11},{8,12},{9,13},{1... | collective-permute-start | bytes 589832 | tf_op jit(solution)/shard_map/ppermute | solution.py:80
  234.2 8.1 %collective-permute-start.4 = (bf16[2,128,384]{2,1,0:T(8,128)(2,1)S(1)}, bf16[2,128,384]{2,1,0:T(8,128)(2,1)S(1)}, u32[]{:S(2)}, u32[]{:S(2)}) collective-permute-start(bf16[2,128,384]{2,1,0:T(8,128)(2,1)S(1)} %fusion.87), channel_id=1, source_target_pairs={{0,12},{1,13},{2,14},{3,15},{4,0},{5,1},{6,2},{7,3},{8,4},{9,5},{1... | collective-permute-start | bytes 589832 | tf_op jit(solution)/shard_map/ppermute | solution.py:81
  242.0 7.5 %collective-permute-start.2 = (bf16[2,128,384]{2,1,0:T(8,128)(2,1)S(1)}, bf16[2,128,384]{2,1,0:T(8,128)(2,1)S(1)}, u32[]{:S(2)}, u32[]{:S(2)}) collective-permute-start(bf16[2,128,384]{2,1,0:T(8,128)(2,1)S(1)} %fusion.75), channel_id=1, source_target_pairs={{0,4},{1,5},{2,6},{3,7},{4,8},{5,9},{6,10},{7,11},{8,12},{9,13},{1... | collective-permute-start | bytes 589832 | tf_op jit(solution)/shard_map/ppermute | solution.py:80
  242.4 8.2 %collective-permute-start.5 = (bf16[2,128,384]{2,1,0:T(8,128)(2,1)S(1)}, bf16[2,128,384]{2,1,0:T(8,128)(2,1)S(1)}, u32[]{:S(2)}, u32[]{:S(2)}) collective-permute-start(bf16[2,128,384]{2,1,0:T(8,128)(2,1)S(1)} %fusion.73), channel_id=1, source_target_pairs={{0,12},{1,13},{2,14},{3,15},{4,0},{5,1},{6,2},{7,3},{8,4},{9,5},{1... | collective-permute-start | bytes 589832 | tf_op jit(solution)/shard_map/ppermute | solution.py:81
  250.6 10.6 %collective-permute-start.3 = (bf16[2,128,384]{2,1,0:T(8,128)(2,1)S(1)}, bf16[2,128,384]{2,1,0:T(8,128)(2,1)S(1)}, u32[]{:S(2)}, u32[]{:S(2)}) collective-permute-start(bf16[2,128,384]{2,1,0:T(8,128)(2,1)S(1)} %fusion.74), channel_id=1, source_target_pairs={{0,4},{1,5},{2,6},{3,7},{4,8},{5,9},{6,10},{7,11},{8,12},{9,13},{1... | collective-permute-start | bytes 589832 | tf_op jit(solution)/shard_map/ppermute | solution.py:80
  250.7 19.4 %collective-permute-start.6 = (bf16[2,128,384]{2,1,0:T(8,128)(2,1)S(1)}, bf16[2,128,384]{2,1,0:T(8,128)(2,1)S(1)}, u32[]{:S(2)}, u32[]{:S(2)}) collective-permute-start(bf16[2,128,384]{2,1,0:T(8,128)(2,1)S(1)} %fusion.72), channel_id=1, source_target_pairs={{0,12},{1,13},{2,14},{3,15},{4,0},{5,1},{6,2},{7,3},{8,4},{9,5},{1... | collective-permute-start | bytes 589832 | tf_op jit(solution)/shard_map/ppermute | solution.py:81
  257.8 8.8 %collective-permute-start.9 = (bf16[2,128,640]{2,1,0:T(8,128)(2,1)S(1)}, bf16[2,128,640]{2,1,0:T(8,128)(2,1)S(1)}, u32[]{:S(2)}, u32[]{:S(2)}) collective-permute-start(bf16[2,128,640]{2,1,0:T(8,128)(2,1)S(1)} %fusion.76), channel_id=1, source_target_pairs={{0,4},{1,5},{2,6},{3,7},{4,8},{5,9},{6,10},{7,11},{8,12},{9,13},{1... | collective-permute-start | bytes 983048 | tf_op jit(solution)/shard_map/ppermute | solution.py:80
  257.9 8.9 %collective-permute-start.12 = (bf16[2,128,640]{2,1,0:T(8,128)(2,1)S(1)}, bf16[2,128,640]{2,1,0:T(8,128)(2,1)S(1)}, u32[]{:S(2)}, u32[]{:S(2)}) collective-permute-start(bf16[2,128,640]{2,1,0:T(8,128)(2,1)S(1)} %fusion.77), channel_id=1, source_target_pairs={{0,12},{1,13},{2,14},{3,15},{4,0},{5,1},{6,2},{7,3},{8,4},{9,5},{1... | collective-permute-start | bytes 983048 | tf_op jit(solution)/shard_map/ppermute | solution.py:81
  262.2 17.4 %copy-start.3 = (f32[2,128,384]{2,1,0:T(8,128)}, f32[2,128,384]{2,1,0:T(8,128)S(1)}, u32[]{:S(2)}) copy-start(f32[2,128,384]{2,1,0:T(8,128)S(1)} %bitcast_add_fusion.9) | copy-start | bytes 1179652
  266.7 8.5 %collective-permute-start.10 = (bf16[2,128,640]{2,1,0:T(8,128)(2,1)S(1)}, bf16[2,128,640]{2,1,0:T(8,128)(2,1)S(1)}, u32[]{:S(2)}, u32[]{:S(2)}) collective-permute-start(bf16[2,128,640]{2,1,0:T(8,128)(2,1)S(1)} %fusion.61), channel_id=1, source_target_pairs={{0,4},{1,5},{2,6},{3,7},{4,8},{5,9},{6,10},{7,11},{8,12},{9,13},{1... | collective-permute-start | bytes 983048 | tf_op jit(solution)/shard_map/ppermute | solution.py:80
  266.8 8.5 %collective-permute-start.13 = (bf16[2,128,640]{2,1,0:T(8,128)(2,1)S(1)}, bf16[2,128,640]{2,1,0:T(8,128)(2,1)S(1)}, u32[]{:S(2)}, u32[]{:S(2)}) collective-permute-start(bf16[2,128,640]{2,1,0:T(8,128)(2,1)S(1)} %fusion.59), channel_id=1, source_target_pairs={{0,12},{1,13},{2,14},{3,15},{4,0},{5,1},{6,2},{7,3},{8,4},{9,5},{1... | collective-permute-start | bytes 983048 | tf_op jit(solution)/shard_map/ppermute | solution.py:81
  270.2 13.6 %copy-start.4 = (f32[2,128,384]{2,1,0:T(8,128)}, f32[2,128,384]{2,1,0:T(8,128)S(1)}, u32[]{:S(2)}) copy-start(f32[2,128,384]{2,1,0:T(8,128)S(1)} %bitcast_add_fusion.6) | copy-start | bytes 1179652
  275.2 8.4 %collective-permute-start.11 = (bf16[2,128,640]{2,1,0:T(8,128)(2,1)S(1)}, bf16[2,128,640]{2,1,0:T(8,128)(2,1)S(1)}, u32[]{:S(2)}, u32[]{:S(2)}) collective-permute-start(bf16[2,128,640]{2,1,0:T(8,128)(2,1)S(1)} %fusion.60), channel_id=1, source_target_pairs={{0,4},{1,5},{2,6},{3,7},{4,8},{5,9},{6,10},{7,11},{8,12},{9,13},{1... | collective-permute-start | bytes 983048 | tf_op jit(solution)/shard_map/ppermute | solution.py:80
  275.4 10.5 %copy-start.6 = (bf16[2048,128]{1,0:T(8,128)(2,1)S(1)}, bf16[2048,128]{1,0:T(8,128)(2,1)}, u32[]{:S(2)}) copy-start(bf16[2048,128]{1,0:T(8,128)(2,1)} %get-tuple-element.114) | copy-start | bytes 1572868
  275.4 10.5 %copy-start.7 = (bf16[2048,128]{1,0:T(8,128)(2,1)S(1)}, bf16[2048,128]{1,0:T(8,128)(2,1)}, u32[]{:S(2)}) copy-start(bf16[2048,128]{1,0:T(8,128)(2,1)} %get-tuple-element.117) | copy-start | bytes 1572868
  275.4 8.2 %collective-permute-start.14 = (bf16[2,128,640]{2,1,0:T(8,128)(2,1)S(1)}, bf16[2,128,640]{2,1,0:T(8,128)(2,1)S(1)}, u32[]{:S(2)}, u32[]{:S(2)}) collective-permute-start(bf16[2,128,640]{2,1,0:T(8,128)(2,1)S(1)} %fusion.58), channel_id=1, source_target_pairs={{0,12},{1,13},{2,14},{3,15},{4,0},{5,1},{6,2},{7,3},{8,4},{9,5},{1... | collective-permute-start | bytes 983048 | tf_op jit(solution)/shard_map/ppermute | solution.py:81
  279.6 10.6 %collective-permute-start.7 = (bf16[128,768]{1,0:T(8,128)(2,1)}, bf16[128,768]{1,0:T(8,128)(2,1)}, u32[]{:S(2)}, u32[]{:S(2)}) collective-permute-start(bf16[128,768]{1,0:T(8,128)(2,1)} %fusion.88), channel_id=1, source_target_pairs={{0,2},{1,3},{2,0},{3,1},{4,6},{5,7},{6,4},{7,5},{8,10},{9,11},{10,... | collective-permute-start | bytes 589832 | tf_op jit(solution)/shard_map/ppermute | solution.py:96
  284.5 7.4 %collective-permute-start.15 = (bf16[128,1280]{1,0:T(8,128)(2,1)}, bf16[128,1280]{1,0:T(8,128)(2,1)}, u32[]{:S(2)}, u32[]{:S(2)}) collective-permute-start(bf16[128,1280]{1,0:T(8,128)(2,1)} %fusion.78), channel_id=1, source_target_pairs={{0,2},{1,3},{2,0},{3,1},{4,6},{5,7},{6,4},{7,5},{8,10},{9,11},{10,... | collective-permute-start | bytes 983048 | tf_op jit(solution)/shard_map/ppermute | solution.py:96
Sparse Core Ops, SparseCore 0:
  10.6 54.5 all-gather.3
  66.9 58.6 all-gather.5
  132.4 52.2 all-gather.7
